TPU v7x, 128 devices: a whole 4x4x4 slice. The times are simulated.
128 devices in a mesh: seq: 16 (over y, x), head: 8 (over z, core).
Axes of the slice: x: 4, y: 4, z: 4, core: 2. Of those that a mesh axis runs over, the one named last changes fastest.
Arguments:
- spectra: bfloat16 [16, 8192, 1024], P('head', 'seq'), may hold values from -6 to 6
- key_bias: float32 [16, 8192], replicated, may hold values from -6 to 330
- valid_bins: int32 [16], replicated, may hold values from 128 to 8192, as said below
- enc_query: bfloat16 [1024, 1024], replicated, may hold values from -0.1875 to 0.1875
- enc_key: bfloat16 [1024, 1024], replicated, may hold values from -0.1875 to 0.1875
- enc_value: bfloat16 [1024, 1024], replicated, may hold values from -0.1875 to 0.1875
- enc_out: bfloat16 [1024, 1024], replicated, may hold values from -1.5 to 1.5
- token_ids: int32 [16, 512], P(None, 'seq'), may hold values from 0 to 27
- embedding: bfloat16 [28, 4096], replicated, may hold values from -6 to 6
- dec_query: bfloat16 [4096, 4096], P(None, 'head'), may hold values from -0.09375 to 0.09375
- mem_key: bfloat16 [1024, 4096], P(None, 'head'), may hold values from -0.1875 to 0.1875
- mem_value: bfloat16 [1024, 4096], P(None, 'head'), may hold values from -0.1875 to 0.1875
- dec_out: bfloat16 [4096, 4096], P('head'), may hold values from -0.5 to 0.5
Outputs:
- encoded: bfloat16 [16, 8192, 1024], P('head', 'seq')
- decoded: bfloat16 [16, 512, 4096], P(None, 'seq', 'head')
Inputs may be any that keep to these rules, and one draw needn't show every extreme that they name: `valid_bins`: each count is a multiple of 128; bins from the count on are padding.
All inputs are finite; a program needn't handle non-finite values.
Results may differ from a plain program's by a relative error of at most 0.018.
Values may be sent and summed in bfloat16 or wider, within the bound.
No kernel may reach another device: no remote copies, remote signals or barrier semaphores. Data moves between devices by JAX's collectives and lax.ppermute only.
A program may use at most 192 MiB of HBM per device.

v0:
```python
import jax
import jax.numpy as jnp
from jax import lax
from jax.sharding import PartitionSpec as P

HE = 16
WINDOW = 512
POOL = 32
HD = 32


epsilon = 1e-05
masked_score = -1e30


def with_halo(block, sides, width):
    for axis, dim in sides:
        count = lax.axis_size(axis)
        forward = [(i, i + 1) for i in range(count - 1)]
        backward = [(target, source) for source, target in forward]
        low = lax.ppermute(
            lax.slice_in_dim(block, block.shape[dim] - width, None, axis=dim), axis, forward
        )
        high = lax.ppermute(lax.slice_in_dim(block, 0, width, axis=dim), axis, backward)
        block = jnp.concatenate([low, block, high], axis=dim)
    return block


def rms_rows(values_in):
    widened = values_in.astype(jnp.float32)
    inverse_rms = lax.rsqrt(jnp.mean(widened * widened, axis=-1, keepdims=True) + epsilon)
    return (widened * inverse_rms).astype(jnp.bfloat16)


def softmax_rows(scores):
    row_top = jnp.max(scores, axis=-1, keepdims=True)
    weights = jnp.exp(scores - row_top)
    return (weights / jnp.sum(weights, axis=-1, keepdims=True)).astype(jnp.bfloat16)


def per_device(
    spectra,
    key_bias,
    valid_bins,
    enc_query,
    enc_key,
    enc_value,
    enc_out,
    token_ids,
    embedding,
    dec_query,
    mem_key,
    mem_value,
    dec_out,
):
    seq_pos = lax.axis_index("seq")
    head_pos = lax.axis_index("head")
    spec_dev, bin_dev, model_width = spectra.shape
    half_span = WINDOW // 2
    head_size = model_width // HE
    first_spec = head_pos * spec_dev
    first_bin = seq_pos * bin_dev
    my_counts = lax.dynamic_slice_in_dim(valid_bins, first_spec, spec_dev, 0)
    bias_pad = jnp.pad(key_bias, ((0, 0), (half_span, half_span)))
    my_bias = lax.dynamic_slice(
        bias_pad, (first_spec, first_bin), (spec_dev, bin_dev + 2 * half_span)
    )
    kv_weights = jnp.concatenate([enc_key, enc_value], axis=1)
    normed = rms_rows(spectra)
    query_enc = jnp.einsum(
        "sbd,de->sbe", normed, enc_query, preferred_element_type=jnp.float32
    ).astype(jnp.bfloat16)
    keyval = jnp.einsum(
        "sbd,de->sbe", normed, kv_weights, preferred_element_type=jnp.float32
    ).astype(jnp.bfloat16)
    keyval = with_halo(keyval, (("seq", 1),), half_span)
    key_span = bin_dev + 2 * half_span
    query_rows = first_bin + jnp.arange(bin_dev, dtype=jnp.int32)
    key_cols = first_bin - half_span + jnp.arange(key_span, dtype=jnp.int32)
    within = jnp.abs(key_cols[None, :] - query_rows[:, None]) <= half_span

    def attend(operands):
        q_one, kv_one, bias_one, count_one = operands
        q_heads = q_one.reshape(bin_dev, HE, head_size)
        key_heads = kv_one[:, :model_width].reshape(key_span, HE, head_size)
        value_heads = kv_one[:, model_width:].reshape(key_span, HE, head_size)
        scores = (
            jnp.einsum("qhd,khd->hqk", q_heads, key_heads, preferred_element_type=jnp.float32)
            * head_size ** (-0.5)
            + bias_one[None, None, :]
        )
        allowed = within & (key_cols[None, :] >= 0) & (key_cols[None, :] < count_one)
        scores = jnp.where(allowed[None], scores, masked_score)
        weights = softmax_rows(scores)
        context = jnp.einsum(
            "hqk,khd->qhd", weights, value_heads, preferred_element_type=jnp.float32
        ).astype(jnp.bfloat16)
        return context.reshape(bin_dev, model_width)

    context = lax.map(attend, (query_enc, keyval, my_bias, my_counts))
    attended = jnp.einsum("sbd,de->sbe", context, enc_out, preferred_element_type=jnp.float32)
    valid_rows = (query_rows[None, :] < my_counts[:, None])[:, :, None]
    encoded = jnp.where(valid_rows, spectra.astype(jnp.float32) + attended, 0.0).astype(
        jnp.bfloat16
    )
    pooled = jnp.mean(
        encoded.astype(jnp.float32).reshape(spec_dev, bin_dev // POOL, POOL, model_width), axis=2
    ).astype(jnp.bfloat16)
    spectra_all = lax.all_gather(pooled, "head", axis=0, tiled=True)
    mem_weights = jnp.concatenate([mem_key, mem_value], axis=1)
    local_width = mem_key.shape[1]
    memory = lax.all_gather(
        jnp.einsum(
            "spd,de->spe", rms_rows(spectra_all), mem_weights, preferred_element_type=jnp.float32
        ).astype(jnp.bfloat16),
        "seq",
        axis=1,
        tiled=True,
    )
    spec_count = memory.shape[0]
    mem_len = memory.shape[1]
    pooled_bias = jnp.max(key_bias.reshape(spec_count, mem_len, POOL), axis=2)
    mem_valid = jnp.arange(mem_len, dtype=jnp.int32)[None, :] * POOL < valid_bins[:, None]
    tok_count = token_ids.shape[1]
    dec_width = embedding.shape[1]
    dec_head = dec_width // HD
    heads_here = local_width // dec_head
    onehot = (
        token_ids[:, :, None] == jnp.arange(embedding.shape[0], dtype=jnp.int32)[None, None, :]
    ).astype(jnp.bfloat16)
    hidden = jnp.einsum(
        "stv,vd->std", onehot, embedding, preferred_element_type=jnp.float32
    ).astype(jnp.bfloat16)
    normed_tok = rms_rows(hidden)
    query_dec = jnp.einsum(
        "std,de->ste", normed_tok, dec_query, preferred_element_type=jnp.float32
    ).astype(jnp.bfloat16)
    query_heads = query_dec.reshape(spec_count, tok_count, heads_here, dec_head)
    key_heads = memory[:, :, :local_width].reshape(spec_count, mem_len, heads_here, dec_head)
    value_heads = memory[:, :, local_width:].reshape(spec_count, mem_len, heads_here, dec_head)
    scores = (
        jnp.einsum("sthd,sphd->shtp", query_heads, key_heads, preferred_element_type=jnp.float32)
        * dec_head ** (-0.5)
        + pooled_bias[:, None, None, :]
    )
    scores = jnp.where(mem_valid[:, None, None, :], scores, masked_score)
    weights = softmax_rows(scores)
    dec_context = jnp.einsum(
        "shtp,sphd->sthd", weights, value_heads, preferred_element_type=jnp.float32
    ).astype(jnp.bfloat16)
    dec_context = dec_context.reshape(spec_count, tok_count, local_width)
    share_width = dec_width // lax.axis_size("head")
    partial_sums = jnp.einsum(
        "ste,ed->std", dec_context, dec_out, preferred_element_type=jnp.float32
    )
    summed = lax.psum_scatter(
        partial_sums.astype(jnp.bfloat16), "head", scatter_dimension=2, tiled=True
    ).astype(jnp.float32)
    own_part = lax.dynamic_slice_in_dim(hidden, head_pos * share_width, share_width, 2)
    decoded = (own_part.astype(jnp.float32) + summed).astype(jnp.bfloat16)
    return (encoded, decoded)


def solution(mesh):
    return jax.shard_map(
        per_device,
        mesh=mesh,
        in_specs=(
            P("head", "seq", None),
            P(),
            P(),
            P(),
            P(),
            P(),
            P(),
            P(None, "seq"),
            P(),
            P(None, "head"),
            P(None, "head"),
            P(None, "head"),
            P("head", None),
        ),
        out_specs=(P("head", "seq", None), P(None, "seq", "head")),
        check_vma=False,
    )
```

profile of v0, /device:TPU:0, one launch (start us, length us, event | category | flops | bytes accessed | tf_op | source)
XLA Modules:
  0.0 351.9 jit_solution(8137123217087698109)
XLA Ops:
  7.2 0.0 copy-start
  7.2 0.0 all-gather.2.cloned.1.call-start
  7.2 2.2 fusion.23
  9.5 7.4 %fusion.41 = bf16[2,512,2048]{2,1,0:T(8,128)(2,1)S(1)} fusion(bf16[1024,1024]{1,0:T(8,128)(2,1)} %param.20, bf16[1024,1024]{1,0:T(8,128)(2,1)} %param.19, bf16[2,512,1024]{2,1,0:T(8,128)(2,1)} %param.15, f32[2,512]{1,0:T(2,128)S(1)} %add_rsqrt_fusion.2), kind=kOutput, calls=%fused_computation.58 | convolution fusion | flops 4308598784 | bytes 10489856 | tf_op jit(solution)/shard_map/sbd,de->sbe/dot_general | solution.py:73
  16.9 0.0 copy-start.8
  16.9 0.0 copy-start.4
  16.9 2.3 fusion.95
  19.2 0.9 copy-done.1
  20.1 4.8 %collective-permute-start = (bf16[2,256,2048]{2,1,0:T(8,128)(2,1)}, bf16[2,256,2048]{2,1,0:T(8,128)(2,1)}, u32[]{:S(2)}, u32[]{:S(2)}) collective-permute-start(bf16[2,256,2048]{2,1,0:T(8,128)(2,1)} %get-tuple-element.122), channel_id=1, source_target_pairs={{0,8},{8,16},{16,24},{24,32},{32,40},{40,48},{48,56},{56,64},{64,7... | collective-permute-start | bytes 6291464 | tf_op jit(solution)/shard_map/ppermute | solution.py:21
  24.9 1.3 collective-permute-start.1
  26.2 0.1 dynamic_slice.25
  26.3 0.1 pad_dynamic-slice_fusion
  26.4 0.7 broadcast_compare_fusion.1
  27.0 6.1 %fusion.49 = bf16[2,512,1024]{2,1,0:T(8,128)(2,1)} fusion(bf16[1024,1024]{1,0:T(8,128)(2,1)} %param.18, bf16[2,512,1024]{2,1,0:T(8,128)(2,1)} %param.15, f32[2,512]{1,0:T(2,128)S(1)} %add_rsqrt_fusion.2), kind=kOutput, calls=%fused_computation.70 | convolution fusion | flops 2151677952 | bytes 6295552 | tf_op jit(solution)/shard_map/sbd,de->sbe/dot_general | solution.py:70
  33.1 35.6 %collective-permute-done = bf16[2,256,2048]{2,1,0:T(8,128)(2,1)} collective-permute-done((bf16[2,256,2048]{2,1,0:T(8,128)(2,1)}, bf16[2,256,2048]{2,1,0:T(8,128)(2,1)}, u32[]{:S(2)}, u32[]{:S(2)}) %collective-permute-start) | collective-permute-done | bytes 2097184 | tf_op jit(solution)/shard_map/ppermute | solution.py:21
  68.7 5.4 %collective-permute-done.1 = bf16[2,256,2048]{2,1,0:T(8,128)(2,1)} collective-permute-done((bf16[2,256,2048]{2,1,0:T(8,128)(2,1)}, bf16[2,256,2048]{2,1,0:T(8,128)(2,1)}, u32[]{:S(2)}, u32[]{:S(2)}) %collective-permute-start.1) | collective-permute-done | bytes 2097184 | tf_op jit(solution)/shard_map/ppermute | solution.py:24
  74.2 6.1 %pad_maximum_fusion = bf16[2,1024,2048]{2,1,0:T(8,128)(2,1)} fusion(bf16[2,256,2048]{2,1,0:T(8,128)(2,1)} %collective-permute-done.1, bf16[2,512,2048]{2,1,0:T(8,128)(2,1)S(1)} %copy-done.2, bf16[2,256,2048]{2,1,0:T(8,128)(2,1)} %collective-permute-done), kind=kLoop, calls=%fused_computation.31 | loop fusion | flops 25165824 | bytes 16777216 | tf_op jit(solution)/shard_map/concatenate | solution.py:25
  80.3 109.5 %while.11 = (s32[]{:T(128)}, bf16[2,512,1024]{1,2,0:T(8,128)(2,1)}, bf16[2,1024,2048]{2,1,0:T(8,128)(2,1)}, s32[2]{0:T(128)S(1)}, bf16[2,512,1024]{2,1,0:T(8,128...) while((s32[]{:T(128)}, bf16[2,512,1024]{1,2,0:T(8,128)(2,1)}, ...), condition=%wide.region_4.5_spmd.clone, body=%wide.region_1.4_spmd.clone.sunk | while | flops 2209353728 | bytes 114383520 | solution.py:100
  80.3 0.6 dynamic_slice.44
  80.9 0.7 fusion.123
  81.6 1.5 fusion.124
  83.1 4.7 %constant_dynamic-slice_fusion.6 = bf16[1,1024,2048]{2,1,0:T(8,128)(2,1)} fusion(bf16[2,1024,2048]{2,1,0:T(8,128)(2,1)} %get-tuple-element.219, s32[]{:T(128)} %get-tuple-element.207), kind=kLoop, calls=%fused_computation.22.clone.1 | loop fusion | bytes 8388612 | tf_op jit(solution)/shard_map/while/body/jit(dynamic_index_in_dim)/dynamic_slice | solution.py:100
  87.8 6.4 %copy.70 = bf16[1,1024,2048]{1,2,0:T(8,128)(2,1)} copy(bf16[1,1024,2048]{2,1,0:T(8,128)(2,1)} %constant_dynamic-slice_fusion.6) | data formatting | bytes 8388608 | tf_op jit(solution)/shard_map/while/body/jit(dynamic_index_in_dim)/dynamic_slice | solution.py:100
  94.2 4.8 %fusion.122 = (bf16[1024,1024]{0,1:T(8,128)(2,1)}, bf16[1024,1024]{0,1:T(8,128)(2,1)}) fusion(bf16[1024,2048]{0,1:T(8,128)(2,1)} %bitcast.108), kind=kLoop, calls=%fused_computation.109.clone.1 | loop fusion | bytes 8388608 | tf_op jit(solution)/shard_map/while/body/eval_jaxpr/slice | solution.py:85
  99.1 0.1 constant_dynamic-slice_fusion.8
  99.1 1.4 copy.71
  100.5 19.5 %fusion.125 = (f32[16,512]{1,0:T(8,128)S(1)}, f32[16,512,1024]{2,1,0:T(8,128)}) fusion(f32[1024]{0:T(1024)S(1)} %bitcast.113, pred[512,1024]{1,0:T(8,128)(4,1)} %fusion.124, bf16[512,16,64]{0,2,1:T(8,128)(2,1)} %bitcast.112, bf16[1024,16,64]{0,2,1:T(8,128)(2,1)} %bitcast.110), kind=kOutput, calls=%fused_computation.110.clone.1 | convolution fusion | flops 1115685888 | bytes 37261312 | tf_op jit(solution)/shard_map/while/body/eval_jaxpr/sub | solution.py:37
  120.1 13.9 %fusion.126 = bf16[16,64,512]{2,1,0:T(8,128)(2,1)S(1)} fusion(bf16[1024,16,64]{0,2,1:T(8,128)(2,1)} %bitcast.109, f32[16,512,1024]{2,1,0:T(8,128)} %get-tuple-element.195, f32[16,512]{1,0:T(8,128)S(1)} %get-tuple-element.196), kind=kOutput, calls=%fused_computation.15.clone.1 | convolution fusion | flops 1091043328 | bytes 36732928 | tf_op jit(solution)/shard_map/while/body/eval_jaxpr/hqk,khd->qhd/dot_general | solution.py:95
  134.0 1.1 constant_dynamic-update-slice_fusion.2
  135.1 0.6 dynamic_slice.44
  135.7 0.7 fusion.123
  136.3 1.5 fusion.124
  137.9 4.7 %constant_dynamic-slice_fusion.6 = bf16[1,1024,2048]{2,1,0:T(8,128)(2,1)} fusion(bf16[2,1024,2048]{2,1,0:T(8,128)(2,1)} %get-tuple-element.219, s32[]{:T(128)} %get-tuple-element.207), kind=kLoop, calls=%fused_computation.22.clone.1 | loop fusion | bytes 8388612 | tf_op jit(solution)/shard_map/while/body/jit(dynamic_index_in_dim)/dynamic_slice | solution.py:100
  142.6 6.4 %copy.70 = bf16[1,1024,2048]{1,2,0:T(8,128)(2,1)} copy(bf16[1,1024,2048]{2,1,0:T(8,128)(2,1)} %constant_dynamic-slice_fusion.6) | data formatting | bytes 8388608 | tf_op jit(solution)/shard_map/while/body/jit(dynamic_index_in_dim)/dynamic_slice | solution.py:100
  149.0 4.8 %fusion.122 = (bf16[1024,1024]{0,1:T(8,128)(2,1)}, bf16[1024,1024]{0,1:T(8,128)(2,1)}) fusion(bf16[1024,2048]{0,1:T(8,128)(2,1)} %bitcast.108), kind=kLoop, calls=%fused_computation.109.clone.1 | loop fusion | bytes 8388608 | tf_op jit(solution)/shard_map/while/body/eval_jaxpr/slice | solution.py:85
  153.8 0.1 constant_dynamic-slice_fusion.8
  153.9 1.4 copy.71
  155.3 19.5 %fusion.125 = (f32[16,512]{1,0:T(8,128)S(1)}, f32[16,512,1024]{2,1,0:T(8,128)}) fusion(f32[1024]{0:T(1024)S(1)} %bitcast.113, pred[512,1024]{1,0:T(8,128)(4,1)} %fusion.124, bf16[512,16,64]{0,2,1:T(8,128)(2,1)} %bitcast.112, bf16[1024,16,64]{0,2,1:T(8,128)(2,1)} %bitcast.110), kind=kOutput, calls=%fused_computation.110.clone.1 | convolution fusion | flops 1115685888 | bytes 37261312 | tf_op jit(solution)/shard_map/while/body/eval_jaxpr/sub | solution.py:37
  174.8 13.9 %fusion.126 = bf16[16,64,512]{2,1,0:T(8,128)(2,1)S(1)} fusion(bf16[1024,16,64]{0,2,1:T(8,128)(2,1)} %bitcast.109, f32[16,512,1024]{2,1,0:T(8,128)} %get-tuple-element.195, f32[16,512]{1,0:T(8,128)S(1)} %get-tuple-element.196), kind=kOutput, calls=%fused_computation.15.clone.1 | convolution fusion | flops 1091043328 | bytes 36732928 | tf_op jit(solution)/shard_map/while/body/eval_jaxpr/hqk,khd->qhd/dot_general | solution.py:95
  188.8 1.0 constant_dynamic-update-slice_fusion.2
  189.8 0.0 copy-start.13
  189.8 6.6 %convert_reduce_fusion = (f32[2,16,1024]{2,1,0:T(8,128)S(1)}, bf16[2,512,1024]{2,1,0:T(8,128)(2,1)}) fusion(bf16[2,512,1024]{1,2,0:T(8,128)(2,1)} %get-tuple-element.44, bf16[1024,1024]{1,0:T(8,128)(2,1)S(1)} %copy-done, bf16[2,512,1024]{2,1,0:T(8,128)(2,1)} %param.15, pred[2,512]{1,0:T(4,128)(4,1)S(1)} %copy-done.7), kind=kOutput, calls=%fused_computation.54 | convolution fusion | flops 2153742336 | bytes 8520704 | tf_op jit(solution)/shard_map/sbd,de->sbe/dot_general | solution.py:101
  196.5 14.4 %all_gather.6 = bf16[16,16,1024]{2,1,0:T(8,128)(2,1)S(1)} all-gather(bf16[2,16,1024]{2,1,0:T(8,128)(2,1)S(1)} %multiply_convert_fusion), channel_id=1, replica_groups=mesh['seq'=16,'head'=8] {'head'}, dimensions={0}, use_global_device_ids=true | all-gather | bytes 589824 | tf_op jit(solution)/shard_map/all_gather | solution.py:109
  210.9 0.2 fusion.74
  211.1 0.0 copy-start.14
  211.1 0.0 copy-start.15
  211.1 1.6 fusion.65
  212.7 0.0 all-gather.2.cloned.1.call-update
  212.7 0.0 reduce-scatter.2.cloned.1.call-start
  212.8 2.0 reshape.182
  214.8 2.2 reduce_max.27
  217.1 0.1 broadcast_compare_fusion
  217.2 1.4 fusion.21
  218.5 1.9 copy-done.6
  220.5 2.4 fusion.69
  222.9 62.1 %all-gather.2.cloned.1.call-done = bf16[16,256,1024]{2,1,0:T(8,128)(2,1)} async-done(((bf16[16,16,1024]{2,1,0:T(8,128)(2,1)}), bf16[16,256,1024]{2,1,0:T(8,128)(2,1)}) %all-gather.2.cloned.1.call-update) | async-done | bytes 8388624 | tf_op jit(solution)/shard_map/all_gather | solution.py:112
  284.9 6.4 %slice_bitcast_fusion.1 = (bf16[16,32,4,8,128]{4,3,2,1,0:T(8,128)(2,1)}, bf16[16,32,4,8,128]{4,3,2,1,0:T(8,128)(2,1)}) fusion(bf16[16,256,1024]{2,1,0:T(8,128)(2,1)} %all-gather.2.cloned.1.call-done), kind=kLoop, calls=%fused_computation.49 | loop fusion | bytes 16777216
  291.4 5.1 %fusion.96 = (f32[16,4,32]{2,1,0:T(4,128)S(1)}, f32[16,4,32,256]{3,2,1,0:T(8,128)}) fusion(f32[16,256]{1,0:T(8,128)S(1)} %reduce_max.27, pred[16,256]{1,0:T(8,128)(4,1)S(1)} %broadcast_compare_fusion, bf16[16,32,4,8,128]{4,3,2,1,0:T(8,128)(2,1)} %get-tuple-element.120, bf16[16,4,4,8,128]{4,3,2,1,0:T(8,128)(2,1)S(1)} %fusion.69), kind=kOutput, calls=%fused_computation.112 | convolution fusion | flops 136839424 | bytes 6844416 | tf_op jit(solution)/shard_map/sub | solution.py:37
  296.5 3.7 %fusion.66 = bf16[16,4,4,8,128]{4,3,2,1,0:T(8,128)(2,1)S(1)} fusion(bf16[16,32,4,8,128]{4,3,2,1,0:T(8,128)(2,1)} %get-tuple-element.121, f32[16,4,32,256]{3,2,1,0:T(8,128)} %get-tuple-element.129, f32[16,4,32]{2,1,0:T(4,128)S(1)} %get-tuple-element.128), kind=kOutput, calls=%fused_computation.77 | convolution fusion | flops 135528448 | bytes 6823936 | tf_op jit(solution)/shard_map/shtp,sphd->sthd/dot_general | solution.py:148
  300.2 0.3 copy-done.11
  300.5 4.3 %convolution_convert_fusion.1 = bf16[16,32,4096]{2,1,0:T(8,128)(2,1)} fusion(bf16[512,4096]{1,0:T(8,128)(2,1)S(1)} %copy-done.11, bf16[16,4,4,8,128]{4,3,2,1,0:T(8,128)(2,1)S(1)} %fusion.66), kind=kOutput, calls=%fused_computation.36 | convolution fusion | flops 2149580800 | bytes 8912896 | tf_op jit(solution)/shard_map/ste,ed->std/dot_general | solution.py:153
  304.8 0.0 reduce-scatter.2.cloned.1.call-update
  304.9 38.1 %reduce-scatter.2.cloned.1.call-done = bf16[16,32,512]{2,1,0:T(8,128)(2,1)} async-done(((bf16[16,32,4096]{2,1,0:T(8,128)(2,1)}), bf16[16,32,512]{2,1,0:T(8,128)(2,1)}) %reduce-scatter.2.cloned.1.call-update) | async-done | bytes 524304 | tf_op jit(solution)/shard_map/reduce_scatter | solution.py:156
  342.9 2.2 add_convert_fusion
  (35 shorter events, 0.1 us)
Async XLA Ops:
  7.2 182.6 %copy-start = (bf16[1024,1024]{1,0:T(8,128)(2,1)S(1)}, bf16[1024,1024]{1,0:T(8,128)(2,1)}, u32[]{:S(2)}) copy-start(bf16[1024,1024]{1,0:T(8,128)(2,1)} %param.21) | copy-start | bytes 6291460
  7.2 277.7 %all-gather.2.cloned.1.call-start = ((), (), s32[]{:S(2)}) async-start(), calls=%async_computation.1 | async-start | bytes 8912896 | tf_op jit(solution)/shard_map/all_gather | solution.py:112
  16.9 3.2 copy-start.1
  16.9 9.3 %copy-start.8 = (s32[16]{0:T(128)S(1)}, s32[16]{0:T(128)}, u32[]{:S(2)}) copy-start(s32[16]{0:T(128)} %param.17) | copy-start | bytes 196
  16.9 9.4 %copy-start.4 = (f32[16,8192]{1,0:T(8,128)S(1)}, f32[16,8192]{1,0:T(8,128)}, u32[]{:S(2)}) copy-start(f32[16,8192]{1,0:T(8,128)} %param.16) | copy-start | bytes 1572868
  20.1 48.7 %collective-permute-start = (bf16[2,256,2048]{2,1,0:T(8,128)(2,1)}, bf16[2,256,2048]{2,1,0:T(8,128)(2,1)}, u32[]{:S(2)}, u32[]{:S(2)}) collective-permute-start(bf16[2,256,2048]{2,1,0:T(8,128)(2,1)} %get-tuple-element.122), channel_id=1, source_target_pairs={{0,8},{8,16},{16,24},{24,32},{32,40},{40,48},{48,56},{56,64},{64,7... | collective-permute-start | bytes 6291464 | tf_op jit(solution)/shard_map/ppermute | solution.py:21
  24.9 49.3 %collective-permute-start.1 = (bf16[2,256,2048]{2,1,0:T(8,128)(2,1)}, bf16[2,256,2048]{2,1,0:T(8,128)(2,1)}, u32[]{:S(2)}, u32[]{:S(2)}) collective-permute-start(bf16[2,256,2048]{2,1,0:T(8,128)(2,1)} %get-tuple-element.123), channel_id=1, source_target_pairs={{8,0},{16,8},{24,16},{32,24},{40,32},{48,40},{56,48},{64,56},{72,6... | collective-permute-start | bytes 6291464 | tf_op jit(solution)/shard_map/ppermute | solution.py:24
  27.0 47.1 %copy-start.2 = (bf16[2,512,2048]{2,1,0:T(8,128)(2,1)S(1)}, bf16[2,512,2048]{2,1,0:T(8,128)(2,1)}, u32[]{:S(2)}) copy-start(bf16[2,512,2048]{2,1,0:T(8,128)(2,1)} %copy-done.1) | copy-start | bytes 12582916
  80.3 109.5 %copy-start.7 = (pred[2,512]{1,0:T(4,128)(4,1)S(1)}, pred[2,512]{1,0:T(4,128)(4,1)}, u32[]{:S(2)}) copy-start(pred[2,512]{1,0:T(4,128)(4,1)} %broadcast_compare_fusion.1) | copy-start | bytes 3076
  94.2 4.8 %copy-start.3 = (bf16[2,512,1024]{2,1,0:T(8,128)(2,1)S(1)}, bf16[2,512,1024]{2,1,0:T(8,128)(2,1)}, u32[]{:S(2)}) copy-start(bf16[2,512,1024]{2,1,0:T(8,128)(2,1)} %get-tuple-element.221) | copy-start | bytes 6291460 | tf_op jit(solution)/shard_map/while
  149.0 4.8 %copy-start.3 = (bf16[2,512,1024]{2,1,0:T(8,128)(2,1)S(1)}, bf16[2,512,1024]{2,1,0:T(8,128)(2,1)}, u32[]{:S(2)}) copy-start(bf16[2,512,1024]{2,1,0:T(8,128)(2,1)} %get-tuple-element.221) | copy-start | bytes 6291460 | tf_op jit(solution)/shard_map/while
  189.8 21.3 %copy-start.12 = (bf16[1024,512]{1,0:T(8,128)(2,1)S(1)}, bf16[1024,512]{1,0:T(8,128)(2,1)}, u32[]{:S(2)}) copy-start(bf16[1024,512]{1,0:T(8,128)(2,1)} %param.26) | copy-start | bytes 3145732
  189.8 21.3 %copy-start.13 = (bf16[1024,512]{1,0:T(8,128)(2,1)S(1)}, bf16[1024,512]{1,0:T(8,128)(2,1)}, u32[]{:S(2)}) copy-start(bf16[1024,512]{1,0:T(8,128)(2,1)} %param.25) | copy-start | bytes 3145732
  196.4 16.3 %copy-start.5 = (f32[16,8192]{1,0:T(8,128)S(1)}, f32[16,8192]{1,0:T(8,128)}, u32[]{:S(2)}) copy-start(f32[16,8192]{1,0:T(8,128)} %param.16) | copy-start | bytes 1572868
  211.1 6.0 %copy-start.9 = (s32[16]{0:T(128)S(1)}, s32[16]{0:T(128)}, u32[]{:S(2)}) copy-start(s32[16]{0:T(128)} %param.17) | copy-start | bytes 196
  211.1 6.0 %copy-start.14 = (bf16[28,4096]{1,0:T(8,128)(2,1)S(1)}, bf16[28,4096]{1,0:T(8,128)(2,1)}, u32[]{:S(2)}) copy-start(bf16[28,4096]{1,0:T(8,128)(2,1)} %param.23) | copy-start | bytes 688132
  211.1 6.0 %copy-start.15 = (s32[16,32]{1,0:T(8,128)S(1)}, s32[16,32]{1,0:T(8,128)}, u32[]{:S(2)}) copy-start(s32[16,32]{1,0:T(8,128)} %param.22) | copy-start | bytes 6148
  212.7 130.2 %reduce-scatter.2.cloned.1.call-start = ((), (), s32[]{:S(2)}) async-start(), calls=%async_computation.2 | async-start | bytes 4718592 | tf_op jit(solution)/shard_map/reduce_scatter | solution.py:156
  217.0 3.4 copy-start.10
  218.5 1.9 copy-start.6
  296.5 4.0 %copy-start.11 = (bf16[512,4096]{1,0:T(8,128)(2,1)S(1)}, bf16[512,4096]{1,0:T(8,128)(2,1)}, u32[]{:S(2)}) copy-start(bf16[512,4096]{1,0:T(8,128)(2,1)} %param.27) | copy-start | bytes 12582916
Sparse Core Ops, SparseCore 0:
  212.8 72.0 all-gather.1
  305.0 37.9 reduce-scatter.1
where the time goes:
time: 353 us; the launch traced here: 352 us
  waiting for transfers between devices  141 us (40%)
  matrix products  106 us (30%)
  local copies, waits for them, and re-layouts  52.2 us (15%)
  other arithmetic  18 us (5%)
  blocking collectives  14.4 us (4%)
  between operations  14.3 us (4%)
  starting transfers between devices  6.18 us (2%)
    all_gather x1, waiting for transfers between devices, per_device(): lax.all_gather(jnp.einsum('spd,de->spe', rms_rows(spectra_all), mem_weigh...  62.1 us
    sub x3, matrix products, softmax_rows(): weights = jnp.exp(scores - row_top)  44.2 us
    reduce_scatter x1, waiting for transfers between devices, per_device(): lax.psum_scatter(partial_sums.astype(jnp.bfloat16), 'head', scatter_dimen...  38.1 us
    ppermute x1, waiting for transfers between devices, with_halo(): lax.ppermute(lax.slice_in_dim(block, block.shape[dim] - width, None, axis...  35.6 us
    dot_general x2, matrix products, attend(): jnp.einsum('hqk,khd->qhd', weights, value_heads, preferred_element_type=j...  27.9 us
    dynamic_slice x12, local copies, waits for them, and re-layouts, per_device(): context = lax.map(attend, (query_enc, keyval, my_bias, my_counts))  26.3 us
    all_gather x1, blocking collectives, per_device(): spectra_all = lax.all_gather(pooled, 'head', axis=0, tiled=True)  14.4 us
    slice x2, local copies, waits for them, and re-layouts, attend(): key_heads = kv_one[:, :model_width].reshape(key_span, HE, head_size)  9.67 us
  transfers between devices with their start and end apart: 4, of which 4 were waited for; matrix products, arithmetic and copies ran while one was open for 4% of the time, Pallas kernels for 0%

commit v1 on v0

--- a/solution.py
+++ b/solution.py
@@ -1,29 +1,20 @@
 import jax
 import jax.numpy as jnp
 from jax import lax
+from jax.experimental import pallas as pl
+from jax.experimental.pallas import tpu as pltpu
 from jax.sharding import PartitionSpec as P
 
 HE = 16
 WINDOW = 512
 POOL = 32
 HD = 32
+QBLOCK = 128
+HGROUP = 512
 
 
 epsilon = 1e-05
 masked_score = -1e30
-
-
-def with_halo(block, sides, width):
-    for axis, dim in sides:
-        count = lax.axis_size(axis)
-        forward = [(i, i + 1) for i in range(count - 1)]
-        backward = [(target, source) for source, target in forward]
-        low = lax.ppermute(
-            lax.slice_in_dim(block, block.shape[dim] - width, None, axis=dim), axis, forward
-        )
-        high = lax.ppermute(lax.slice_in_dim(block, 0, width, axis=dim), axis, backward)
-        block = jnp.concatenate([low, block, high], axis=dim)
-    return block
 
 
 def rms_rows(values_in):
@@ -36,6 +27,63 @@
     row_top = jnp.max(scores, axis=-1, keepdims=True)
     weights = jnp.exp(scores - row_top)
     return (weights / jnp.sum(weights, axis=-1, keepdims=True)).astype(jnp.bfloat16)
+
+
+def band_kernel(q_ref, k_ref, v_ref, b_ref, o_ref):
+    qb = pl.program_id(2)
+    q0 = pl.multiple_of(qb * QBLOCK, QBLOCK)
+    kwin = QBLOCK + WINDOW
+    bias = b_ref[0, 0]
+    lane = lax.broadcasted_iota(jnp.int32, (1, 128), 1)
+    low = lane < 64
+    for pair in range(HGROUP // 128):
+        cols = slice(pair * 128, (pair + 1) * 128)
+        q = q_ref[0, :, cols] * 0.125
+        k = k_ref[0, pl.ds(q0, kwin), cols]
+        v = v_ref[0, pl.ds(q0, kwin), cols]
+        out = None
+        for half in range(2):
+            sel = low if half == 0 else jnp.logical_not(low)
+            qh = jnp.where(sel, q, jnp.zeros_like(q))
+            s = lax.dot_general(
+                qh, k, (((1,), (1,)), ((), ())), preferred_element_type=jnp.float32
+            ) + bias
+            m = jnp.max(s, axis=1, keepdims=True)
+            p = jnp.exp(s - m)
+            total = jnp.sum(p, axis=1, keepdims=True)
+            pv = jnp.dot(p.astype(jnp.bfloat16), v, preferred_element_type=jnp.float32)
+            pv = pv / total
+            out = pv if out is None else jnp.where(low, out, pv)
+        o_ref[0, :, cols] = out.astype(o_ref.dtype)
+
+
+def band_attention(query_enc, keyval, full_bias):
+    spec_dev, bin_dev, width = query_enc.shape
+    key_span = keyval.shape[1]
+    groups = width // HGROUP
+    qblocks = bin_dev // QBLOCK
+    kwin = QBLOCK + WINDOW
+    return pl.pallas_call(
+        band_kernel,
+        out_shape=jax.ShapeDtypeStruct(query_enc.shape, jnp.bfloat16),
+        grid=(spec_dev, groups, qblocks),
+        in_specs=[
+            pl.BlockSpec((1, QBLOCK, HGROUP), lambda s, g, b: (s, b, g)),
+            pl.BlockSpec((1, key_span, HGROUP), lambda s, g, b: (s, 0, g)),
+            pl.BlockSpec((1, key_span, HGROUP), lambda s, g, b: (s, 0, groups + g)),
+            pl.BlockSpec((1, 1, QBLOCK, kwin), lambda s, g, b: (s, b, 0, 0)),
+        ],
+        out_specs=pl.BlockSpec((1, QBLOCK, HGROUP), lambda s, g, b: (s, b, g)),
+        compiler_params=pltpu.CompilerParams(
+            dimension_semantics=("arbitrary", "arbitrary", "arbitrary")
+        ),
+        cost_estimate=pl.CostEstimate(
+            flops=spec_dev * bin_dev * kwin * width * 8,
+            transcendentals=spec_dev * bin_dev * kwin * HE,
+            bytes_accessed=spec_dev * (bin_dev * width * 4 + key_span * width * 4)
+            + full_bias.size * 4,
+        ),
+    )(query_enc, keyval, keyval, full_bias)
 
 
 def per_device(
@@ -57,7 +105,6 @@
     head_pos = lax.axis_index("head")
     spec_dev, bin_dev, model_width = spectra.shape
     half_span = WINDOW // 2
-    head_size = model_width // HE
     first_spec = head_pos * spec_dev
     first_bin = seq_pos * bin_dev
     my_counts = lax.dynamic_slice_in_dim(valid_bins, first_spec, spec_dev, 0)
@@ -66,38 +113,43 @@
         bias_pad, (first_spec, first_bin), (spec_dev, bin_dev + 2 * half_span)
     )
     kv_weights = jnp.concatenate([enc_key, enc_value], axis=1)
+
+    count = lax.axis_size("seq")
+    forward = [(i, i + 1) for i in range(count - 1)]
+    backward = [(target, source) for source, target in forward]
+    low_edge = lax.ppermute(spectra[:, bin_dev - half_span :], "seq", forward)
+    high_edge = lax.ppermute(spectra[:, :half_span], "seq", backward)
+
     normed = rms_rows(spectra)
     query_enc = jnp.einsum(
         "sbd,de->sbe", normed, enc_query, preferred_element_type=jnp.float32
     ).astype(jnp.bfloat16)
-    keyval = jnp.einsum(
+    keyval_mid = jnp.einsum(
         "sbd,de->sbe", normed, kv_weights, preferred_element_type=jnp.float32
     ).astype(jnp.bfloat16)
-    keyval = with_halo(keyval, (("seq", 1),), half_span)
+    edges = rms_rows(jnp.concatenate([low_edge, high_edge], axis=1))
+    keyval_edges = jnp.einsum(
+        "sbd,de->sbe", edges, kv_weights, preferred_element_type=jnp.float32
+    ).astype(jnp.bfloat16)
+    keyval = jnp.concatenate(
+        [keyval_edges[:, :half_span], keyval_mid, keyval_edges[:, half_span:]], axis=1
+    )
     key_span = bin_dev + 2 * half_span
+    kwin = QBLOCK + WINDOW
+    key_cols = first_bin - half_span + jnp.arange(key_span, dtype=jnp.int32)
+    col_ok = (key_cols[None, :] >= 0) & (key_cols[None, :] < my_counts[:, None])
+    col_bias = jnp.where(col_ok, my_bias, masked_score)
+    windows = jnp.stack(
+        [col_bias[:, b * QBLOCK : b * QBLOCK + kwin] for b in range(bin_dev // QBLOCK)], axis=1
+    )
+    offset = (
+        jnp.arange(kwin, dtype=jnp.int32)[None, :] - jnp.arange(QBLOCK, dtype=jnp.int32)[:, None]
+    )
+    band = (offset >= 0) & (offset <= WINDOW)
+    full_bias = jnp.where(band[None, None], windows[:, :, None, :], masked_score)
+    context = band_attention(query_enc, keyval, full_bias)
+
     query_rows = first_bin + jnp.arange(bin_dev, dtype=jnp.int32)
-    key_cols = first_bin - half_span + jnp.arange(key_span, dtype=jnp.int32)
-    within = jnp.abs(key_cols[None, :] - query_rows[:, None]) <= half_span
-
-    def attend(operands):
-        q_one, kv_one, bias_one, count_one = operands
-        q_heads = q_one.reshape(bin_dev, HE, head_size)
-        key_heads = kv_one[:, :model_width].reshape(key_span, HE, head_size)
-        value_heads = kv_one[:, model_width:].reshape(key_span, HE, head_size)
-        scores = (
-            jnp.einsum("qhd,khd->hqk", q_heads, key_heads, preferred_element_type=jnp.float32)
-            * head_size ** (-0.5)
-            + bias_one[None, None, :]
-        )
-        allowed = within & (key_cols[None, :] >= 0) & (key_cols[None, :] < count_one)
-        scores = jnp.where(allowed[None], scores, masked_score)
-        weights = softmax_rows(scores)
-        context = jnp.einsum(
-            "hqk,khd->qhd", weights, value_heads, preferred_element_type=jnp.float32
-        ).astype(jnp.bfloat16)
-        return context.reshape(bin_dev, model_width)
-
-    context = lax.map(attend, (query_enc, keyval, my_bias, my_counts))
     attended = jnp.einsum("sbd,de->sbe", context, enc_out, preferred_element_type=jnp.float32)
     valid_rows = (query_rows[None, :] < my_counts[:, None])[:, :, None]
     encoded = jnp.where(valid_rows, spectra.astype(jnp.float32) + attended, 0.0).astype(

time: 353 us -> 261 us (0.74)
  matrix products: 106 us -> 42.5 us
  Pallas kernels: 0 us -> 45 us
  local copies, waits for them, and re-layouts: 52.2 us -> 13.2 us
  waiting for transfers between devices: 141 us -> 113 us
  other arithmetic: 18 us -> 11.5 us
    pallas_call x0 -> x1, Pallas kernels: none -> 45 us  [band_attention(): pl.pallas_call(band_kernel, out_shape=jax.ShapeDtypeStruct(query_enc.shap...]
    sub x3 -> x1, matrix products: 44.2 us -> 5.15 us  [softmax_rows(): weights = jnp.exp(scores - row_top)]
    ppermute x2, waiting for transfers between devices: 41 us -> 7.41 us  [the longest x1 6.23 us: per_device(): high_edge = lax.ppermute(spectra[:, :half_span], 'seq', backward)]
    dynamic_slice x13 -> x0, local copies, waits for them, and re-layouts: 26.4 us -> none  [the longest x12 26.3 us: per_device(): context = lax.map(attend, (query_enc, keyval, my_bias, my_counts))]
    dot_general x2 -> x1, matrix products: 27.9 us -> 6.49 us  [per_device(): jnp.einsum('sbd,de->sbe', edges, kv_weights, preferred_element_type=jnp.f...]
    slice x3 -> x2, local copies, waits for them, and re-layouts: 12 us -> 3.72 us  [the longest x1 3.21 us: per_device(): low_edge = lax.ppermute(spectra[:, bin_dev - half_span:], 'seq', forward)]
    all_gather x1, waiting for transfers between devices: 62.1 us -> 67.5 us  [per_device(): lax.all_gather(jnp.einsum('spd,de->spe', rms_rows(spectra_all), mem_weigh...]
  transfers between devices with their start and end apart: 4 -> 4, of which waited for: 4 -> 4; matrix products, arithmetic and copies ran while one was open for 4% -> 7% of each run, Pallas kernels for 0% -> 0%
where the time goes in v1:
time: 261 us
  waiting for transfers between devices  113 us (43%)
  Pallas kernels  45 us (17%)
  matrix products  42.5 us (16%)
  blocking collectives  14.6 us (6%)
  between operations  14.3 us (5%)
  local copies, waits for them, and re-layouts  13.2 us (5%)
  other arithmetic  11.5 us (4%)
  starting transfers between devices  7.12 us (3%)
    all_gather x1, waiting for transfers between devices, per_device(): lax.all_gather(jnp.einsum('spd,de->spe', rms_rows(spectra_all), mem_weigh...  67.5 us
    pallas_call x1, Pallas kernels, band_attention(): pl.pallas_call(band_kernel, out_shape=jax.ShapeDtypeStruct(query_enc.shap...  45 us
    reduce_scatter x1, waiting for transfers between devices, per_device(): lax.psum_scatter(partial_sums.astype(jnp.bfloat16), 'head', scatter_dimen...  38.1 us
    all_gather x1, blocking collectives, per_device(): spectra_all = lax.all_gather(pooled, 'head', axis=0, tiled=True)  14.6 us
    unnamed x31, local copies, waits for them, and re-layouts  8.73 us
    dot_general x1, matrix products, per_device(): jnp.einsum('sbd,de->sbe', edges, kv_weights, preferred_element_type=jnp.f...  6.49 us
    dot_general x1, matrix products, per_device(): jnp.einsum('sbd,de->sbe', context, enc_out, preferred_element_type=jnp.fl...  6.33 us
    ppermute x1, waiting for transfers between devices, per_device(): high_edge = lax.ppermute(spectra[:, :half_span], 'seq', backward)  6.23 us
  transfers between devices with their start and end apart: 4, of which 4 were waited for; matrix products, arithmetic and copies ran while one was open for 7% of the time, Pallas kernels for 0%

profile of v1, /device:TPU:0, one launch (start us, length us, event | category | flops | bytes accessed | tf_op | source)
XLA Modules:
  0.0 261.2 jit_solution(1444267615691278458)
XLA Ops:
  7.2 0.0 copy-start
  7.2 0.0 copy-start.6
  7.2 0.0 copy-start.4
  7.2 0.0 all-gather.2.cloned.1.call-start
  7.2 0.0 copy-start.2
  7.3 3.2 %fusion.78 = (bf16[2,256,1024]{2,1,0:T(8,128)(2,1)}, bf16[2,256,1024]{2,1,0:T(8,128)(2,1)}) fusion(bf16[2,512,1024]{2,1,0:T(8,128)(2,1)} %param.13), kind=kLoop, calls=%fused_computation.102 | loop fusion | bytes 4194304 | tf_op jit(solution)/shard_map/slice | solution.py:120
  10.5 1.3 collective-permute-start.1
  11.8 5.5 %collective-permute-start = (bf16[2,256,1024]{2,1,0:T(8,128)(2,1)}, bf16[2,256,1024]{2,1,0:T(8,128)(2,1)}, u32[]{:S(2)}, u32[]{:S(2)}) collective-permute-start(bf16[2,256,1024]{2,1,0:T(8,128)(2,1)} %get-tuple-element.6), channel_id=1, source_target_pairs={{0,8},{8,16},{16,24},{24,32},{32,40},{40,48},{48,56},{56,64},{64,7... | collective-permute-start | bytes 3145736 | tf_op jit(solution)/shard_map/ppermute | solution.py:120
  17.3 0.0 copy-done.2
  17.3 0.5 fusion.5
  17.9 0.0 copy-done.6
  17.9 0.1 dynamic_slice.9
  18.0 0.0 copy-done.4
  18.0 0.1 and_select_fusion
  18.1 0.0 copy-start.3
  18.1 0.0 copy-start.9
  18.2 0.0 copy-start.10
  18.2 6.1 %fusion.29.q_ref = bf16[2,512,1024]{2,1,0:T(8,128)(2,1)} fusion(bf16[1024,1024]{1,0:T(8,128)(2,1)} %param.16, bf16[2,512,1024]{2,1,0:T(8,128)(2,1)} %param.13, f32[2,512]{1,0:T(2,128)S(1)} %add_rsqrt_fusion.3), kind=kOutput, calls=%fused_computation.48 | convolution fusion | flops 2151677952 | bytes 6295552 | tf_op jit(solution)/shard_map/sbd,de->sbe/dot_general | solution.py:124
  24.2 1.8 broadcast_select_fusion.b_ref
  26.0 0.1 broadcast_compare_fusion.2
  26.1 0.0 copy-done.3
  26.1 0.0 copy-done.9
  26.1 0.0 copy-done.10
  26.1 5.1 %convolution_convert_fusion.2 = bf16[2,512,2048]{2,1,0:T(8,128)(2,1)S(1)} fusion(bf16[1024,1024]{1,0:T(8,128)(2,1)S(1)} %copy-done.9, bf16[1024,1024]{1,0:T(8,128)(2,1)S(1)} %copy-done.10, bf16[2,512,1024]{2,1,0:T(8,128)(2,1)S(1)} %copy-done.3, f32[2,512]{1,0:T(2,128)S(1)} %add_rsqrt_fusion.3), kind=kOutput, calls=%fused_computation.33 | convolution fusion | flops 4308598784 | bytes 10489856 | tf_op jit(solution)/shard_map/sbd,de->sbe/dot_general | solution.py:127
  31.2 6.2 %collective-permute-done.1 = bf16[2,256,1024]{2,1,0:T(8,128)(2,1)} collective-permute-done((bf16[2,256,1024]{2,1,0:T(8,128)(2,1)}, bf16[2,256,1024]{2,1,0:T(8,128)(2,1)}, u32[]{:S(2)}, u32[]{:S(2)}) %collective-permute-start.1) | collective-permute-done | bytes 1048608 | tf_op jit(solution)/shard_map/ppermute | solution.py:121
  37.4 1.2 collective-permute-done
  38.6 2.0 fusion.3
  40.6 6.5 %convolution_convert_fusion.3 = bf16[2,512,2048]{2,1,0:T(8,128)(2,1)S(1)} fusion(bf16[1024,1024]{1,0:T(8,128)(2,1)S(1)} %copy-done.9, bf16[1024,1024]{1,0:T(8,128)(2,1)S(1)} %copy-done.10, f32[2,512]{1,0:T(2,128)S(1)} %add_rsqrt_fusion.2, bf16[2,256,1024]{2,1,0:T(8,128)(2,1)} %collective-permute-done.1, bf16[2,256,1024]{2,1,0:T(8,128)(2,1)} %collective-permute-done), kind=kOutput, calls=%fused_computation.34 | convolution fusion | flops 4311744512 | bytes 10489856 | tf_op jit(solution)/shard_map/sbd,de->sbe/dot_general | solution.py:131
  47.1 0.5 fusion.77
  47.6 4.0 %pad_maximum_fusion.k_ref.v_ref = bf16[2,1024,2048]{2,1,0:T(8,128)(2,1)} fusion(bf16[2,256,2048]{2,1,0:T(8,128)(2,1)S(1)} %get-tuple-element.5, bf16[2,512,2048]{2,1,0:T(8,128)(2,1)S(1)} %convolution_convert_fusion.2, bf16[2,256,2048]{2,1,0:T(8,128)(2,1)S(1)} %get-tuple-element.4), kind=kLoop, calls=%fused_computation.5 | loop fusion | flops 25165824 | bytes 16777216 | tf_op jit(solution)/shard_map/concatenate | solution.py:134
  51.6 45.0 %shard_map.140 = bf16[2,512,1024]{2,1,0:T(8,128)(2,1)} custom-call(bf16[2,512,1024]{2,1,0:T(8,128)(2,1)} %fusion.29.q_ref, bf16[2,1024,2048]{2,1,0:T(8,128)(2,1)} %pad_maximum_fusion.k_ref.v_ref, bf16[2,1024,2048]{2,1,0:T(8,128)(2,1)} %pad_maximum_fusion.k_ref.v_ref, f32[2,4,128,640]{3,2,1,0:T(8,128)} %broadcast_select_fusion.b_ref), custom_call_target="tpu_custom_call" | custom-call | flops 5368709120 | bytes 15204352 | tf_op jit(solution)/shard_map/pallas_call | solution.py:66
  96.6 0.0 copy-done
  96.6 0.0 copy-start.11
  96.6 0.0 copy-start.12
  96.6 6.3 %convert_reduce_fusion = (f32[2,16,1024]{2,1,0:T(8,128)S(1)}, bf16[2,512,1024]{2,1,0:T(8,128)(2,1)}) fusion(bf16[2,512,1024]{2,1,0:T(8,128)(2,1)} %shard_map.140, bf16[1024,1024]{1,0:T(8,128)(2,1)S(1)} %copy-done, bf16[2,512,1024]{2,1,0:T(8,128)(2,1)} %param.13, pred[2,512]{1,0:T(4,128)(4,1)S(1)} %broadcast_compare_fusion.2), kind=kOutput, calls=%fused_computation.29 | convolution fusion | flops 2153742336 | bytes 8520704 | tf_op jit(solution)/shard_map/sbd,de->sbe/dot_general | solution.py:153
  102.9 14.6 %all_gather.6 = bf16[16,16,1024]{2,1,0:T(8,128)(2,1)S(1)} all-gather(bf16[2,16,1024]{2,1,0:T(8,128)(2,1)S(1)} %multiply_convert_fusion), channel_id=1, replica_groups=mesh['seq'=16,'head'=8] {'head'}, dimensions={0}, use_global_device_ids=true | all-gather | bytes 589824 | tf_op jit(solution)/shard_map/all_gather | solution.py:161
  117.5 0.2 fusion.54
  117.7 0.0 copy-done.11
  117.7 0.0 copy-done.12
  117.7 0.0 copy-start.13
  117.7 0.0 copy-start.14
  117.8 1.6 fusion.45
  119.3 0.0 all-gather.2.cloned.1.call-update
  119.3 0.3 reduce-scatter.2.cloned.1.call-start
  119.6 0.7 reshape.150
  120.3 0.6 reduce_max.18
  120.9 0.0 copy-start.7
  120.9 0.1 broadcast_compare_fusion
  121.0 0.0 copy-done.13
  121.0 0.0 copy-done.14
  121.0 1.4 fusion.1
  122.4 1.9 copy-done.5
  124.3 0.0 copy-done.7
  124.4 2.4 fusion.49
  126.7 67.5 %all-gather.2.cloned.1.call-done = bf16[16,256,1024]{2,1,0:T(8,128)(2,1)} async-done(((bf16[16,16,1024]{2,1,0:T(8,128)(2,1)}), bf16[16,256,1024]{2,1,0:T(8,128)(2,1)}) %all-gather.2.cloned.1.call-update) | async-done | bytes 8388624 | tf_op jit(solution)/shard_map/all_gather | solution.py:164
  194.2 6.4 %slice_bitcast_fusion.1 = (bf16[16,32,4,8,128]{4,3,2,1,0:T(8,128)(2,1)}, bf16[16,32,4,8,128]{4,3,2,1,0:T(8,128)(2,1)}) fusion(bf16[16,256,1024]{2,1,0:T(8,128)(2,1)} %all-gather.2.cloned.1.call-done), kind=kLoop, calls=%fused_computation.27 | loop fusion | bytes 16777216
  200.6 5.2 %fusion.79 = (f32[16,4,32]{2,1,0:T(4,128)S(1)}, f32[16,4,32,256]{3,2,1,0:T(8,128)}) fusion(f32[16,256]{1,0:T(8,128)S(1)} %reduce_max.18, pred[16,256]{1,0:T(8,128)(4,1)S(1)} %broadcast_compare_fusion, bf16[16,32,4,8,128]{4,3,2,1,0:T(8,128)(2,1)} %get-tuple-element.2, bf16[16,4,4,8,128]{4,3,2,1,0:T(8,128)(2,1)S(1)} %fusion.49), kind=kOutput, calls=%fused_computation.103 | convolution fusion | flops 136839424 | bytes 6844416 | tf_op jit(solution)/shard_map/sub | solution.py:28
  205.8 3.7 %fusion.46 = bf16[16,4,4,8,128]{4,3,2,1,0:T(8,128)(2,1)S(1)} fusion(bf16[16,32,4,8,128]{4,3,2,1,0:T(8,128)(2,1)} %get-tuple-element.3, f32[16,4,32,256]{3,2,1,0:T(8,128)} %get-tuple-element.17, f32[16,4,32]{2,1,0:T(4,128)S(1)} %get-tuple-element.16), kind=kOutput, calls=%fused_computation.56 | convolution fusion | flops 135528448 | bytes 6823936 | tf_op jit(solution)/shard_map/shtp,sphd->sthd/dot_general | solution.py:200
  209.5 0.3 copy-done.8
  209.8 4.3 %convolution_convert_fusion.1 = bf16[16,32,4096]{2,1,0:T(8,128)(2,1)} fusion(bf16[512,4096]{1,0:T(8,128)(2,1)S(1)} %copy-done.8, bf16[16,4,4,8,128]{4,3,2,1,0:T(8,128)(2,1)S(1)} %fusion.46), kind=kOutput, calls=%fused_computation.10 | convolution fusion | flops 2149580800 | bytes 8912896 | tf_op jit(solution)/shard_map/ste,ed->std/dot_general | solution.py:205
  214.1 0.0 reduce-scatter.2.cloned.1.call-update
  214.1 38.1 %reduce-scatter.2.cloned.1.call-done = bf16[16,32,512]{2,1,0:T(8,128)(2,1)} async-done(((bf16[16,32,4096]{2,1,0:T(8,128)(2,1)}), bf16[16,32,512]{2,1,0:T(8,128)(2,1)}) %reduce-scatter.2.cloned.1.call-update) | async-done | bytes 524304 | tf_op jit(solution)/shard_map/reduce_scatter | solution.py:208
  252.2 2.2 add_convert_fusion
  254.3 0.0 copy-done.1
  (16 shorter events, 0.1 us)
Async XLA Ops:
  7.2 89.4 %copy-start = (bf16[1024,1024]{1,0:T(8,128)(2,1)S(1)}, bf16[1024,1024]{1,0:T(8,128)(2,1)}, u32[]{:S(2)}) copy-start(bf16[1024,1024]{1,0:T(8,128)(2,1)} %param.19) | copy-start | bytes 6291460
  7.2 10.7 %copy-start.6 = (s32[16]{0:T(128)S(1)}, s32[16]{0:T(128)}, u32[]{:S(2)}) copy-start(s32[16]{0:T(128)} %param.15) | copy-start | bytes 196
  7.2 10.8 %copy-start.4 = (f32[16,8192]{1,0:T(8,128)S(1)}, f32[16,8192]{1,0:T(8,128)}, u32[]{:S(2)}) copy-start(f32[16,8192]{1,0:T(8,128)} %param.14) | copy-start | bytes 1572868
  7.2 187.0 %all-gather.2.cloned.1.call-start = ((), (), s32[]{:S(2)}) async-start(), calls=%async_computation.1 | async-start | bytes 8912896 | tf_op jit(solution)/shard_map/all_gather | solution.py:164
  7.2 10.1 %copy-start.2 = (bf16[2,512,1024]{2,1,0:T(8,128)(2,1)S(1)}, bf16[2,512,1024]{2,1,0:T(8,128)(2,1)}, u32[]{:S(2)}) copy-start(bf16[2,512,1024]{2,1,0:T(8,128)(2,1)} %param.13) | copy-start | bytes 6291460
  10.5 26.9 %collective-permute-start.1 = (bf16[2,256,1024]{2,1,0:T(8,128)(2,1)}, bf16[2,256,1024]{2,1,0:T(8,128)(2,1)}, u32[]{:S(2)}, u32[]{:S(2)}) collective-permute-start(bf16[2,256,1024]{2,1,0:T(8,128)(2,1)} %get-tuple-element.7), channel_id=1, source_target_pairs={{8,0},{16,8},{24,16},{32,24},{40,32},{48,40},{56,48},{64,56},{72,6... | collective-permute-start | bytes 3145736 | tf_op jit(solution)/shard_map/ppermute | solution.py:121
  11.8 26.8 %collective-permute-start = (bf16[2,256,1024]{2,1,0:T(8,128)(2,1)}, bf16[2,256,1024]{2,1,0:T(8,128)(2,1)}, u32[]{:S(2)}, u32[]{:S(2)}) collective-permute-start(bf16[2,256,1024]{2,1,0:T(8,128)(2,1)} %get-tuple-element.6), channel_id=1, source_target_pairs={{0,8},{8,16},{16,24},{24,32},{32,40},{40,48},{48,56},{56,64},{64,7... | collective-permute-start | bytes 3145736 | tf_op jit(solution)/shard_map/ppermute | solution.py:120
  18.1 7.9 %copy-start.3 = (bf16[2,512,1024]{2,1,0:T(8,128)(2,1)S(1)}, bf16[2,512,1024]{2,1,0:T(8,128)(2,1)}, u32[]{:S(2)}) copy-start(bf16[2,512,1024]{2,1,0:T(8,128)(2,1)} %param.13) | copy-start | bytes 6291460
  18.1 7.9 %copy-start.9 = (bf16[1024,1024]{1,0:T(8,128)(2,1)S(1)}, bf16[1024,1024]{1,0:T(8,128)(2,1)}, u32[]{:S(2)}) copy-start(bf16[1024,1024]{1,0:T(8,128)(2,1)} %param.18) | copy-start | bytes 6291460
  18.2 7.9 %copy-start.10 = (bf16[1024,1024]{1,0:T(8,128)(2,1)S(1)}, bf16[1024,1024]{1,0:T(8,128)(2,1)}, u32[]{:S(2)}) copy-start(bf16[1024,1024]{1,0:T(8,128)(2,1)} %param.17) | copy-start | bytes 6291460
  96.6 21.1 %copy-start.11 = (bf16[1024,512]{1,0:T(8,128)(2,1)S(1)}, bf16[1024,512]{1,0:T(8,128)(2,1)}, u32[]{:S(2)}) copy-start(bf16[1024,512]{1,0:T(8,128)(2,1)} %param.24) | copy-start | bytes 3145732
  96.6 21.1 %copy-start.12 = (bf16[1024,512]{1,0:T(8,128)(2,1)S(1)}, bf16[1024,512]{1,0:T(8,128)(2,1)}, u32[]{:S(2)}) copy-start(bf16[1024,512]{1,0:T(8,128)(2,1)} %param.23) | copy-start | bytes 3145732
  117.7 3.3 %copy-start.13 = (bf16[28,4096]{1,0:T(8,128)(2,1)S(1)}, bf16[28,4096]{1,0:T(8,128)(2,1)}, u32[]{:S(2)}) copy-start(bf16[28,4096]{1,0:T(8,128)(2,1)} %param.21) | copy-start | bytes 688132
  117.7 3.3 %copy-start.14 = (s32[16,32]{1,0:T(8,128)S(1)}, s32[16,32]{1,0:T(8,128)}, u32[]{:S(2)}) copy-start(s32[16,32]{1,0:T(8,128)} %param.20) | copy-start | bytes 6148
  119.3 132.8 %reduce-scatter.2.cloned.1.call-start = ((), (), s32[]{:S(2)}) async-start(), calls=%async_computation.2 | async-start | bytes 4718592 | tf_op jit(solution)/shard_map/reduce_scatter | solution.py:208
  120.9 3.4 %copy-start.7 = (bf16[4096,512]{1,0:T(8,128)(2,1)S(1)}, bf16[4096,512]{1,0:T(8,128)(2,1)}, u32[]{:S(2)}) copy-start(bf16[4096,512]{1,0:T(8,128)(2,1)} %param.22) | copy-start | bytes 12582916
  122.4 1.9 copy-start.5
  205.8 4.0 %copy-start.8 = (bf16[512,4096]{1,0:T(8,128)(2,1)S(1)}, bf16[512,4096]{1,0:T(8,128)(2,1)}, u32[]{:S(2)}) copy-start(bf16[512,4096]{1,0:T(8,128)(2,1)} %param.25) | copy-start | bytes 12582916
  209.8 44.5 %copy-start.1 = (bf16[1024,1024]{1,0:T(8,128)(2,1)S(1)}, bf16[1024,1024]{1,0:T(8,128)(2,1)}, u32[]{:S(2)}) copy-start(bf16[1024,1024]{1,0:T(8,128)(2,1)} %param.19) | copy-start | bytes 6291460
Sparse Core Ops, SparseCore 0:
  119.5 74.6 all-gather.1
  214.2 37.9 reduce-scatter.1

commit v2 on v1

--- a/solution.py
+++ b/solution.py
@@ -161,18 +161,16 @@
     spectra_all = lax.all_gather(pooled, "head", axis=0, tiled=True)
     mem_weights = jnp.concatenate([mem_key, mem_value], axis=1)
     local_width = mem_key.shape[1]
-    memory = lax.all_gather(
-        jnp.einsum(
-            "spd,de->spe", rms_rows(spectra_all), mem_weights, preferred_element_type=jnp.float32
-        ).astype(jnp.bfloat16),
-        "seq",
-        axis=1,
-        tiled=True,
-    )
-    spec_count = memory.shape[0]
+    memory_part = jnp.einsum(
+        "spd,de->spe", rms_rows(spectra_all), mem_weights, preferred_element_type=jnp.float32
+    ).astype(jnp.bfloat16)
+    memory = lax.all_to_all(memory_part, "seq", 0, 1, tiled=True)
+    spec_count = key_bias.shape[0]
     mem_len = memory.shape[1]
-    pooled_bias = jnp.max(key_bias.reshape(spec_count, mem_len, POOL), axis=2)
-    mem_valid = jnp.arange(mem_len, dtype=jnp.int32)[None, :] * POOL < valid_bins[:, None]
+    bias_row = lax.dynamic_slice_in_dim(key_bias, seq_pos, 1, 0)
+    pooled_bias = jnp.max(bias_row.reshape(1, mem_len, POOL), axis=2)
+    count_row = lax.dynamic_slice_in_dim(valid_bins, seq_pos, 1, 0)
+    mem_valid = jnp.arange(mem_len, dtype=jnp.int32)[None, :] * POOL < count_row[:, None]
     tok_count = token_ids.shape[1]
     dec_width = embedding.shape[1]
     dec_head = dec_width // HD
@@ -187,9 +185,11 @@
     query_dec = jnp.einsum(
         "std,de->ste", normed_tok, dec_query, preferred_element_type=jnp.float32
     ).astype(jnp.bfloat16)
-    query_heads = query_dec.reshape(spec_count, tok_count, heads_here, dec_head)
-    key_heads = memory[:, :, :local_width].reshape(spec_count, mem_len, heads_here, dec_head)
-    value_heads = memory[:, :, local_width:].reshape(spec_count, mem_len, heads_here, dec_head)
+    query_one = lax.all_to_all(query_dec, "seq", 0, 1, tiled=True)
+    all_tok = query_one.shape[1]
+    query_heads = query_one.reshape(1, all_tok, heads_here, dec_head)
+    key_heads = memory[:, :, :local_width].reshape(1, mem_len, heads_here, dec_head)
+    value_heads = memory[:, :, local_width:].reshape(1, mem_len, heads_here, dec_head)
     scores = (
         jnp.einsum("sthd,sphd->shtp", query_heads, key_heads, preferred_element_type=jnp.float32)
         * dec_head ** (-0.5)
@@ -197,10 +197,11 @@
     )
     scores = jnp.where(mem_valid[:, None, None, :], scores, masked_score)
     weights = softmax_rows(scores)
-    dec_context = jnp.einsum(
+    context_one = jnp.einsum(
         "shtp,sphd->sthd", weights, value_heads, preferred_element_type=jnp.float32
     ).astype(jnp.bfloat16)
-    dec_context = dec_context.reshape(spec_count, tok_count, local_width)
+    context_one = context_one.reshape(1, all_tok, local_width)
+    dec_context = lax.all_to_all(context_one, "seq", 1, 0, tiled=True)
     share_width = dec_width // lax.axis_size("head")
     partial_sums = jnp.einsum(
         "ste,ed->std", dec_context, dec_out, preferred_element_type=jnp.float32

time: 261 us -> 231 us (0.89)
  waiting for transfers between devices: 113 us -> 44.1 us
  starting transfers between devices: 7.12 us -> 22.2 us
  blocking collectives: 14.6 us -> 28.5 us
  other arithmetic: 11.5 us -> 17.8 us
    all_gather x1 -> x0, waiting for transfers between devices: 67.5 us -> none  [per_device(): lax.all_gather(jnp.einsum('spd,de->spe', rms_rows(spectra_all), mem_weigh...]
    all_to_all x0 -> x2, starting transfers between devices: none -> 15.2 us  [the longest x1 8 us: per_device(): query_one = lax.all_to_all(query_dec, 'seq', 0, 1, tiled=True)]
    all_to_all x0 -> x1, blocking collectives: none -> 14.2 us  [per_device(): dec_context = lax.all_to_all(context_one, 'seq', 1, 0, tiled=True)]
    all_to_all x0 -> x2, waiting for transfers between devices: none -> 8.44 us  [the longest x1 8.44 us: per_device(): memory = lax.all_to_all(memory_part, 'seq', 0, 1, tiled=True)]
    ppermute x1, waiting for transfers between devices: 6.23 us -> 0.01 us  [per_device(): high_edge = lax.ppermute(spectra[:, :half_span], 'seq', backward)]
    unnamed x0 -> x1, other arithmetic: none -> 4.66 us
    unnamed x31 -> x29, local copies, waits for them, and re-layouts: 8.73 us -> 6.51 us
  transfers between devices with their start and end apart: 4 -> 5, of which waited for: 4 -> 2; matrix products, arithmetic and copies ran while one was open for 7% -> 19% of each run, Pallas kernels for 0% -> 20%
where the time goes in v2:
time: 231 us; the launch traced here: 230 us
  Pallas kernels  45 us (19%)
  waiting for transfers between devices  44.1 us (19%)
  matrix products  42.4 us (18%)
  blocking collectives  28.5 us (12%)
  starting transfers between devices  22.2 us (10%)
  other arithmetic  17.8 us (8%)
  local copies, waits for them, and re-layouts  15.6 us (7%)
  between operations  14.4 us (6%)
    pallas_call x1, Pallas kernels, band_attention(): pl.pallas_call(band_kernel, out_shape=jax.ShapeDtypeStruct(query_enc.shap...  45 us
    reduce_scatter x1, waiting for transfers between devices, per_device(): lax.psum_scatter(partial_sums.astype(jnp.bfloat16), 'head', scatter_dimen...  35.7 us
    all_gather x1, blocking collectives, per_device(): spectra_all = lax.all_gather(pooled, 'head', axis=0, tiled=True)  14.3 us
    all_to_all x1, blocking collectives, per_device(): dec_context = lax.all_to_all(context_one, 'seq', 1, 0, tiled=True)  14.2 us
    all_to_all x1, waiting for transfers between devices, per_device(): memory = lax.all_to_all(memory_part, 'seq', 0, 1, tiled=True)  8.44 us
    all_to_all x1, starting transfers between devices, per_device(): query_one = lax.all_to_all(query_dec, 'seq', 0, 1, tiled=True)  8 us
    all_to_all x1, starting transfers between devices, per_device(): memory = lax.all_to_all(memory_part, 'seq', 0, 1, tiled=True)  7.21 us
    unnamed x29, local copies, waits for them, and re-layouts  6.51 us
  transfers between devices with their start and end apart: 5, of which 2 were waited for; matrix products, arithmetic and copies ran while one was open for 19% of the time, Pallas kernels for 20%

profile of v2, /device:TPU:0, one launch (start us, length us, event | category | flops | bytes accessed | tf_op | source)
XLA Modules:
  0.0 230.0 jit_solution(16284151198049669336)
XLA Ops:
  7.2 0.0 copy-start
  7.2 0.0 copy-start.9
  7.2 0.0 copy-start.10
  7.2 0.0 copy-start.4
  7.2 3.2 %fusion.64 = (bf16[2,256,1024]{2,1,0:T(8,128)(2,1)}, bf16[2,256,1024]{2,1,0:T(8,128)(2,1)}) fusion(bf16[2,512,1024]{2,1,0:T(8,128)(2,1)} %param.13), kind=kLoop, calls=%fused_computation.89 | loop fusion | bytes 4194304 | tf_op jit(solution)/shard_map/slice | solution.py:120
  10.4 1.4 collective-permute-start.1
  11.9 5.5 %collective-permute-start = (bf16[2,256,1024]{2,1,0:T(8,128)(2,1)}, bf16[2,256,1024]{2,1,0:T(8,128)(2,1)}, u32[]{:S(2)}, u32[]{:S(2)}) collective-permute-start(bf16[2,256,1024]{2,1,0:T(8,128)(2,1)} %get-tuple-element.4), channel_id=1, source_target_pairs={{0,8},{8,16},{16,24},{24,32},{32,40},{40,48},{48,56},{56,64},{64,7... | collective-permute-start | bytes 3145736 | tf_op jit(solution)/shard_map/ppermute | solution.py:120
  17.4 0.0 copy-done.9
  17.4 0.0 copy-done.10
  17.4 1.4 fusion.1
  18.8 2.0 copy-done.3
  20.8 0.0 copy-done.4
  20.8 3.2 %fusion.31 = bf16[16,32,512]{2,1,0:T(8,128)(2,1)} fusion(bf16[4096,512]{1,0:T(8,128)(2,1)S(1)} %copy-done.4, bf16[16,32,4096]{2,1,0:T(8,128)(2,1)S(1)} %get-tuple-element.15, f32[16,32]{1,0:T(8,128)S(1)} %add_rsqrt_fusion), kind=kOutput, calls=%fused_computation.45 | convolution fusion | flops 2154037248 | bytes 8914944 | tf_op jit(solution)/shard_map/std,de->ste/dot_general | solution.py:185
  23.9 8.0 %all-to-all-start.1 = ((bf16[16,32,512]{2,1,0:T(8,128)(2,1)}), bf16[16,32,512]{2,1,0:T(8,128)(2,1)S(1)}, u32[]{:S(2)}, u32[]{:S(2)}) async-start(bf16[16,32,512]{2,1,0:T(8,128)(2,1)} %fusion.31), calls=%async_computation.1 | async-start | bytes 1048576 | tf_op jit(solution)/shard_map/all_to_all | solution.py:188
  32.0 2.1 fusion.5
  34.1 0.0 copy-done.11
  34.1 0.1 dynamic_slice.15
  34.2 0.1 and_select_fusion
  34.4 0.0 copy-start.1
  34.4 0.0 copy-start.5
  34.4 0.0 copy-start.6
  34.4 6.1 %fusion.23.q_ref = bf16[2,512,1024]{2,1,0:T(8,128)(2,1)} fusion(bf16[1024,1024]{1,0:T(8,128)(2,1)} %param.16, bf16[2,512,1024]{2,1,0:T(8,128)(2,1)} %param.13, f32[2,512]{1,0:T(2,128)S(1)} %add_rsqrt_fusion.3), kind=kOutput, calls=%fused_computation.40 | convolution fusion | flops 2151677952 | bytes 6295552 | tf_op jit(solution)/shard_map/sbd,de->sbe/dot_general | solution.py:124
  40.5 1.7 broadcast_select_fusion.b_ref
  42.2 0.1 broadcast_compare_fusion.1
  42.2 0.0 copy-done.1
  42.3 4.9 %convolution_convert_fusion.2 = bf16[2,512,2048]{2,1,0:T(8,128)(2,1)S(1)} fusion(bf16[1024,1024]{1,0:T(8,128)(2,1)S(1)} %copy-done.5, bf16[1024,1024]{1,0:T(8,128)(2,1)S(1)} %copy-done.6, bf16[2,512,1024]{2,1,0:T(8,128)(2,1)S(1)} %copy-done.1, f32[2,512]{1,0:T(2,128)S(1)} %add_rsqrt_fusion.3), kind=kOutput, calls=%fused_computation.25 | convolution fusion | flops 4308598784 | bytes 10489856 | tf_op jit(solution)/shard_map/sbd,de->sbe/dot_general | solution.py:127
  47.2 0.0 collective-permute-done.1
  47.2 0.0 collective-permute-done
  47.2 2.0 fusion.3
  49.2 6.5 %convolution_convert_fusion.3 = bf16[2,512,2048]{2,1,0:T(8,128)(2,1)S(1)} fusion(bf16[1024,1024]{1,0:T(8,128)(2,1)S(1)} %copy-done.5, bf16[1024,1024]{1,0:T(8,128)(2,1)S(1)} %copy-done.6, f32[2,512]{1,0:T(2,128)S(1)} %add_rsqrt_fusion.2, bf16[2,256,1024]{2,1,0:T(8,128)(2,1)} %collective-permute-done.1, bf16[2,256,1024]{2,1,0:T(8,128)(2,1)} %collective-permute-done), kind=kOutput, calls=%fused_computation.26 | convolution fusion | flops 4311744512 | bytes 10489856 | tf_op jit(solution)/shard_map/sbd,de->sbe/dot_general | solution.py:131
  55.7 0.5 fusion.63
  56.2 4.0 %pad_maximum_fusion.k_ref.v_ref = bf16[2,1024,2048]{2,1,0:T(8,128)(2,1)} fusion(bf16[2,256,2048]{2,1,0:T(8,128)(2,1)S(1)} %get-tuple-element.3, bf16[2,512,2048]{2,1,0:T(8,128)(2,1)S(1)} %convolution_convert_fusion.2, bf16[2,256,2048]{2,1,0:T(8,128)(2,1)S(1)} %get-tuple-element.2), kind=kLoop, calls=%fused_computation.5 | loop fusion | flops 25165824 | bytes 16777216 | tf_op jit(solution)/shard_map/concatenate | solution.py:134
  60.2 45.0 %shard_map.140 = bf16[2,512,1024]{2,1,0:T(8,128)(2,1)} custom-call(bf16[2,512,1024]{2,1,0:T(8,128)(2,1)} %fusion.23.q_ref, bf16[2,1024,2048]{2,1,0:T(8,128)(2,1)} %pad_maximum_fusion.k_ref.v_ref, bf16[2,1024,2048]{2,1,0:T(8,128)(2,1)} %pad_maximum_fusion.k_ref.v_ref, f32[2,4,128,640]{3,2,1,0:T(8,128)} %broadcast_select_fusion.b_ref), custom_call_target="tpu_custom_call" | custom-call | flops 5368709120 | bytes 15204352 | tf_op jit(solution)/shard_map/pallas_call | solution.py:66
  105.2 0.0 copy-start.8
  105.2 6.3 %convert_reduce_fusion = (f32[2,16,1024]{2,1,0:T(8,128)S(1)}, bf16[2,512,1024]{2,1,0:T(8,128)(2,1)}) fusion(bf16[2,512,1024]{2,1,0:T(8,128)(2,1)} %shard_map.140, bf16[1024,1024]{1,0:T(8,128)(2,1)S(1)} %copy-done, bf16[2,512,1024]{2,1,0:T(8,128)(2,1)} %param.13, pred[2,512]{1,0:T(4,128)(4,1)S(1)} %broadcast_compare_fusion.1), kind=kOutput, calls=%fused_computation.21 | convolution fusion | flops 2153742336 | bytes 8520704 | tf_op jit(solution)/shard_map/sbd,de->sbe/dot_general | solution.py:153
  111.5 14.3 %all_gather.3 = bf16[16,16,1024]{2,1,0:T(8,128)(2,1)S(1)} all-gather(bf16[2,16,1024]{2,1,0:T(8,128)(2,1)S(1)} %multiply_convert_fusion), channel_id=1, replica_groups=mesh['seq'=16,'head'=8] {'head'}, dimensions={0}, use_global_device_ids=true | all-gather | bytes 589824 | tf_op jit(solution)/shard_map/all_gather | solution.py:161
  125.8 0.2 fusion.37
  126.0 0.0 copy-done.7
  126.0 1.6 fusion.36
  127.6 0.0 all-to-all-done.1
  127.6 7.2 %all-to-all-start = ((bf16[16,16,1024]{2,1,0:T(8,128)(2,1)}), bf16[16,16,1024]{2,1,0:T(8,128)(2,1)S(1)}, u32[]{:S(2)}, u32[]{:S(2)}) async-start(bf16[16,16,1024]{2,1,0:T(8,128)(2,1)} %fusion.36), calls=%async_computation | async-start | bytes 1048576 | tf_op jit(solution)/shard_map/all_to_all | solution.py:167
  134.8 0.0 reduce-scatter.2.cloned.1.call-start
  134.9 0.7 dynamic_slice.18
  135.5 1.0 dynamic-slice_reduce_fusion
  136.6 0.1 reshape.175
  136.7 0.1 reduce_max.18
  136.8 0.7 multiply_compare_fusion
  137.5 0.9 reshape.173
  138.4 8.4 %all-to-all-done = bf16[16,16,1024]{2,1,0:T(8,128)(2,1)S(1)} async-done(((bf16[16,16,1024]{2,1,0:T(8,128)(2,1)}), bf16[16,16,1024]{2,1,0:T(8,128)(2,1)S(1)}, u32[]{:S(2)}, u32[]{:S(2)}) %all-to-all-start) | async-done | bytes 524320 | tf_op jit(solution)/shard_map/all_to_all | solution.py:167
  146.9 0.1 copy.35
  147.0 0.1 copy.44
  147.2 3.3 %fusion.66 = (f32[4,512]{1,0:T(4,128)S(1)}, f32[4,512,256]{1,2,0:T(8,128)}) fusion(f32[256]{0:T(256)S(1)} %reduce_max.18, pred[256]{0:T(512)(128)(4,1)S(1)} %multiply_compare_fusion, bf16[256,4,128]{0,2,1:T(8,128)(2,1)S(1)} %bitcast.67, bf16[512,4,128]{2,1,0:T(4,128)(2,1)} %reshape.173), kind=kOutput, calls=%fused_computation.91 | convolution fusion | flops 136839424 | bytes 2893056 | tf_op jit(solution)/shard_map/sub | solution.py:28
  150.5 2.7 %convolution_convert_fusion.4 = bf16[4,128,512]{2,1,0:T(8,128)(2,1)} fusion(bf16[256,4,128]{0,2,1:T(8,128)(2,1)S(1)} %bitcast.66, f32[4,512,256]{1,2,0:T(8,128)} %get-tuple-element.17, f32[4,512]{1,0:T(4,128)S(1)} %get-tuple-element.16), kind=kOutput, calls=%fused_computation.46 | convolution fusion | flops 135528448 | bytes 2891776 | tf_op jit(solution)/shard_map/shtp,sphd->sthd/dot_general | solution.py:200
  153.2 2.4 %copy.40 = bf16[1,512,512]{2,0,1:T(2,128)(2,1)S(1)} copy(bf16[1,512,512]{1,2,0:T(8,128)(2,1)} %bitcast.64) | data formatting | bytes 1048576 | tf_op jit(solution)/shard_map/reshape | solution.py:203
  155.6 0.6 broadcast.138
  156.2 4.7 %reduce.9 = bf16[512,512]{1,0:T(8,128)(2,1)} reduce(bf16[512,1,512]{2,1,0:T(2,128)(2,1)S(1)} %bitcast.62, bf16[]{:T(256)} %broadcast.138), dimensions={1}, to_apply=%bitcast.51.reduce_sub_computation | reduce | bytes 1048578
  160.9 1.4 reshape.193
  162.3 14.2 %all_to_all.33 = bf16[16,2,8192]{2,1,0:T(2,128)(2,1)} all-to-all(bf16[16,2,8192]{2,1,0:T(2,128)(2,1)S(1)} %reshape.193), channel_id=1, replica_groups=mesh['seq'=16,'head'=8] {'seq'}, dimensions={0} | all-to-all | bytes 1048576 | tf_op jit(solution)/shard_map/all_to_all | solution.py:204
  176.5 2.2 reshape.194
  178.7 0.1 copy.43
  178.8 6.5 %convolution_convert_fusion.1 = bf16[16,32,4096]{2,1,0:T(8,128)(2,1)} fusion(bf16[16,32,512]{2,1,0:T(8,128)(2,1)S(1)} %bitcast.65, bf16[512,4096]{1,0:T(8,128)(2,1)} %param.25), kind=kOutput, calls=%fused_computation.10 | convolution fusion | flops 2149580800 | bytes 8912896 | tf_op jit(solution)/shard_map/ste,ed->std/dot_general | solution.py:206
  185.3 0.0 reduce-scatter.2.cloned.1.call-update
  185.3 35.7 %reduce-scatter.2.cloned.1.call-done = bf16[16,32,512]{2,1,0:T(8,128)(2,1)} async-done(((bf16[16,32,4096]{2,1,0:T(8,128)(2,1)}), bf16[16,32,512]{2,1,0:T(8,128)(2,1)}) %reduce-scatter.2.cloned.1.call-update) | async-done | bytes 524304 | tf_op jit(solution)/shard_map/reduce_scatter | solution.py:209
  221.0 2.2 add_convert_fusion
  (22 shorter events, 0.2 us)
Async XLA Ops:
  7.2 98.0 %copy-start = (bf16[1024,1024]{1,0:T(8,128)(2,1)S(1)}, bf16[1024,1024]{1,0:T(8,128)(2,1)}, u32[]{:S(2)}) copy-start(bf16[1024,1024]{1,0:T(8,128)(2,1)} %param.19) | copy-start | bytes 6291460
  7.2 10.2 %copy-start.9 = (bf16[28,4096]{1,0:T(8,128)(2,1)S(1)}, bf16[28,4096]{1,0:T(8,128)(2,1)}, u32[]{:S(2)}) copy-start(bf16[28,4096]{1,0:T(8,128)(2,1)} %param.21) | copy-start | bytes 688132
  7.2 10.2 %copy-start.10 = (s32[16,32]{1,0:T(8,128)S(1)}, s32[16,32]{1,0:T(8,128)}, u32[]{:S(2)}) copy-start(s32[16,32]{1,0:T(8,128)} %param.20) | copy-start | bytes 6148
  7.2 13.6 %copy-start.4 = (bf16[4096,512]{1,0:T(8,128)(2,1)S(1)}, bf16[4096,512]{1,0:T(8,128)(2,1)}, u32[]{:S(2)}) copy-start(bf16[4096,512]{1,0:T(8,128)(2,1)} %param.22) | copy-start | bytes 12582916
  10.4 36.7 %collective-permute-start.1 = (bf16[2,256,1024]{2,1,0:T(8,128)(2,1)}, bf16[2,256,1024]{2,1,0:T(8,128)(2,1)}, u32[]{:S(2)}, u32[]{:S(2)}) collective-permute-start(bf16[2,256,1024]{2,1,0:T(8,128)(2,1)} %get-tuple-element.5), channel_id=1, source_target_pairs={{8,0},{16,8},{24,16},{32,24},{40,32},{48,40},{56,48},{64,56},{72,6... | collective-permute-start | bytes 3145736 | tf_op jit(solution)/shard_map/ppermute | solution.py:121
  11.9 35.3 %collective-permute-start = (bf16[2,256,1024]{2,1,0:T(8,128)(2,1)}, bf16[2,256,1024]{2,1,0:T(8,128)(2,1)}, u32[]{:S(2)}, u32[]{:S(2)}) collective-permute-start(bf16[2,256,1024]{2,1,0:T(8,128)(2,1)} %get-tuple-element.4), channel_id=1, source_target_pairs={{0,8},{8,16},{16,24},{24,32},{32,40},{40,48},{48,56},{56,64},{64,7... | collective-permute-start | bytes 3145736 | tf_op jit(solution)/shard_map/ppermute | solution.py:120
  18.8 2.0 copy-start.3
  20.8 13.4 %copy-start.11 = (s32[16]{0:T(128)S(1)}, s32[16]{0:T(128)}, u32[]{:S(2)}) copy-start(s32[16]{0:T(128)} %param.15) | copy-start | bytes 196
  20.8 13.5 %copy-start.2 = (f32[16,8192]{1,0:T(8,128)S(1)}, f32[16,8192]{1,0:T(8,128)}, u32[]{:S(2)}) copy-start(f32[16,8192]{1,0:T(8,128)} %param.14) | copy-start | bytes 1572868
  23.9 103.7 %all-to-all-start.1 = ((bf16[16,32,512]{2,1,0:T(8,128)(2,1)}), bf16[16,32,512]{2,1,0:T(8,128)(2,1)S(1)}, u32[]{:S(2)}, u32[]{:S(2)}) async-start(bf16[16,32,512]{2,1,0:T(8,128)(2,1)} %fusion.31), calls=%async_computation.1 | async-start | bytes 1048576 | tf_op jit(solution)/shard_map/all_to_all | solution.py:188
  34.4 7.9 %copy-start.1 = (bf16[2,512,1024]{2,1,0:T(8,128)(2,1)S(1)}, bf16[2,512,1024]{2,1,0:T(8,128)(2,1)}, u32[]{:S(2)}) copy-start(bf16[2,512,1024]{2,1,0:T(8,128)(2,1)} %param.13) | copy-start | bytes 6291460
  34.4 7.9 %copy-start.5 = (bf16[1024,1024]{1,0:T(8,128)(2,1)S(1)}, bf16[1024,1024]{1,0:T(8,128)(2,1)}, u32[]{:S(2)}) copy-start(bf16[1024,1024]{1,0:T(8,128)(2,1)} %param.18) | copy-start | bytes 6291460
  34.4 7.9 %copy-start.6 = (bf16[1024,1024]{1,0:T(8,128)(2,1)S(1)}, bf16[1024,1024]{1,0:T(8,128)(2,1)}, u32[]{:S(2)}) copy-start(bf16[1024,1024]{1,0:T(8,128)(2,1)} %param.17) | copy-start | bytes 6291460
  105.2 20.9 %copy-start.7 = (bf16[1024,512]{1,0:T(8,128)(2,1)S(1)}, bf16[1024,512]{1,0:T(8,128)(2,1)}, u32[]{:S(2)}) copy-start(bf16[1024,512]{1,0:T(8,128)(2,1)} %param.24) | copy-start | bytes 3145732
  105.2 20.9 %copy-start.8 = (bf16[1024,512]{1,0:T(8,128)(2,1)S(1)}, bf16[1024,512]{1,0:T(8,128)(2,1)}, u32[]{:S(2)}) copy-start(bf16[1024,512]{1,0:T(8,128)(2,1)} %param.23) | copy-start | bytes 3145732
  127.6 19.3 %all-to-all-start = ((bf16[16,16,1024]{2,1,0:T(8,128)(2,1)}), bf16[16,16,1024]{2,1,0:T(8,128)(2,1)S(1)}, u32[]{:S(2)}, u32[]{:S(2)}) async-start(bf16[16,16,1024]{2,1,0:T(8,128)(2,1)} %fusion.36), calls=%async_computation | async-start | bytes 1048576 | tf_op jit(solution)/shard_map/all_to_all | solution.py:167
  134.8 86.2 %reduce-scatter.2.cloned.1.call-start = ((), (), s32[]{:S(2)}) async-start(), calls=%async_computation.4 | async-start | bytes 4718592 | tf_op jit(solution)/shard_map/reduce_scatter | solution.py:209
Sparse Core Ops, SparseCore 0:
  185.4 35.5 reduce-scatter.1

commit v3 on v2

--- a/solution.py
+++ b/solution.py
@@ -11,6 +11,7 @@
 HD = 32
 QBLOCK = 128
 HGROUP = 512
+DEC_CHUNKS = 2
 
 
 epsilon = 1e-05
@@ -186,31 +187,41 @@
         "std,de->ste", normed_tok, dec_query, preferred_element_type=jnp.float32
     ).astype(jnp.bfloat16)
     query_one = lax.all_to_all(query_dec, "seq", 0, 1, tiled=True)
-    all_tok = query_one.shape[1]
-    query_heads = query_one.reshape(1, all_tok, heads_here, dec_head)
+    seq_count = lax.axis_size("seq")
+    query_one = query_one.reshape(seq_count, tok_count, local_width)
     key_heads = memory[:, :, :local_width].reshape(1, mem_len, heads_here, dec_head)
     value_heads = memory[:, :, local_width:].reshape(1, mem_len, heads_here, dec_head)
-    scores = (
-        jnp.einsum("sthd,sphd->shtp", query_heads, key_heads, preferred_element_type=jnp.float32)
-        * dec_head ** (-0.5)
-        + pooled_bias[:, None, None, :]
-    )
-    scores = jnp.where(mem_valid[:, None, None, :], scores, masked_score)
-    weights = softmax_rows(scores)
-    context_one = jnp.einsum(
-        "shtp,sphd->sthd", weights, value_heads, preferred_element_type=jnp.float32
-    ).astype(jnp.bfloat16)
-    context_one = context_one.reshape(1, all_tok, local_width)
-    dec_context = lax.all_to_all(context_one, "seq", 1, 0, tiled=True)
     share_width = dec_width // lax.axis_size("head")
-    partial_sums = jnp.einsum(
-        "ste,ed->std", dec_context, dec_out, preferred_element_type=jnp.float32
-    )
-    summed = lax.psum_scatter(
-        partial_sums.astype(jnp.bfloat16), "head", scatter_dimension=2, tiled=True
-    ).astype(jnp.float32)
     own_part = lax.dynamic_slice_in_dim(hidden, head_pos * share_width, share_width, 2)
-    decoded = (own_part.astype(jnp.float32) + summed).astype(jnp.bfloat16)
+    sub = tok_count // DEC_CHUNKS
+    pieces = []
+    for piece in range(DEC_CHUNKS):
+        query_piece = query_one[:, piece * sub : (piece + 1) * sub].reshape(
+            1, seq_count * sub, heads_here, dec_head
+        )
+        scores = (
+            jnp.einsum(
+                "sthd,sphd->shtp", query_piece, key_heads, preferred_element_type=jnp.float32
+            )
+            * dec_head ** (-0.5)
+            + pooled_bias[:, None, None, :]
+        )
+        scores = jnp.where(mem_valid[:, None, None, :], scores, masked_score)
+        weights = softmax_rows(scores)
+        context_piece = jnp.einsum(
+            "shtp,sphd->sthd", weights, value_heads, preferred_element_type=jnp.float32
+        ).astype(jnp.bfloat16)
+        context_piece = context_piece.reshape(seq_count, sub, local_width)
+        dec_context = lax.all_to_all(context_piece, "seq", 0, 0, tiled=True)
+        partial_sums = jnp.einsum(
+            "ste,ed->std", dec_context, dec_out, preferred_element_type=jnp.float32
+        )
+        summed = lax.psum_scatter(
+            partial_sums.astype(jnp.bfloat16), "head", scatter_dimension=2, tiled=True
+        ).astype(jnp.float32)
+        own_piece = own_part[:, piece * sub : (piece + 1) * sub]
+        pieces.append((own_piece.astype(jnp.float32) + summed).astype(jnp.bfloat16))
+    decoded = jnp.concatenate(pieces, axis=1)
     return (encoded, decoded)
 
 

time: 231 us -> 244 us (1.056)
  waiting for transfers between devices: 44.1 us -> 53.4 us
  blocking collectives: 28.5 us -> 37.4 us
  other arithmetic: 17.8 us -> 13.2 us
  local copies, waits for them, and re-layouts: 15.6 us -> 11 us
  matrix products: 42.4 us -> 46.4 us
    reduce_scatter x1 -> x2, waiting for transfers between devices: 35.7 us -> 46.5 us  [per_device(): lax.psum_scatter(partial_sums.astype(jnp.bfloat16), 'head', scatter_dimen...]
    all_to_all x1 -> x2, blocking collectives: 14.2 us -> 23.1 us  [per_device(): dec_context = lax.all_to_all(context_piece, 'seq', 0, 0, tiled=True)]
    unnamed x1 -> x0, other arithmetic: 4.66 us -> none
    unnamed x29 -> x25, local copies, waits for them, and re-layouts: 6.51 us -> 2.15 us
    dot_general x1 -> x2, matrix products: 6.46 us -> 9.54 us  [per_device(): jnp.einsum('ste,ed->std', dec_context, dec_out, preferred_element_type=jn...]
  transfers between devices with their start and end apart: 5 -> 6, of which waited for: 2 -> 3; matrix products, arithmetic and copies ran while one was open for 19% -> 22% of each run, Pallas kernels for 20% -> 19%
where the time goes in v3:
time: 244 us; the launch traced here: 243 us
  waiting for transfers between devices  53.4 us (22%)
  matrix products  46.4 us (19%)
  Pallas kernels  45 us (18%)
  blocking collectives  37.4 us (15%)
  starting transfers between devices  22.2 us (9%)
  between operations  14.4 us (6%)
  other arithmetic  13.2 us (5%)
  local copies, waits for them, and re-layouts  11 us (5%)
    reduce_scatter x2, waiting for transfers between devices, per_device(): lax.psum_scatter(partial_sums.astype(jnp.bfloat16), 'head', scatter_dimen...  46.5 us
    pallas_call x1, Pallas kernels, band_attention(): pl.pallas_call(band_kernel, out_shape=jax.ShapeDtypeStruct(query_enc.shap...  45 us
    all_to_all x2, blocking collectives, per_device(): dec_context = lax.all_to_all(context_piece, 'seq', 0, 0, tiled=True)  23.1 us
    all_gather x1, blocking collectives, per_device(): spectra_all = lax.all_gather(pooled, 'head', axis=0, tiled=True)  14.3 us
    dot_general x2, matrix products, per_device(): jnp.einsum('ste,ed->std', dec_context, dec_out, preferred_element_type=jn...  9.54 us
    all_to_all x1, starting transfers between devices, per_device(): query_one = lax.all_to_all(query_dec, 'seq', 0, 1, tiled=True)  8 us
    all_to_all x1, starting transfers between devices, per_device(): memory = lax.all_to_all(memory_part, 'seq', 0, 1, tiled=True)  7.21 us
    all_to_all x1, waiting for transfers between devices, per_device(): memory = lax.all_to_all(memory_part, 'seq', 0, 1, tiled=True)  6.89 us
  transfers between devices with their start and end apart: 6, of which 3 were waited for; matrix products, arithmetic and copies ran while one was open for 22% of the time, Pallas kernels for 19%

profile of v3, /device:TPU:0, one launch (start us, length us, event | category | flops | bytes accessed | tf_op | source)
XLA Modules:
  0.0 243.0 jit_solution(6830753675966637630)
XLA Ops:
  7.2 0.0 copy-start
  7.2 3.2 %fusion.77 = (bf16[2,256,1024]{2,1,0:T(8,128)(2,1)}, bf16[2,256,1024]{2,1,0:T(8,128)(2,1)}) fusion(bf16[2,512,1024]{2,1,0:T(8,128)(2,1)} %param.13), kind=kLoop, calls=%fused_computation.105 | loop fusion | bytes 4194304 | tf_op jit(solution)/shard_map/slice | solution.py:121
  10.4 1.4 collective-permute-start.1
  11.9 5.5 %collective-permute-start = (bf16[2,256,1024]{2,1,0:T(8,128)(2,1)}, bf16[2,256,1024]{2,1,0:T(8,128)(2,1)}, u32[]{:S(2)}, u32[]{:S(2)}) collective-permute-start(bf16[2,256,1024]{2,1,0:T(8,128)(2,1)} %get-tuple-element.6), channel_id=1, source_target_pairs={{0,8},{8,16},{16,24},{24,32},{32,40},{40,48},{48,56},{56,64},{64,7... | collective-permute-start | bytes 3145736 | tf_op jit(solution)/shard_map/ppermute | solution.py:121
  17.4 0.0 copy-done.10
  17.4 1.4 fusion.2
  18.8 2.0 copy-done.3
  20.8 3.2 %fusion.40 = bf16[16,32,512]{2,1,0:T(8,128)(2,1)} fusion(bf16[4096,512]{1,0:T(8,128)(2,1)S(1)} %copy-done.4, bf16[16,32,4096]{2,1,0:T(8,128)(2,1)S(1)} %get-tuple-element.19, f32[16,32]{1,0:T(8,128)S(1)} %add_rsqrt_fusion), kind=kOutput, calls=%fused_computation.54 | convolution fusion | flops 2154037248 | bytes 8914944 | tf_op jit(solution)/shard_map/std,de->ste/dot_general | solution.py:186
  23.9 8.0 %all-to-all-start.1 = ((bf16[16,32,512]{2,1,0:T(8,128)(2,1)}), bf16[16,32,512]{2,1,0:T(8,128)(2,1)S(1)}, u32[]{:S(2)}, u32[]{:S(2)}) async-start(bf16[16,32,512]{2,1,0:T(8,128)(2,1)} %fusion.40), calls=%async_computation.1 | async-start | bytes 1048576 | tf_op jit(solution)/shard_map/all_to_all | solution.py:189
  32.0 2.1 fusion.6
  34.1 0.1 dynamic_slice.15
  34.2 0.1 and_select_fusion
  34.4 0.0 copy-start.1
  34.4 0.0 copy-start.5
  34.4 0.0 copy-start.6
  34.4 6.1 %fusion.25.q_ref = bf16[2,512,1024]{2,1,0:T(8,128)(2,1)} fusion(bf16[1024,1024]{1,0:T(8,128)(2,1)} %param.16, bf16[2,512,1024]{2,1,0:T(8,128)(2,1)} %param.13, f32[2,512]{1,0:T(2,128)S(1)} %add_rsqrt_fusion.3), kind=kOutput, calls=%fused_computation.40 | convolution fusion | flops 2151677952 | bytes 6295552 | tf_op jit(solution)/shard_map/sbd,de->sbe/dot_general | solution.py:125
  40.5 1.7 broadcast_select_fusion.b_ref
  42.2 0.1 broadcast_compare_fusion.1
  42.3 4.9 %convolution_convert_fusion.3 = bf16[2,512,2048]{2,1,0:T(8,128)(2,1)S(1)} fusion(bf16[1024,1024]{1,0:T(8,128)(2,1)S(1)} %copy-done.5, bf16[1024,1024]{1,0:T(8,128)(2,1)S(1)} %copy-done.6, bf16[2,512,1024]{2,1,0:T(8,128)(2,1)S(1)} %copy-done.1, f32[2,512]{1,0:T(2,128)S(1)} %add_rsqrt_fusion.3), kind=kOutput, calls=%fused_computation.28 | convolution fusion | flops 4308598784 | bytes 10489856 | tf_op jit(solution)/shard_map/sbd,de->sbe/dot_general | solution.py:128
  47.2 0.0 collective-permute-done.1
  47.2 0.0 collective-permute-done
  47.2 2.0 fusion.4
  49.2 6.5 %convolution_convert_fusion.4 = bf16[2,512,2048]{2,1,0:T(8,128)(2,1)S(1)} fusion(bf16[1024,1024]{1,0:T(8,128)(2,1)S(1)} %copy-done.5, bf16[1024,1024]{1,0:T(8,128)(2,1)S(1)} %copy-done.6, f32[2,512]{1,0:T(2,128)S(1)} %add_rsqrt_fusion.2, bf16[2,256,1024]{2,1,0:T(8,128)(2,1)} %collective-permute-done.1, bf16[2,256,1024]{2,1,0:T(8,128)(2,1)} %collective-permute-done), kind=kOutput, calls=%fused_computation.29 | convolution fusion | flops 4311744512 | bytes 10489856 | tf_op jit(solution)/shard_map/sbd,de->sbe/dot_general | solution.py:132
  55.7 0.5 fusion.76
  56.2 4.0 %pad_maximum_fusion.k_ref.v_ref = bf16[2,1024,2048]{2,1,0:T(8,128)(2,1)} fusion(bf16[2,256,2048]{2,1,0:T(8,128)(2,1)S(1)} %get-tuple-element.5, bf16[2,512,2048]{2,1,0:T(8,128)(2,1)S(1)} %convolution_convert_fusion.3, bf16[2,256,2048]{2,1,0:T(8,128)(2,1)S(1)} %get-tuple-element.4), kind=kLoop, calls=%fused_computation.6 | loop fusion | flops 25165824 | bytes 16777216 | tf_op jit(solution)/shard_map/concatenate | solution.py:135
  60.2 45.0 %shard_map.140 = bf16[2,512,1024]{2,1,0:T(8,128)(2,1)} custom-call(bf16[2,512,1024]{2,1,0:T(8,128)(2,1)} %fusion.25.q_ref, bf16[2,1024,2048]{2,1,0:T(8,128)(2,1)} %pad_maximum_fusion.k_ref.v_ref, bf16[2,1024,2048]{2,1,0:T(8,128)(2,1)} %pad_maximum_fusion.k_ref.v_ref, f32[2,4,128,640]{3,2,1,0:T(8,128)} %broadcast_select_fusion.b_ref), custom_call_target="tpu_custom_call" | custom-call | flops 5368709120 | bytes 15204352 | tf_op jit(solution)/shard_map/pallas_call | solution.py:67
  105.2 0.0 copy-start.8
  105.2 6.3 %convert_reduce_fusion = (f32[2,16,1024]{2,1,0:T(8,128)S(1)}, bf16[2,512,1024]{2,1,0:T(8,128)(2,1)}) fusion(bf16[2,512,1024]{2,1,0:T(8,128)(2,1)} %shard_map.140, bf16[1024,1024]{1,0:T(8,128)(2,1)S(1)} %copy-done, bf16[2,512,1024]{2,1,0:T(8,128)(2,1)} %param.13, pred[2,512]{1,0:T(4,128)(4,1)S(1)} %broadcast_compare_fusion.1), kind=kOutput, calls=%fused_computation.23 | convolution fusion | flops 2153742336 | bytes 8520704 | tf_op jit(solution)/shard_map/sbd,de->sbe/dot_general | solution.py:154
  111.5 14.3 %all_gather.3 = bf16[16,16,1024]{2,1,0:T(8,128)(2,1)S(1)} all-gather(bf16[2,16,1024]{2,1,0:T(8,128)(2,1)S(1)} %multiply_convert_fusion), channel_id=1, replica_groups=mesh['seq'=16,'head'=8] {'head'}, dimensions={0}, use_global_device_ids=true | all-gather | bytes 589824 | tf_op jit(solution)/shard_map/all_gather | solution.py:162
  125.8 0.2 fusion.48
  126.0 1.6 fusion.45
  127.6 0.0 all-to-all-done.1
  127.6 7.2 %all-to-all-start = ((bf16[16,16,1024]{2,1,0:T(8,128)(2,1)}), bf16[16,16,1024]{2,1,0:T(8,128)(2,1)S(1)}, u32[]{:S(2)}, u32[]{:S(2)}) async-start(bf16[16,16,1024]{2,1,0:T(8,128)(2,1)} %fusion.45), calls=%async_computation | async-start | bytes 1048576 | tf_op jit(solution)/shard_map/all_to_all | solution.py:168
  134.8 0.0 reduce-scatter.3.cloned.1.call-start
  134.9 0.7 dynamic_slice.18
  135.5 1.0 dynamic-slice_reduce_fusion
  136.6 0.1 reshape.207
  136.7 0.1 reduce_max.27
  136.8 0.7 multiply_compare_fusion
  137.5 0.7 fusion.78
  138.2 1.7 reshape.205
  140.0 6.9 %all-to-all-done = bf16[16,16,1024]{2,1,0:T(8,128)(2,1)S(1)} async-done(((bf16[16,16,1024]{2,1,0:T(8,128)(2,1)}), bf16[16,16,1024]{2,1,0:T(8,128)(2,1)S(1)}, u32[]{:S(2)}, u32[]{:S(2)}) %all-to-all-start) | async-done | bytes 524320 | tf_op jit(solution)/shard_map/all_to_all | solution.py:168
  146.9 0.1 copy.35
  147.0 0.1 copy.49
  147.2 2.5 %fusion.80 = (f32[4,256]{1,0:T(4,128)S(1)}, f32[4,256,256]{1,2,0:T(8,128)}) fusion(bf16[256,4,128]{0,2,1:T(8,128)(2,1)S(1)} %bitcast.69, f32[256]{0:T(256)S(1)} %reduce_max.27, pred[256]{0:T(512)(128)(4,1)S(1)} %multiply_compare_fusion, bf16[256,4,128]{2,1,0:T(4,128)(2,1)} %reshape.205), kind=kOutput, calls=%fused_computation.108 | convolution fusion | flops 68419840 | bytes 1578240 | tf_op jit(solution)/shard_map/sub | solution.py:29
  149.7 1.5 fusion.46
  151.1 0.2 copy.40
  151.3 0.1 reshape.208
  151.4 11.5 %all_to_all.31 = bf16[16,16,512]{2,1,0:T(8,128)(2,1)S(1)} all-to-all(bf16[16,16,512]{2,1,0:T(8,128)(2,1)S(1)} %reshape.208), channel_id=1, replica_groups=mesh['seq'=16,'head'=8] {'seq'}, dimensions={0} | all-to-all | bytes 524288 | tf_op jit(solution)/shard_map/all_to_all | solution.py:215
  162.9 4.8 %convolution_convert_fusion.2 = bf16[16,16,4096]{2,1,0:T(8,128)(2,1)} fusion(bf16[16,16,512]{2,1,0:T(8,128)(2,1)S(1)} %all_to_all.31, bf16[512,4096]{1,0:T(8,128)(2,1)} %param.25), kind=kOutput, calls=%fused_computation.14 | convolution fusion | flops 1074790400 | bytes 6553600 | tf_op jit(solution)/shard_map/ste,ed->std/dot_general | solution.py:216
  167.7 0.0 reduce-scatter.3.cloned.1.call-update
  167.7 0.0 reduce-scatter.5.cloned.1.call-start
  167.8 0.1 reshape.209
  167.8 1.5 fusion.83
  169.4 1.5 fusion.47
  170.8 0.2 copy.44
  171.0 0.1 reshape.210
  171.1 11.6 %all_to_all.32 = bf16[16,16,512]{2,1,0:T(8,128)(2,1)S(1)} all-to-all(bf16[16,16,512]{2,1,0:T(8,128)(2,1)S(1)} %reshape.210), channel_id=1, replica_groups=mesh['seq'=16,'head'=8] {'seq'}, dimensions={0} | all-to-all | bytes 524288 | tf_op jit(solution)/shard_map/all_to_all | solution.py:215
  182.7 4.7 %convolution_convert_fusion.1 = bf16[16,16,4096]{2,1,0:T(8,128)(2,1)} fusion(bf16[16,16,512]{2,1,0:T(8,128)(2,1)S(1)} %all_to_all.32, bf16[512,4096]{1,0:T(8,128)(2,1)} %param.25), kind=kOutput, calls=%fused_computation.13 | convolution fusion | flops 1074790400 | bytes 6553600 | tf_op jit(solution)/shard_map/ste,ed->std/dot_general | solution.py:216
  187.5 0.0 reduce-scatter.5.cloned.1.call-update
  187.5 11.6 %reduce-scatter.3.cloned.1.call-done = bf16[16,16,512]{2,1,0:T(8,128)(2,1)} async-done(((bf16[16,16,4096]{2,1,0:T(8,128)(2,1)}), bf16[16,16,512]{2,1,0:T(8,128)(2,1)}) %reduce-scatter.3.cloned.1.call-update) | async-done | bytes 262160 | tf_op jit(solution)/shard_map/reduce_scatter | solution.py:219
  199.1 34.8 %reduce-scatter.5.cloned.1.call-done = bf16[16,16,512]{2,1,0:T(8,128)(2,1)} async-done(((bf16[16,16,4096]{2,1,0:T(8,128)(2,1)}), bf16[16,16,512]{2,1,0:T(8,128)(2,1)}) %reduce-scatter.5.cloned.1.call-update) | async-done | bytes 262160 | tf_op jit(solution)/shard_map/reduce_scatter | solution.py:219
  234.0 1.4 add_convert_fusion.1
  235.3 0.8 pad_maximum_fusion.3
  (30 shorter events, 0.2 us)
Async XLA Ops:
  7.2 98.0 %copy-start = (bf16[1024,1024]{1,0:T(8,128)(2,1)S(1)}, bf16[1024,1024]{1,0:T(8,128)(2,1)}, u32[]{:S(2)}) copy-start(bf16[1024,1024]{1,0:T(8,128)(2,1)} %param.19) | copy-start | bytes 6291460
  7.2 10.2 %copy-start.9 = (bf16[28,4096]{1,0:T(8,128)(2,1)S(1)}, bf16[28,4096]{1,0:T(8,128)(2,1)}, u32[]{:S(2)}) copy-start(bf16[28,4096]{1,0:T(8,128)(2,1)} %param.21) | copy-start | bytes 688132
  7.2 10.2 %copy-start.10 = (s32[16,32]{1,0:T(8,128)S(1)}, s32[16,32]{1,0:T(8,128)}, u32[]{:S(2)}) copy-start(s32[16,32]{1,0:T(8,128)} %param.20) | copy-start | bytes 6148
  7.2 13.6 %copy-start.4 = (bf16[4096,512]{1,0:T(8,128)(2,1)S(1)}, bf16[4096,512]{1,0:T(8,128)(2,1)}, u32[]{:S(2)}) copy-start(bf16[4096,512]{1,0:T(8,128)(2,1)} %param.22) | copy-start | bytes 12582916
  10.4 36.7 %collective-permute-start.1 = (bf16[2,256,1024]{2,1,0:T(8,128)(2,1)}, bf16[2,256,1024]{2,1,0:T(8,128)(2,1)}, u32[]{:S(2)}, u32[]{:S(2)}) collective-permute-start(bf16[2,256,1024]{2,1,0:T(8,128)(2,1)} %get-tuple-element.7), channel_id=1, source_target_pairs={{8,0},{16,8},{24,16},{32,24},{40,32},{48,40},{56,48},{64,56},{72,6... | collective-permute-start | bytes 3145736 | tf_op jit(solution)/shard_map/ppermute | solution.py:122
  11.9 35.3 %collective-permute-start = (bf16[2,256,1024]{2,1,0:T(8,128)(2,1)}, bf16[2,256,1024]{2,1,0:T(8,128)(2,1)}, u32[]{:S(2)}, u32[]{:S(2)}) collective-permute-start(bf16[2,256,1024]{2,1,0:T(8,128)(2,1)} %get-tuple-element.6), channel_id=1, source_target_pairs={{0,8},{8,16},{16,24},{24,32},{32,40},{40,48},{48,56},{56,64},{64,7... | collective-permute-start | bytes 3145736 | tf_op jit(solution)/shard_map/ppermute | solution.py:121
  18.8 2.0 copy-start.3
  20.8 13.4 %copy-start.11 = (s32[16]{0:T(128)S(1)}, s32[16]{0:T(128)}, u32[]{:S(2)}) copy-start(s32[16]{0:T(128)} %param.15) | copy-start | bytes 196
  20.8 13.5 %copy-start.2 = (f32[16,8192]{1,0:T(8,128)S(1)}, f32[16,8192]{1,0:T(8,128)}, u32[]{:S(2)}) copy-start(f32[16,8192]{1,0:T(8,128)} %param.14) | copy-start | bytes 1572868
  23.9 103.7 %all-to-all-start.1 = ((bf16[16,32,512]{2,1,0:T(8,128)(2,1)}), bf16[16,32,512]{2,1,0:T(8,128)(2,1)S(1)}, u32[]{:S(2)}, u32[]{:S(2)}) async-start(bf16[16,32,512]{2,1,0:T(8,128)(2,1)} %fusion.40), calls=%async_computation.1 | async-start | bytes 1048576 | tf_op jit(solution)/shard_map/all_to_all | solution.py:189
  34.4 7.9 %copy-start.1 = (bf16[2,512,1024]{2,1,0:T(8,128)(2,1)S(1)}, bf16[2,512,1024]{2,1,0:T(8,128)(2,1)}, u32[]{:S(2)}) copy-start(bf16[2,512,1024]{2,1,0:T(8,128)(2,1)} %param.13) | copy-start | bytes 6291460
  34.4 7.9 %copy-start.5 = (bf16[1024,1024]{1,0:T(8,128)(2,1)S(1)}, bf16[1024,1024]{1,0:T(8,128)(2,1)}, u32[]{:S(2)}) copy-start(bf16[1024,1024]{1,0:T(8,128)(2,1)} %param.18) | copy-start | bytes 6291460
  34.4 7.9 %copy-start.6 = (bf16[1024,1024]{1,0:T(8,128)(2,1)S(1)}, bf16[1024,1024]{1,0:T(8,128)(2,1)}, u32[]{:S(2)}) copy-start(bf16[1024,1024]{1,0:T(8,128)(2,1)} %param.17) | copy-start | bytes 6291460
  105.2 20.9 %copy-start.7 = (bf16[1024,512]{1,0:T(8,128)(2,1)S(1)}, bf16[1024,512]{1,0:T(8,128)(2,1)}, u32[]{:S(2)}) copy-start(bf16[1024,512]{1,0:T(8,128)(2,1)} %param.24) | copy-start | bytes 3145732
  105.2 20.9 %copy-start.8 = (bf16[1024,512]{1,0:T(8,128)(2,1)S(1)}, bf16[1024,512]{1,0:T(8,128)(2,1)}, u32[]{:S(2)}) copy-start(bf16[1024,512]{1,0:T(8,128)(2,1)} %param.23) | copy-start | bytes 3145732
  127.6 19.3 %all-to-all-start = ((bf16[16,16,1024]{2,1,0:T(8,128)(2,1)}), bf16[16,16,1024]{2,1,0:T(8,128)(2,1)S(1)}, u32[]{:S(2)}, u32[]{:S(2)}) async-start(bf16[16,16,1024]{2,1,0:T(8,128)(2,1)} %fusion.45), calls=%async_computation | async-start | bytes 1048576 | tf_op jit(solution)/shard_map/all_to_all | solution.py:168
  134.8 64.3 %reduce-scatter.3.cloned.1.call-start = ((), (), s32[]{:S(2)}) async-start(), calls=%async_computation.6 | async-start | bytes 2359296 | tf_op jit(solution)/shard_map/reduce_scatter | solution.py:219
  167.7 66.2 %reduce-scatter.5.cloned.1.call-start = ((), (), s32[]{:S(2)}) async-start(), calls=%async_computation.7 | async-start | bytes 2359296 | tf_op jit(solution)/shard_map/reduce_scatter | solution.py:219
Sparse Core Ops, SparseCore 0:
  167.8 31.2 reduce-scatter.2
  201.5 32.4 reduce-scatter.4

commit v4 on v2

--- a/solution.py
+++ b/solution.py
@@ -9,7 +9,7 @@
 WINDOW = 512
 POOL = 32
 HD = 32
-QBLOCK = 128
+QBLOCK = 256
 HGROUP = 512
 
 
@@ -175,17 +175,26 @@
     dec_width = embedding.shape[1]
     dec_head = dec_width // HD
     heads_here = local_width // dec_head
+    share_width = dec_width // lax.axis_size("head")
+    vocab = embedding.shape[0]
     onehot = (
-        token_ids[:, :, None] == jnp.arange(embedding.shape[0], dtype=jnp.int32)[None, None, :]
-    ).astype(jnp.bfloat16)
-    hidden = jnp.einsum(
-        "stv,vd->std", onehot, embedding, preferred_element_type=jnp.float32
-    ).astype(jnp.bfloat16)
-    normed_tok = rms_rows(hidden)
-    query_dec = jnp.einsum(
-        "std,de->ste", normed_tok, dec_query, preferred_element_type=jnp.float32
-    ).astype(jnp.bfloat16)
-    query_one = lax.all_to_all(query_dec, "seq", 0, 1, tiled=True)
+        token_ids[:, :, None] == jnp.arange(vocab, dtype=jnp.int32)[None, None, :]
+    ).astype(jnp.bfloat16)
+    own_table = lax.dynamic_slice_in_dim(embedding, head_pos * share_width, share_width, 1)
+    own_part = jnp.einsum(
+        "stv,vd->std", onehot, own_table, preferred_element_type=jnp.float32
+    ).astype(jnp.bfloat16)
+    ids_all = lax.all_gather(token_ids, "seq", axis=1, tiled=True)
+    ids_one = lax.dynamic_slice_in_dim(ids_all, seq_pos, 1, 0)
+    onehot_one = (
+        ids_one[:, :, None] == jnp.arange(vocab, dtype=jnp.int32)[None, None, :]
+    ).astype(jnp.bfloat16)
+    hidden_one = jnp.einsum(
+        "stv,vd->std", onehot_one, embedding, preferred_element_type=jnp.float32
+    ).astype(jnp.bfloat16)
+    query_one = jnp.einsum(
+        "std,de->ste", rms_rows(hidden_one), dec_query, preferred_element_type=jnp.float32
+    ).astype(jnp.bfloat16)
     all_tok = query_one.shape[1]
     query_heads = query_one.reshape(1, all_tok, heads_here, dec_head)
     key_heads = memory[:, :, :local_width].reshape(1, mem_len, heads_here, dec_head)
@@ -202,14 +211,12 @@
     ).astype(jnp.bfloat16)
     context_one = context_one.reshape(1, all_tok, local_width)
     dec_context = lax.all_to_all(context_one, "seq", 1, 0, tiled=True)
-    share_width = dec_width // lax.axis_size("head")
     partial_sums = jnp.einsum(
         "ste,ed->std", dec_context, dec_out, preferred_element_type=jnp.float32
     )
     summed = lax.psum_scatter(
         partial_sums.astype(jnp.bfloat16), "head", scatter_dimension=2, tiled=True
     ).astype(jnp.float32)
-    own_part = lax.dynamic_slice_in_dim(hidden, head_pos * share_width, share_width, 2)
     decoded = (own_part.astype(jnp.float32) + summed).astype(jnp.bfloat16)
     return (encoded, decoded)
 

time: 231 us -> 248 us (1.074)
  blocking collectives: 28.5 us -> 67.3 us
  Pallas kernels: 45 us -> 30.1 us
  matrix products: 42.4 us -> 52.5 us
  starting transfers between devices: 22.2 us -> 12.7 us
  waiting for transfers between devices: 44.1 us -> 40.6 us
  other arithmetic: 17.8 us -> 14.7 us
    all_gather x0 -> x1, blocking collectives: none -> 38.8 us  [per_device(): ids_all = lax.all_gather(token_ids, 'seq', axis=1, tiled=True)]
    pallas_call x1, Pallas kernels: 45 us -> 30.1 us  [band_attention(): pl.pallas_call(band_kernel, out_shape=jax.ShapeDtypeStruct(query_enc.shap...]
    dot_general x2 -> x3, matrix products: 4.55 us -> 13.3 us  [the longest x1 6.72 us: per_device(): jnp.einsum('std,de->ste', rms_rows(hidden_one), dec_query, preferred_elem...]
    all_to_all x1 -> x0, starting transfers between devices: 8 us -> none  [per_device(): query_one = lax.all_to_all(query_dec, 'seq', 0, 1, tiled=True)]
    all_to_all x1, waiting for transfers between devices: 8.44 us -> 5.04 us  [per_device(): memory = lax.all_to_all(memory_part, 'seq', 0, 1, tiled=True)]
    unnamed x29 -> x25, local copies, waits for them, and re-layouts: 6.51 us -> 5.56 us
  transfers between devices with their start and end apart: 5 -> 4, of which waited for: 2 -> 2; matrix products, arithmetic and copies ran while one was open for 19% -> 13% of each run, Pallas kernels for 20% -> 0%
where the time goes in v4:
time: 248 us; the launch traced here: 247 us
  blocking collectives  67.3 us (27%)
  matrix products  52.5 us (21%)
  waiting for transfers between devices  40.6 us (16%)
  Pallas kernels  30.1 us (12%)
  other arithmetic  14.7 us (6%)
  local copies, waits for them, and re-layouts  14.4 us (6%)
  between operations  14.4 us (6%)
  starting transfers between devices  12.7 us (5%)
    all_gather x1, blocking collectives, per_device(): ids_all = lax.all_gather(token_ids, 'seq', axis=1, tiled=True)  38.8 us
    reduce_scatter x1, waiting for transfers between devices, per_device(): lax.psum_scatter(partial_sums.astype(jnp.bfloat16), 'head', scatter_dimen...  35.5 us
    pallas_call x1, Pallas kernels, band_attention(): pl.pallas_call(band_kernel, out_shape=jax.ShapeDtypeStruct(query_enc.shap...  30.1 us
    all_gather x1, blocking collectives, per_device(): spectra_all = lax.all_gather(pooled, 'head', axis=0, tiled=True)  14.4 us
    all_to_all x1, blocking collectives, per_device(): dec_context = lax.all_to_all(context_one, 'seq', 1, 0, tiled=True)  14.2 us
    dot_general x1, matrix products, per_device(): jnp.einsum('sbd,de->sbe', normed, kv_weights, preferred_element_type=jnp....  6.77 us
    dot_general x1, matrix products, per_device(): jnp.einsum('std,de->ste', rms_rows(hidden_one), dec_query, preferred_elem...  6.72 us
    dot_general x1, matrix products, per_device(): jnp.einsum('ste,ed->std', dec_context, dec_out, preferred_element_type=jn...  6.46 us
  transfers between devices with their start and end apart: 4, of which 2 were waited for; matrix products, arithmetic and copies ran while one was open for 13% of the time, Pallas kernels for 0%

profile of v4, /device:TPU:0, one launch (start us, length us, event | category | flops | bytes accessed | tf_op | source)
XLA Modules:
  0.0 246.8 jit_solution(6474129514860707599)
XLA Ops:
  7.2 0.0 copy-start
  7.2 0.0 copy-start.1
  7.2 0.0 copy-start.8
  7.2 0.0 copy-start.3
  7.2 3.2 %fusion.61 = (bf16[2,256,1024]{2,1,0:T(8,128)(2,1)}, bf16[2,256,1024]{2,1,0:T(8,128)(2,1)}) fusion(bf16[2,512,1024]{2,1,0:T(8,128)(2,1)} %param.13), kind=kLoop, calls=%fused_computation.93 | loop fusion | bytes 4194304 | tf_op jit(solution)/shard_map/slice | solution.py:120
  10.4 1.3 collective-permute-start.1
  11.7 5.5 %collective-permute-start = (bf16[2,256,1024]{2,1,0:T(8,128)(2,1)}, bf16[2,256,1024]{2,1,0:T(8,128)(2,1)}, u32[]{:S(2)}, u32[]{:S(2)}) collective-permute-start(bf16[2,256,1024]{2,1,0:T(8,128)(2,1)} %get-tuple-element.4), channel_id=1, source_target_pairs={{0,8},{8,16},{16,24},{24,32},{32,40},{40,48},{48,56},{56,64},{64,7... | collective-permute-start | bytes 3145736 | tf_op jit(solution)/shard_map/ppermute | solution.py:120
  17.3 0.0 copy-done.1
  17.3 0.5 fusion.5
  17.8 0.1 fusion.45
  17.9 0.0 copy-done.8
  17.9 0.1 dynamic_slice.18
  18.0 0.6 dynamic_slice.21
  18.6 1.0 dynamic-slice_reduce_fusion
  19.6 0.8 and_select_fusion
  20.5 0.1 broadcast_compare_fusion.1
  20.6 0.1 reshape.200
  20.7 0.7 multiply_compare_fusion
  21.3 0.0 copy-done.3
  21.3 38.8 %all-gather = s32[16,32,16]{1,2,0:T(8,128)S(1)} all-gather(s32[1,32,16]{1,2,0:T(8,128)S(1)} %bitcast.67), channel_id=1, replica_groups=mesh['seq'=16,'head'=8] {'seq'}, dimensions={0}, use_global_device_ids=true | all-gather | bytes 34816 | tf_op jit(solution)/shard_map/all_gather | solution.py:187
  60.2 0.7 copy.38
  60.9 1.0 reshape.205
  61.9 5.9 %fusion.22.q_ref = bf16[2,512,1024]{2,1,0:T(8,128)(2,1)} fusion(bf16[1024,1024]{1,0:T(8,128)(2,1)} %param.16, bf16[2,512,1024]{2,1,0:T(8,128)(2,1)} %param.13, f32[2,512]{1,0:T(2,128)S(1)} %add_rsqrt_fusion.2), kind=kOutput, calls=%fused_computation.39 | convolution fusion | flops 2151677952 | bytes 6295552 | tf_op jit(solution)/shard_map/sbd,de->sbe/dot_general | solution.py:124
  67.8 1.9 broadcast_select_fusion.b_ref
  69.7 0.1 reduce_max.18
  69.8 0.0 copy-start.2
  69.9 0.0 copy-start.4
  69.9 4.4 %fusion.1 = (f32[512]{0:T(512)S(1)}, bf16[512,4096]{1,0:T(8,128)(2,1)}) fusion(bf16[28,4096]{1,0:T(8,128)(2,1)} %param.21, s32[512]{0:T(512)S(1)} %bitcast.68), kind=kOutput, calls=%fused_computation.3 | convolution fusion | flops 125842944 | bytes 4427776 | tf_op jit(solution)/shard_map/stv,vd->std/dot_general | solution.py:192
  74.2 0.0 copy-done.2
  74.3 0.0 copy-start.5
  74.3 6.8 %convolution_convert_fusion.2 = bf16[2,512,2048]{2,1,0:T(8,128)(2,1)S(1)} fusion(bf16[1024,1024]{1,0:T(8,128)(2,1)S(1)} %copy-done.4, bf16[1024,1024]{1,0:T(8,128)(2,1)} %param.17, bf16[2,512,1024]{2,1,0:T(8,128)(2,1)S(1)} %copy-done.2, f32[2,512]{1,0:T(2,128)S(1)} %add_rsqrt_fusion.2), kind=kOutput, calls=%fused_computation.24 | convolution fusion | flops 4308598784 | bytes 10489856 | tf_op jit(solution)/shard_map/sbd,de->sbe/dot_general | solution.py:127
  81.0 0.0 collective-permute-done.1
  81.1 0.0 collective-permute-done
  81.1 1.7 fusion.3
  82.8 6.1 %convolution_convert_fusion.3 = bf16[2,512,2048]{2,1,0:T(8,128)(2,1)S(1)} fusion(bf16[1024,1024]{1,0:T(8,128)(2,1)S(1)} %copy-done.4, bf16[1024,1024]{1,0:T(8,128)(2,1)S(1)} %copy-done.5, f32[2,512]{1,0:T(2,128)S(1)} %add_rsqrt_fusion.1, bf16[2,256,1024]{2,1,0:T(8,128)(2,1)S(1)} %collective-permute-done.1, bf16[2,256,1024]{2,1,0:T(8,128)(2,1)} %collective-permute-done), kind=kOutput, calls=%fused_computation.25 | convolution fusion | flops 4311744512 | bytes 10489856 | tf_op jit(solution)/shard_map/sbd,de->sbe/dot_general | solution.py:131
  89.0 0.5 fusion.60
  89.5 4.0 %pad_maximum_fusion.k_ref.v_ref = bf16[2,1024,2048]{2,1,0:T(8,128)(2,1)} fusion(bf16[2,256,2048]{2,1,0:T(8,128)(2,1)S(1)} %get-tuple-element.3, bf16[2,512,2048]{2,1,0:T(8,128)(2,1)S(1)} %convolution_convert_fusion.2, bf16[2,256,2048]{2,1,0:T(8,128)(2,1)S(1)} %get-tuple-element.2), kind=kLoop, calls=%fused_computation.5 | loop fusion | flops 25165824 | bytes 16777216 | tf_op jit(solution)/shard_map/concatenate | solution.py:134
  93.4 30.1 %shard_map.140 = bf16[2,512,1024]{2,1,0:T(8,128)(2,1)} custom-call(bf16[2,512,1024]{2,1,0:T(8,128)(2,1)} %fusion.22.q_ref, bf16[2,1024,2048]{2,1,0:T(8,128)(2,1)} %pad_maximum_fusion.k_ref.v_ref, bf16[2,1024,2048]{2,1,0:T(8,128)(2,1)} %pad_maximum_fusion.k_ref.v_ref, f32[2,2,256,768]{3,2,1,0:T(8,128)} %broadcast_select_fusion.b_ref), custom_call_target="tpu_custom_call" | custom-call | flops 6442450944 | bytes 15728640 | tf_op jit(solution)/shard_map/pallas_call | solution.py:66
  123.5 0.0 copy-done
  123.5 0.0 copy-start.7
  123.5 6.3 %convert_reduce_fusion = (f32[2,16,1024]{2,1,0:T(8,128)S(1)}, bf16[2,512,1024]{2,1,0:T(8,128)(2,1)}) fusion(bf16[2,512,1024]{2,1,0:T(8,128)(2,1)} %shard_map.140, bf16[1024,1024]{1,0:T(8,128)(2,1)S(1)} %copy-done, bf16[2,512,1024]{2,1,0:T(8,128)(2,1)} %param.13, pred[2,512]{1,0:T(4,128)(4,1)S(1)} %broadcast_compare_fusion.1), kind=kOutput, calls=%fused_computation.21 | convolution fusion | flops 2153742336 | bytes 8520704 | tf_op jit(solution)/shard_map/sbd,de->sbe/dot_general | solution.py:153
  129.9 14.4 %all_gather.6 = bf16[16,16,1024]{2,1,0:T(8,128)(2,1)S(1)} all-gather(bf16[2,16,1024]{2,1,0:T(8,128)(2,1)S(1)} %multiply_convert_fusion), channel_id=1, replica_groups=mesh['seq'=16,'head'=8] {'head'}, dimensions={0}, use_global_device_ids=true | all-gather | bytes 589824 | tf_op jit(solution)/shard_map/all_gather | solution.py:161
  144.2 0.2 fusion.37
  144.4 0.0 copy-done.7
  144.4 1.6 fusion.33
  146.0 5.7 %all-to-all-start = ((bf16[16,16,1024]{2,1,0:T(8,128)(2,1)}), bf16[16,16,1024]{2,1,0:T(8,128)(2,1)S(1)}, u32[]{:S(2)}, u32[]{:S(2)}) async-start(bf16[16,16,1024]{2,1,0:T(8,128)(2,1)} %fusion.33), calls=%async_computation | async-start | bytes 1048576 | tf_op jit(solution)/shard_map/all_to_all | solution.py:167
  151.7 0.3 reduce-scatter.2.cloned.1.call-start
  151.9 6.7 %fusion.30 = bf16[512,512]{0,1:T(8,128)(2,1)} fusion(bf16[4096,512]{1,0:T(8,128)(2,1)} %param.22, bf16[512,4096]{1,0:T(8,128)(2,1)} %get-tuple-element.13, f32[512]{0:T(512)S(1)} %add_rsqrt_fusion.3), kind=kOutput, calls=%fused_computation.44 | convolution fusion | flops 2154037248 | bytes 8914944 | tf_op jit(solution)/shard_map/std,de->ste/dot_general | solution.py:195
  158.7 5.0 %all-to-all-done = bf16[16,16,1024]{2,1,0:T(8,128)(2,1)S(1)} async-done(((bf16[16,16,1024]{2,1,0:T(8,128)(2,1)}), bf16[16,16,1024]{2,1,0:T(8,128)(2,1)S(1)}, u32[]{:S(2)}, u32[]{:S(2)}) %all-to-all-start) | async-done | bytes 524320 | tf_op jit(solution)/shard_map/all_to_all | solution.py:167
  163.8 0.1 copy.37
  163.9 0.1 copy.48
  164.0 3.3 %fusion.63 = (f32[4,512]{1,0:T(4,128)S(1)}, f32[4,512,256]{1,2,0:T(8,128)}) fusion(f32[256]{0:T(256)S(1)} %reduce_max.18, pred[256]{0:T(512)(128)(4,1)S(1)} %multiply_compare_fusion, bf16[512,4,128]{0,2,1:T(8,128)(2,1)} %bitcast.69, bf16[256,4,128]{0,2,1:T(8,128)(2,1)S(1)} %bitcast.66), kind=kOutput, calls=%fused_computation.95 | convolution fusion | flops 136839424 | bytes 2893056 | tf_op jit(solution)/shard_map/sub | solution.py:28
  167.3 2.7 %convolution_convert_fusion.4 = bf16[4,128,512]{2,1,0:T(8,128)(2,1)} fusion(bf16[256,4,128]{0,2,1:T(8,128)(2,1)S(1)} %bitcast.65, f32[4,512,256]{1,2,0:T(8,128)} %get-tuple-element.15, f32[4,512]{1,0:T(4,128)S(1)} %get-tuple-element.14), kind=kOutput, calls=%fused_computation.45 | convolution fusion | flops 135528448 | bytes 2891776 | tf_op jit(solution)/shard_map/shtp,sphd->sthd/dot_general | solution.py:209
  170.0 2.4 copy.43
  172.5 0.6 broadcast.144
  173.1 4.7 %reduce.11 = bf16[512,512]{1,0:T(8,128)(2,1)} reduce(bf16[512,1,512]{2,1,0:T(2,128)(2,1)S(1)} %bitcast.61, bf16[]{:T(256)} %broadcast.144), dimensions={1}, to_apply=%bitcast.49.reduce_sub_computation | reduce | bytes 1048578
  177.7 1.4 reshape.221
  179.1 14.2 %all_to_all.24 = bf16[16,2,8192]{2,1,0:T(2,128)(2,1)} all-to-all(bf16[16,2,8192]{2,1,0:T(2,128)(2,1)S(1)} %reshape.221), channel_id=1, replica_groups=mesh['seq'=16,'head'=8] {'seq'}, dimensions={0} | all-to-all | bytes 1048576 | tf_op jit(solution)/shard_map/all_to_all | solution.py:213
  193.3 2.2 reshape.222
  195.5 0.1 copy.47
  195.7 6.5 %convolution_convert_fusion.1 = bf16[16,32,4096]{2,1,0:T(8,128)(2,1)} fusion(bf16[16,32,512]{2,1,0:T(8,128)(2,1)S(1)} %bitcast.64, bf16[512,4096]{1,0:T(8,128)(2,1)} %param.25), kind=kOutput, calls=%fused_computation.10 | convolution fusion | flops 2149580800 | bytes 8912896 | tf_op jit(solution)/shard_map/ste,ed->std/dot_general | solution.py:214
  202.1 0.0 reduce-scatter.2.cloned.1.call-update
  202.2 35.5 %reduce-scatter.2.cloned.1.call-done = bf16[16,32,512]{2,1,0:T(8,128)(2,1)} async-done(((bf16[16,32,4096]{2,1,0:T(8,128)(2,1)}), bf16[16,32,512]{2,1,0:T(8,128)(2,1)}) %reduce-scatter.2.cloned.1.call-update) | async-done | bytes 524304 | tf_op jit(solution)/shard_map/reduce_scatter | solution.py:217
  237.7 2.2 fusion.36
  (17 shorter events, 0.1 us)
Async XLA Ops:
  7.2 116.3 %copy-start = (bf16[1024,1024]{1,0:T(8,128)(2,1)S(1)}, bf16[1024,1024]{1,0:T(8,128)(2,1)}, u32[]{:S(2)}) copy-start(bf16[1024,1024]{1,0:T(8,128)(2,1)} %param.19) | copy-start | bytes 6291460
  7.2 10.1 %copy-start.1 = (bf16[2,512,1024]{2,1,0:T(8,128)(2,1)S(1)}, bf16[2,512,1024]{2,1,0:T(8,128)(2,1)}, u32[]{:S(2)}) copy-start(bf16[2,512,1024]{2,1,0:T(8,128)(2,1)} %param.13) | copy-start | bytes 6291460
  7.2 10.7 %copy-start.8 = (s32[16]{0:T(128)S(1)}, s32[16]{0:T(128)}, u32[]{:S(2)}) copy-start(s32[16]{0:T(128)} %param.15) | copy-start | bytes 196
  7.2 14.1 %copy-start.3 = (s32[16,32]{1,0:T(8,128)S(1)}, s32[16,32]{1,0:T(8,128)}, u32[]{:S(2)}) copy-start(s32[16,32]{1,0:T(8,128)} %param.20) | copy-start | bytes 6148
  10.4 70.6 %collective-permute-start.1 = (bf16[2,256,1024]{2,1,0:T(8,128)(2,1)}, bf16[2,256,1024]{2,1,0:T(8,128)(2,1)S(1)}, u32[]{:S(2)}, u32[]{:S(2)}) collective-permute-start(bf16[2,256,1024]{2,1,0:T(8,128)(2,1)} %get-tuple-element.5), channel_id=1, source_target_pairs={{8,0},{16,8},{24,16},{32,24},{40,32},{48,40},{56,48},{64,56},{72,6... | collective-permute-start | bytes 3145736 | tf_op jit(solution)/shard_map/ppermute | solution.py:121
  11.7 69.3 %collective-permute-start = (bf16[2,256,1024]{2,1,0:T(8,128)(2,1)}, bf16[2,256,1024]{2,1,0:T(8,128)(2,1)}, u32[]{:S(2)}, u32[]{:S(2)}) collective-permute-start(bf16[2,256,1024]{2,1,0:T(8,128)(2,1)} %get-tuple-element.4), channel_id=1, source_target_pairs={{0,8},{8,16},{16,24},{24,32},{32,40},{40,48},{48,56},{56,64},{64,7... | collective-permute-start | bytes 3145736 | tf_op jit(solution)/shard_map/ppermute | solution.py:120
  69.8 4.4 %copy-start.2 = (bf16[2,512,1024]{2,1,0:T(8,128)(2,1)S(1)}, bf16[2,512,1024]{2,1,0:T(8,128)(2,1)}, u32[]{:S(2)}) copy-start(bf16[2,512,1024]{2,1,0:T(8,128)(2,1)} %param.13) | copy-start | bytes 6291460
  69.9 4.4 %copy-start.4 = (bf16[1024,1024]{1,0:T(8,128)(2,1)S(1)}, bf16[1024,1024]{1,0:T(8,128)(2,1)}, u32[]{:S(2)}) copy-start(bf16[1024,1024]{1,0:T(8,128)(2,1)} %param.18) | copy-start | bytes 6291460
  74.3 8.5 %copy-start.5 = (bf16[1024,1024]{1,0:T(8,128)(2,1)S(1)}, bf16[1024,1024]{1,0:T(8,128)(2,1)}, u32[]{:S(2)}) copy-start(bf16[1024,1024]{1,0:T(8,128)(2,1)} %param.17) | copy-start | bytes 6291460
  123.5 20.9 %copy-start.6 = (bf16[1024,512]{1,0:T(8,128)(2,1)S(1)}, bf16[1024,512]{1,0:T(8,128)(2,1)}, u32[]{:S(2)}) copy-start(bf16[1024,512]{1,0:T(8,128)(2,1)} %param.24) | copy-start | bytes 3145732
  123.5 20.9 %copy-start.7 = (bf16[1024,512]{1,0:T(8,128)(2,1)S(1)}, bf16[1024,512]{1,0:T(8,128)(2,1)}, u32[]{:S(2)}) copy-start(bf16[1024,512]{1,0:T(8,128)(2,1)} %param.23) | copy-start | bytes 3145732
  146.0 17.7 %all-to-all-start = ((bf16[16,16,1024]{2,1,0:T(8,128)(2,1)}), bf16[16,16,1024]{2,1,0:T(8,128)(2,1)S(1)}, u32[]{:S(2)}, u32[]{:S(2)}) async-start(bf16[16,16,1024]{2,1,0:T(8,128)(2,1)} %fusion.33), calls=%async_computation | async-start | bytes 1048576 | tf_op jit(solution)/shard_map/all_to_all | solution.py:167
  151.7 86.0 %reduce-scatter.2.cloned.1.call-start = ((), (), s32[]{:S(2)}) async-start(), calls=%async_computation.3 | async-start | bytes 4718592 | tf_op jit(solution)/shard_map/reduce_scatter | solution.py:217
Sparse Core Ops, SparseCore 0:
  202.3 35.3 reduce-scatter.1

commit v5 on v4

--- a/solution.py
+++ b/solution.py
@@ -164,14 +164,22 @@
     memory_part = jnp.einsum(
         "spd,de->spe", rms_rows(spectra_all), mem_weights, preferred_element_type=jnp.float32
     ).astype(jnp.bfloat16)
-    memory = lax.all_to_all(memory_part, "seq", 0, 1, tiled=True)
-    spec_count = key_bias.shape[0]
+    spec_count, part_len, part_width = memory_part.shape
+    tok_count = token_ids.shape[1]
+    id_rows = jnp.zeros((spec_count, 1, part_width), jnp.bfloat16)
+    id_rows = id_rows.at[:, 0, :tok_count].set(token_ids.astype(jnp.bfloat16))
+    payload = jnp.concatenate([memory_part, id_rows], axis=1)
+    received = lax.all_to_all(payload, "seq", 0, 1, tiled=True)
+    seq_count = lax.axis_size("seq")
+    received = received.reshape(seq_count, part_len + 1, part_width)
+    memory = received[:, :part_len].reshape(1, seq_count * part_len, part_width)
+    ids_one = received[:, part_len, :tok_count].reshape(1, seq_count * tok_count)
+    ids_one = ids_one.astype(jnp.int32)
     mem_len = memory.shape[1]
     bias_row = lax.dynamic_slice_in_dim(key_bias, seq_pos, 1, 0)
     pooled_bias = jnp.max(bias_row.reshape(1, mem_len, POOL), axis=2)
     count_row = lax.dynamic_slice_in_dim(valid_bins, seq_pos, 1, 0)
     mem_valid = jnp.arange(mem_len, dtype=jnp.int32)[None, :] * POOL < count_row[:, None]
-    tok_count = token_ids.shape[1]
     dec_width = embedding.shape[1]
     dec_head = dec_width // HD
     heads_here = local_width // dec_head
@@ -184,8 +192,6 @@
     own_part = jnp.einsum(
         "stv,vd->std", onehot, own_table, preferred_element_type=jnp.float32
     ).astype(jnp.bfloat16)
-    ids_all = lax.all_gather(token_ids, "seq", axis=1, tiled=True)
-    ids_one = lax.dynamic_slice_in_dim(ids_all, seq_pos, 1, 0)
     onehot_one = (
         ids_one[:, :, None] == jnp.arange(vocab, dtype=jnp.int32)[None, None, :]
     ).astype(jnp.bfloat16)

time: 248 us -> 223 us (0.90)
  blocking collectives: 67.3 us -> 29.3 us
  waiting for transfers between devices: 40.6 us -> 54.3 us
  matrix products: 52.5 us -> 48.1 us
  starting transfers between devices: 12.7 us -> 16.7 us
    all_gather x1 -> x0, blocking collectives: 38.8 us -> none  [per_device(): ids_all = lax.all_gather(token_ids, 'seq', axis=1, tiled=True)]
    all_to_all x1, waiting for transfers between devices: 5.04 us -> 12.3 us  [per_device(): received = lax.all_to_all(payload, 'seq', 0, 1, tiled=True)]
    ppermute x1, waiting for transfers between devices: 0.01 us -> 5.09 us  [per_device(): high_edge = lax.ppermute(spectra[:, :half_span], 'seq', backward)]
    all_to_all x1, starting transfers between devices: 5.66 us -> 9.87 us  [per_device(): received = lax.all_to_all(payload, 'seq', 0, 1, tiled=True)]
  transfers between devices with their start and end apart: 4 -> 4, of which waited for: 2 -> 4; matrix products, arithmetic and copies ran while one was open for 13% -> 8% of each run, Pallas kernels for 0% -> 0%
where the time goes in v5:
time: 223 us; the launch traced here: 222 us
  waiting for transfers between devices  54.3 us (24%)
  matrix products  48.1 us (22%)
  Pallas kernels  30.1 us (13%)
  blocking collectives  29.3 us (13%)
  starting transfers between devices  16.7 us (7%)
  other arithmetic  15.8 us (7%)
  between operations  14.4 us (6%)
  local copies, waits for them, and re-layouts  13.5 us (6%)
    reduce_scatter x1, waiting for transfers between devices, per_device(): lax.psum_scatter(partial_sums.astype(jnp.bfloat16), 'head', scatter_dimen...  35.7 us
    pallas_call x1, Pallas kernels, band_attention(): pl.pallas_call(band_kernel, out_shape=jax.ShapeDtypeStruct(query_enc.shap...  30.1 us
    all_gather x1, blocking collectives, per_device(): spectra_all = lax.all_gather(pooled, 'head', axis=0, tiled=True)  14.8 us
    all_to_all x1, blocking collectives, per_device(): dec_context = lax.all_to_all(context_one, 'seq', 1, 0, tiled=True)  14.5 us
    all_to_all x1, waiting for transfers between devices, per_device(): received = lax.all_to_all(payload, 'seq', 0, 1, tiled=True)  12.3 us
    all_to_all x1, starting transfers between devices, per_device(): received = lax.all_to_all(payload, 'seq', 0, 1, tiled=True)  9.87 us
    dot_general x1, matrix products, per_device(): jnp.einsum('ste,ed->std', dec_context, dec_out, preferred_element_type=jn...  6.47 us
    dot_general x1, matrix products, per_device(): jnp.einsum('sbd,de->sbe', context, enc_out, preferred_element_type=jnp.fl...  6.33 us
  transfers between devices with their start and end apart: 4, of which 4 were waited for; matrix products, arithmetic and copies ran while one was open for 8% of the time, Pallas kernels for 0%

profile of v5, /device:TPU:0, one launch (start us, length us, event | category | flops | bytes accessed | tf_op | source)
XLA Modules:
  0.0 222.3 jit_solution(9572851843820703897)
XLA Ops:
  7.2 0.0 copy-start
  7.2 0.0 copy-start.1
  7.2 0.0 copy-start.9
  7.2 0.0 copy-start.4
  7.2 3.2 %fusion.64 = (bf16[2,256,1024]{2,1,0:T(8,128)(2,1)}, bf16[2,256,1024]{2,1,0:T(8,128)(2,1)}) fusion(bf16[2,512,1024]{2,1,0:T(8,128)(2,1)} %param.15), kind=kLoop, calls=%fused_computation.98 | loop fusion | bytes 4194304 | tf_op jit(solution)/shard_map/slice | solution.py:120
  10.4 1.3 collective-permute-start.1
  11.7 5.5 %collective-permute-start = (bf16[2,256,1024]{2,1,0:T(8,128)(2,1)}, bf16[2,256,1024]{2,1,0:T(8,128)(2,1)}, u32[]{:S(2)}, u32[]{:S(2)}) collective-permute-start(bf16[2,256,1024]{2,1,0:T(8,128)(2,1)} %get-tuple-element.16), channel_id=1, source_target_pairs={{0,8},{8,16},{16,24},{24,32},{32,40},{40,48},{48,56},{56,64},{64,7... | collective-permute-start | bytes 3145736 | tf_op jit(solution)/shard_map/ppermute | solution.py:120
  17.3 0.0 copy-done.1
  17.3 0.5 fusion.5
  17.8 0.1 fusion.47
  17.9 0.0 copy-done.9
  17.9 0.1 dynamic_slice.15
  18.0 0.8 and_select_fusion
  18.9 0.0 copy-done.4
  18.9 0.0 copy-start.2
  18.9 0.0 copy-start.5
  18.9 0.0 copy-start.6
  18.9 6.1 %fusion.22.q_ref = bf16[2,512,1024]{2,1,0:T(8,128)(2,1)} fusion(bf16[1024,1024]{1,0:T(8,128)(2,1)} %param.18, bf16[2,512,1024]{2,1,0:T(8,128)(2,1)} %param.15, f32[2,512]{1,0:T(2,128)S(1)} %add_rsqrt_fusion.2), kind=kOutput, calls=%fused_computation.39 | convolution fusion | flops 2151677952 | bytes 6295552 | tf_op jit(solution)/shard_map/sbd,de->sbe/dot_general | solution.py:124
  25.0 2.0 broadcast_select_fusion.b_ref
  27.0 0.1 broadcast_compare_fusion.1
  27.1 0.0 copy-done.2
  27.1 0.0 copy-done.5
  27.1 5.1 %convolution_convert_fusion.2 = bf16[2,512,2048]{2,1,0:T(8,128)(2,1)S(1)} fusion(bf16[1024,1024]{1,0:T(8,128)(2,1)S(1)} %copy-done.5, bf16[1024,1024]{1,0:T(8,128)(2,1)S(1)} %copy-done.6, bf16[2,512,1024]{2,1,0:T(8,128)(2,1)S(1)} %copy-done.2, f32[2,512]{1,0:T(2,128)S(1)} %add_rsqrt_fusion.2), kind=kOutput, calls=%fused_computation.24 | convolution fusion | flops 4308598784 | bytes 10489856 | tf_op jit(solution)/shard_map/sbd,de->sbe/dot_general | solution.py:127
  32.2 5.1 %collective-permute-done.1 = bf16[2,256,1024]{2,1,0:T(8,128)(2,1)S(1)} collective-permute-done((bf16[2,256,1024]{2,1,0:T(8,128)(2,1)}, bf16[2,256,1024]{2,1,0:T(8,128)(2,1)S(1)}, u32[]{:S(2)}, u32[]{:S(2)}) %collective-permute-start.1) | collective-permute-done | bytes 1048608 | tf_op jit(solution)/shard_map/ppermute | solution.py:121
  37.3 1.3 collective-permute-done
  38.6 1.7 fusion.3
  40.3 6.1 %convolution_convert_fusion.3 = bf16[2,512,2048]{2,1,0:T(8,128)(2,1)S(1)} fusion(bf16[1024,1024]{1,0:T(8,128)(2,1)S(1)} %copy-done.5, bf16[1024,1024]{1,0:T(8,128)(2,1)S(1)} %copy-done.6, f32[2,512]{1,0:T(2,128)S(1)} %add_rsqrt_fusion.1, bf16[2,256,1024]{2,1,0:T(8,128)(2,1)S(1)} %collective-permute-done.1, bf16[2,256,1024]{2,1,0:T(8,128)(2,1)} %collective-permute-done), kind=kOutput, calls=%fused_computation.25 | convolution fusion | flops 4311744512 | bytes 10489856 | tf_op jit(solution)/shard_map/sbd,de->sbe/dot_general | solution.py:131
  46.4 0.5 fusion.63
  46.9 4.0 %pad_maximum_fusion.k_ref.v_ref = bf16[2,1024,2048]{2,1,0:T(8,128)(2,1)} fusion(bf16[2,256,2048]{2,1,0:T(8,128)(2,1)S(1)} %get-tuple-element.15, bf16[2,512,2048]{2,1,0:T(8,128)(2,1)S(1)} %convolution_convert_fusion.2, bf16[2,256,2048]{2,1,0:T(8,128)(2,1)S(1)} %get-tuple-element.14), kind=kLoop, calls=%fused_computation.5 | loop fusion | flops 25165824 | bytes 16777216 | tf_op jit(solution)/shard_map/concatenate | solution.py:134
  50.9 30.1 %shard_map.140 = bf16[2,512,1024]{2,1,0:T(8,128)(2,1)} custom-call(bf16[2,512,1024]{2,1,0:T(8,128)(2,1)} %fusion.22.q_ref, bf16[2,1024,2048]{2,1,0:T(8,128)(2,1)} %pad_maximum_fusion.k_ref.v_ref, bf16[2,1024,2048]{2,1,0:T(8,128)(2,1)} %pad_maximum_fusion.k_ref.v_ref, f32[2,2,256,768]{3,2,1,0:T(8,128)} %broadcast_select_fusion.b_ref), custom_call_target="tpu_custom_call" | custom-call | flops 6442450944 | bytes 15728640 | tf_op jit(solution)/shard_map/pallas_call | solution.py:66
  81.0 0.0 copy-start.8
  81.0 6.3 %convert_reduce_fusion = (f32[2,16,1024]{2,1,0:T(8,128)S(1)}, bf16[2,512,1024]{2,1,0:T(8,128)(2,1)}) fusion(bf16[2,512,1024]{2,1,0:T(8,128)(2,1)} %shard_map.140, bf16[1024,1024]{1,0:T(8,128)(2,1)S(1)} %copy-done, bf16[2,512,1024]{2,1,0:T(8,128)(2,1)} %param.15, pred[2,512]{1,0:T(4,128)(4,1)S(1)} %broadcast_compare_fusion.1), kind=kOutput, calls=%fused_computation.21 | convolution fusion | flops 2153742336 | bytes 8520704 | tf_op jit(solution)/shard_map/sbd,de->sbe/dot_general | solution.py:153
  87.4 14.8 %all_gather.3 = bf16[16,16,1024]{2,1,0:T(8,128)(2,1)S(1)} all-gather(bf16[2,16,1024]{2,1,0:T(8,128)(2,1)S(1)} %multiply_convert_fusion), channel_id=1, replica_groups=mesh['seq'=16,'head'=8] {'head'}, dimensions={0}, use_global_device_ids=true | all-gather | bytes 589824 | tf_op jit(solution)/shard_map/all_gather | solution.py:161
  102.2 0.2 fusion.38
  102.4 0.0 copy-done.7
  102.4 0.8 fusion.34
  103.2 1.0 fusion.44
  104.1 9.9 %all-to-all-start = ((bf16[16,17,1024]{2,1,0:T(8,128)(2,1)}), bf16[16,17,1024]{2,1,0:T(8,128)(2,1)S(1)}, u32[]{:S(2)}, u32[]{:S(2)}) async-start(bf16[16,17,1024]{2,1,0:T(8,128)(2,1)} %fusion.44), calls=%async_computation | async-start | bytes 1572864 | tf_op jit(solution)/shard_map/all_to_all | solution.py:172
  114.0 0.0 reduce-scatter.2.cloned.1.call-start
  114.1 0.6 dynamic_slice.18
  114.7 1.0 dynamic-slice_reduce_fusion
  115.7 0.1 reshape.254
  115.8 0.1 reduce_max.18
  115.9 0.7 multiply_compare_fusion
  116.6 12.3 %all-to-all-done = bf16[16,17,1024]{2,1,0:T(8,128)(2,1)S(1)} async-done(((bf16[16,17,1024]{2,1,0:T(8,128)(2,1)}), bf16[16,17,1024]{2,1,0:T(8,128)(2,1)S(1)}, u32[]{:S(2)}, u32[]{:S(2)}) %all-to-all-start) | async-done | bytes 557088 | tf_op jit(solution)/shard_map/all_to_all | solution.py:172
  128.9 0.8 copy.38
  129.8 0.1 reshape.258
  129.9 4.2 %fusion.1 = (f32[512]{0:T(512)S(1)}, bf16[512,4096]{1,0:T(8,128)(2,1)}) fusion(bf16[28,4096]{1,0:T(8,128)(2,1)} %param.23, s32[512]{0:T(512)S(1)} %reshape.258), kind=kOutput, calls=%fused_computation.3 | convolution fusion | flops 125842944 | bytes 4427776 | tf_op jit(solution)/shard_map/stv,vd->std/dot_general | solution.py:198
  134.1 0.1 copy.48
  134.2 5.9 %fusion.31 = bf16[512,512]{0,1:T(8,128)(2,1)S(1)} fusion(bf16[4096,512]{1,0:T(8,128)(2,1)} %param.24, bf16[512,4096]{1,0:T(8,128)(2,1)} %get-tuple-element.25, f32[512]{0:T(512)S(1)} %add_rsqrt_fusion.3), kind=kOutput, calls=%fused_computation.46 | convolution fusion | flops 2154037248 | bytes 8914944 | tf_op jit(solution)/shard_map/std,de->ste/dot_general | solution.py:201
  140.1 0.0 copy-start.3
  140.1 2.3 %fusion.66 = (f32[4,512]{1,0:T(4,128)S(1)}, f32[4,512,256]{1,2,0:T(8,128)}) fusion(f32[256]{0:T(256)S(1)} %reduce_max.18, pred[256]{0:T(512)(128)(4,1)S(1)} %multiply_compare_fusion, bf16[512,4,128]{0,2,1:T(8,128)(2,1)S(1)} %bitcast.63, bf16[256,4,128]{0,2,1:T(8,128)(2,1)S(1)} %bitcast.62), kind=kOutput, calls=%fused_computation.100 | convolution fusion | flops 136839424 | bytes 2893056 | tf_op jit(solution)/shard_map/sub | solution.py:28
  142.4 2.7 %convolution_convert_fusion.4 = bf16[4,128,512]{2,1,0:T(8,128)(2,1)} fusion(bf16[256,4,128]{0,2,1:T(8,128)(2,1)S(1)} %bitcast.61, f32[4,512,256]{1,2,0:T(8,128)} %get-tuple-element.27, f32[4,512]{1,0:T(4,128)S(1)} %get-tuple-element.26), kind=kOutput, calls=%fused_computation.47 | convolution fusion | flops 135528448 | bytes 2891776 | tf_op jit(solution)/shard_map/shtp,sphd->sthd/dot_general | solution.py:215
  145.1 2.4 %copy.43 = bf16[1,512,512]{2,0,1:T(2,128)(2,1)S(1)} copy(bf16[1,512,512]{1,2,0:T(8,128)(2,1)} %bitcast.59) | data formatting | bytes 1048576 | tf_op jit(solution)/shard_map/reshape | solution.py:218
  147.6 0.6 broadcast.182
  148.1 4.7 %reduce.17 = bf16[512,512]{1,0:T(8,128)(2,1)} reduce(bf16[512,1,512]{2,1,0:T(2,128)(2,1)S(1)} %bitcast.57, bf16[]{:T(256)} %broadcast.182), dimensions={1}, to_apply=%bitcast.45.reduce_sub_computation | reduce | bytes 1048578
  152.8 1.4 reshape.279
  154.2 14.5 %all_to_all.21 = bf16[16,2,8192]{2,1,0:T(2,128)(2,1)} all-to-all(bf16[16,2,8192]{2,1,0:T(2,128)(2,1)S(1)} %reshape.279), channel_id=1, replica_groups=mesh['seq'=16,'head'=8] {'seq'}, dimensions={0} | all-to-all | bytes 1048576 | tf_op jit(solution)/shard_map/all_to_all | solution.py:219
  168.7 2.2 reshape.280
  171.0 0.1 copy.47
  171.1 6.5 %convolution_convert_fusion.1 = bf16[16,32,4096]{2,1,0:T(8,128)(2,1)} fusion(bf16[16,32,512]{2,1,0:T(8,128)(2,1)S(1)} %bitcast.60, bf16[512,4096]{1,0:T(8,128)(2,1)} %param.27), kind=kOutput, calls=%fused_computation.10 | convolution fusion | flops 2149580800 | bytes 8912896 | tf_op jit(solution)/shard_map/ste,ed->std/dot_general | solution.py:220
  177.6 0.0 reduce-scatter.2.cloned.1.call-update
  177.6 35.7 %reduce-scatter.2.cloned.1.call-done = bf16[16,32,512]{2,1,0:T(8,128)(2,1)} async-done(((bf16[16,32,4096]{2,1,0:T(8,128)(2,1)}), bf16[16,32,512]{2,1,0:T(8,128)(2,1)}) %reduce-scatter.2.cloned.1.call-update) | async-done | bytes 524304 | tf_op jit(solution)/shard_map/reduce_scatter | solution.py:223
  213.2 2.2 fusion.37
  (21 shorter events, 0.2 us)
Async XLA Ops:
  7.2 73.8 %copy-start = (bf16[1024,1024]{1,0:T(8,128)(2,1)S(1)}, bf16[1024,1024]{1,0:T(8,128)(2,1)}, u32[]{:S(2)}) copy-start(bf16[1024,1024]{1,0:T(8,128)(2,1)} %param.21) | copy-start | bytes 6291460
  7.2 10.1 %copy-start.1 = (bf16[2,512,1024]{2,1,0:T(8,128)(2,1)S(1)}, bf16[2,512,1024]{2,1,0:T(8,128)(2,1)}, u32[]{:S(2)}) copy-start(bf16[2,512,1024]{2,1,0:T(8,128)(2,1)} %param.15) | copy-start | bytes 6291460
  7.2 10.7 %copy-start.9 = (s32[16]{0:T(128)S(1)}, s32[16]{0:T(128)}, u32[]{:S(2)}) copy-start(s32[16]{0:T(128)} %param.17) | copy-start | bytes 196
  7.2 11.7 %copy-start.4 = (s32[16,32]{1,0:T(8,128)S(1)}, s32[16,32]{1,0:T(8,128)}, u32[]{:S(2)}) copy-start(s32[16,32]{1,0:T(8,128)} %param.22) | copy-start | bytes 6148
  10.4 26.8 %collective-permute-start.1 = (bf16[2,256,1024]{2,1,0:T(8,128)(2,1)}, bf16[2,256,1024]{2,1,0:T(8,128)(2,1)S(1)}, u32[]{:S(2)}, u32[]{:S(2)}) collective-permute-start(bf16[2,256,1024]{2,1,0:T(8,128)(2,1)} %get-tuple-element.17), channel_id=1, source_target_pairs={{8,0},{16,8},{24,16},{32,24},{40,32},{48,40},{56,48},{64,56},{72,6... | collective-permute-start | bytes 3145736 | tf_op jit(solution)/shard_map/ppermute | solution.py:121
  11.7 26.8 %collective-permute-start = (bf16[2,256,1024]{2,1,0:T(8,128)(2,1)}, bf16[2,256,1024]{2,1,0:T(8,128)(2,1)}, u32[]{:S(2)}, u32[]{:S(2)}) collective-permute-start(bf16[2,256,1024]{2,1,0:T(8,128)(2,1)} %get-tuple-element.16), channel_id=1, source_target_pairs={{0,8},{8,16},{16,24},{24,32},{32,40},{40,48},{48,56},{56,64},{64,7... | collective-permute-start | bytes 3145736 | tf_op jit(solution)/shard_map/ppermute | solution.py:120
  18.9 8.2 %copy-start.2 = (bf16[2,512,1024]{2,1,0:T(8,128)(2,1)S(1)}, bf16[2,512,1024]{2,1,0:T(8,128)(2,1)}, u32[]{:S(2)}) copy-start(bf16[2,512,1024]{2,1,0:T(8,128)(2,1)} %param.15) | copy-start | bytes 6291460
  18.9 8.2 %copy-start.5 = (bf16[1024,1024]{1,0:T(8,128)(2,1)S(1)}, bf16[1024,1024]{1,0:T(8,128)(2,1)}, u32[]{:S(2)}) copy-start(bf16[1024,1024]{1,0:T(8,128)(2,1)} %param.20) | copy-start | bytes 6291460
  18.9 8.2 %copy-start.6 = (bf16[1024,1024]{1,0:T(8,128)(2,1)S(1)}, bf16[1024,1024]{1,0:T(8,128)(2,1)}, u32[]{:S(2)}) copy-start(bf16[1024,1024]{1,0:T(8,128)(2,1)} %param.19) | copy-start | bytes 6291460
  81.0 21.4 %copy-start.7 = (bf16[1024,512]{1,0:T(8,128)(2,1)S(1)}, bf16[1024,512]{1,0:T(8,128)(2,1)}, u32[]{:S(2)}) copy-start(bf16[1024,512]{1,0:T(8,128)(2,1)} %param.26) | copy-start | bytes 3145732
  81.0 21.4 %copy-start.8 = (bf16[1024,512]{1,0:T(8,128)(2,1)S(1)}, bf16[1024,512]{1,0:T(8,128)(2,1)}, u32[]{:S(2)}) copy-start(bf16[1024,512]{1,0:T(8,128)(2,1)} %param.25) | copy-start | bytes 3145732
  104.1 24.7 %all-to-all-start = ((bf16[16,17,1024]{2,1,0:T(8,128)(2,1)}), bf16[16,17,1024]{2,1,0:T(8,128)(2,1)S(1)}, u32[]{:S(2)}, u32[]{:S(2)}) async-start(bf16[16,17,1024]{2,1,0:T(8,128)(2,1)} %fusion.44), calls=%async_computation | async-start | bytes 1572864 | tf_op jit(solution)/shard_map/all_to_all | solution.py:172
  114.0 99.2 %reduce-scatter.2.cloned.1.call-start = ((), (), s32[]{:S(2)}) async-start(), calls=%async_computation.3 | async-start | bytes 4718592 | tf_op jit(solution)/shard_map/reduce_scatter | solution.py:223
  140.1 2.3 %copy-start.3 = (bf16[1,256,512]{1,2,0:T(8,128)(2,1)S(1)}, bf16[1,256,512]{1,2,0:T(8,128)(2,1)}, u32[]{:S(2)}) copy-start(bf16[1,256,512]{1,2,0:T(8,128)(2,1)} %copy.38) | copy-start | bytes 786436
Sparse Core Ops, SparseCore 0:
  177.7 35.4 reduce-scatter.1

commit v6 on v5

--- a/solution.py
+++ b/solution.py
@@ -166,15 +166,14 @@
     ).astype(jnp.bfloat16)
     spec_count, part_len, part_width = memory_part.shape
     tok_count = token_ids.shape[1]
-    id_rows = jnp.zeros((spec_count, 1, part_width), jnp.bfloat16)
-    id_rows = id_rows.at[:, 0, :tok_count].set(token_ids.astype(jnp.bfloat16))
-    payload = jnp.concatenate([memory_part, id_rows], axis=1)
+    id_cols = jnp.zeros((spec_count, part_len, 128), jnp.bfloat16)
+    id_cols = id_cols.at[:, 0, :tok_count].set(token_ids.astype(jnp.bfloat16))
+    payload = jnp.concatenate([memory_part, id_cols], axis=2)
     received = lax.all_to_all(payload, "seq", 0, 1, tiled=True)
     seq_count = lax.axis_size("seq")
-    received = received.reshape(seq_count, part_len + 1, part_width)
-    memory = received[:, :part_len].reshape(1, seq_count * part_len, part_width)
-    ids_one = received[:, part_len, :tok_count].reshape(1, seq_count * tok_count)
-    ids_one = ids_one.astype(jnp.int32)
+    memory = received[:, :, :part_width]
+    ids_one = received.reshape(seq_count, part_len, part_width + 128)[:, 0, part_width : part_width + tok_count]
+    ids_one = ids_one.reshape(1, seq_count * tok_count).astype(jnp.int32)
     mem_len = memory.shape[1]
     bias_row = lax.dynamic_slice_in_dim(key_bias, seq_pos, 1, 0)
     pooled_bias = jnp.max(bias_row.reshape(1, mem_len, POOL), axis=2)
@@ -195,11 +194,11 @@
     onehot_one = (
         ids_one[:, :, None] == jnp.arange(vocab, dtype=jnp.int32)[None, None, :]
     ).astype(jnp.bfloat16)
-    hidden_one = jnp.einsum(
-        "stv,vd->std", onehot_one, embedding, preferred_element_type=jnp.float32
+    query_table = jnp.einsum(
+        "vd,de->ve", rms_rows(embedding), dec_query, preferred_element_type=jnp.float32
     ).astype(jnp.bfloat16)
     query_one = jnp.einsum(
-        "std,de->ste", rms_rows(hidden_one), dec_query, preferred_element_type=jnp.float32
+        "stv,ve->ste", onehot_one, query_table, preferred_element_type=jnp.float32
     ).astype(jnp.bfloat16)
     all_tok = query_one.shape[1]
     query_heads = query_one.reshape(1, all_tok, heads_here, dec_head)

time: 223 us -> 216 us (0.969)
  matrix products: 48.1 us -> 41.2 us
  local copies, waits for them, and re-layouts: 13.5 us -> 16.2 us
  waiting for transfers between devices: 54.3 us -> 51.8 us
    dot_general x2 -> x1, matrix products: 10.1 us -> 3.44 us  [per_device(): jnp.einsum('stv,ve->ste', onehot_one, query_table, preferred_element_type...]
    all_to_all x1, waiting for transfers between devices: 12.3 us -> 10 us  [per_device(): received = lax.all_to_all(payload, 'seq', 0, 1, tiled=True)]
    unnamed x25 -> x29, local copies, waits for them, and re-layouts: 4.55 us -> 5.6 us
where the time goes in v6:
time: 216 us; the launch traced here: 215 us
  waiting for transfers between devices  51.8 us (24%)
  matrix products  41.2 us (19%)
  Pallas kernels  30.1 us (14%)
  blocking collectives  29 us (13%)
  starting transfers between devices  16.7 us (8%)
  local copies, waits for them, and re-layouts  16.2 us (8%)
  other arithmetic  15.9 us (7%)
  between operations  14.4 us (7%)
    reduce_scatter x1, waiting for transfers between devices, per_device(): lax.psum_scatter(partial_sums.astype(jnp.bfloat16), 'head', scatter_dimen...  35.6 us
    pallas_call x1, Pallas kernels, band_attention(): pl.pallas_call(band_kernel, out_shape=jax.ShapeDtypeStruct(query_enc.shap...  30.1 us
    all_gather x1, blocking collectives, per_device(): spectra_all = lax.all_gather(pooled, 'head', axis=0, tiled=True)  14.8 us
    all_to_all x1, blocking collectives, per_device(): dec_context = lax.all_to_all(context_one, 'seq', 1, 0, tiled=True)  14.2 us
    all_to_all x1, waiting for transfers between devices, per_device(): received = lax.all_to_all(payload, 'seq', 0, 1, tiled=True)  10 us
    all_to_all x1, starting transfers between devices, per_device(): received = lax.all_to_all(payload, 'seq', 0, 1, tiled=True)  9.89 us
    dot_general x1, matrix products, per_device(): jnp.einsum('ste,ed->std', dec_context, dec_out, preferred_element_type=jn...  6.46 us
    dot_general x1, matrix products, per_device(): jnp.einsum('sbd,de->sbe', context, enc_out, preferred_element_type=jnp.fl...  6.33 us
  transfers between devices with their start and end apart: 4, of which 4 were waited for; matrix products, arithmetic and copies ran while one was open for 8% of the time, Pallas kernels for 0%

profile of v6, /device:TPU:0, one launch (start us, length us, event | category | flops | bytes accessed | tf_op | source)
XLA Modules:
  0.0 215.4 jit_solution(10409456797400920906)
XLA Ops:
  7.2 0.0 copy-start
  7.2 0.0 copy-start.1
  7.2 0.0 copy-start.11
  7.2 0.0 copy-start.6
  7.2 3.2 %fusion.62 = (bf16[2,256,1024]{2,1,0:T(8,128)(2,1)}, bf16[2,256,1024]{2,1,0:T(8,128)(2,1)}) fusion(bf16[2,512,1024]{2,1,0:T(8,128)(2,1)} %param.15), kind=kLoop, calls=%fused_computation.97 | loop fusion | bytes 4194304 | tf_op jit(solution)/shard_map/slice | solution.py:120
  10.4 1.3 collective-permute-start.1
  11.7 5.5 %collective-permute-start = (bf16[2,256,1024]{2,1,0:T(8,128)(2,1)}, bf16[2,256,1024]{2,1,0:T(8,128)(2,1)}, u32[]{:S(2)}, u32[]{:S(2)}) collective-permute-start(bf16[2,256,1024]{2,1,0:T(8,128)(2,1)} %get-tuple-element.16), channel_id=1, source_target_pairs={{0,8},{8,16},{16,24},{24,32},{32,40},{40,48},{48,56},{56,64},{64,7... | collective-permute-start | bytes 3145736 | tf_op jit(solution)/shard_map/ppermute | solution.py:120
  17.3 0.0 copy-done.1
  17.3 0.5 fusion.3
  17.8 0.1 fusion.38
  17.9 0.0 copy-done.11
  17.9 0.1 dynamic_slice.15
  18.0 0.8 and_select_fusion
  18.9 0.0 copy-done.6
  18.9 0.0 copy-start.7
  18.9 0.0 copy-start.8
  18.9 6.1 %fusion.17.q_ref = bf16[2,512,1024]{2,1,0:T(8,128)(2,1)} fusion(bf16[1024,1024]{1,0:T(8,128)(2,1)} %param.18, bf16[2,512,1024]{2,1,0:T(8,128)(2,1)} %param.15, f32[2,512]{1,0:T(2,128)S(1)} %add_rsqrt_fusion.2), kind=kOutput, calls=%fused_computation.32 | convolution fusion | flops 2151677952 | bytes 6295552 | tf_op jit(solution)/shard_map/sbd,de->sbe/dot_general | solution.py:124
  25.0 2.0 broadcast_select_fusion.b_ref
  27.0 0.1 broadcast_compare_fusion.1
  27.1 0.0 copy-done.7
  27.1 0.0 copy-done.8
  27.1 0.3 copy-done.2
  27.4 4.9 %convolution_convert_fusion.1 = bf16[2,512,2048]{2,1,0:T(8,128)(2,1)S(1)} fusion(bf16[1024,1024]{1,0:T(8,128)(2,1)S(1)} %copy-done.7, bf16[1024,1024]{1,0:T(8,128)(2,1)S(1)} %copy-done.8, bf16[2,512,1024]{2,1,0:T(8,128)(2,1)S(1)} %copy-done.2, f32[2,512]{1,0:T(2,128)S(1)} %add_rsqrt_fusion.2), kind=kOutput, calls=%fused_computation.17 | convolution fusion | flops 4308598784 | bytes 10489856 | tf_op jit(solution)/shard_map/sbd,de->sbe/dot_general | solution.py:127
  32.3 5.0 %collective-permute-done.1 = bf16[2,256,1024]{2,1,0:T(8,128)(2,1)S(1)} collective-permute-done((bf16[2,256,1024]{2,1,0:T(8,128)(2,1)}, bf16[2,256,1024]{2,1,0:T(8,128)(2,1)S(1)}, u32[]{:S(2)}, u32[]{:S(2)}) %collective-permute-start.1) | collective-permute-done | bytes 1048608 | tf_op jit(solution)/shard_map/ppermute | solution.py:121
  37.3 1.3 collective-permute-done
  38.6 1.7 fusion.1
  40.3 6.1 %convolution_convert_fusion.2 = bf16[2,512,2048]{2,1,0:T(8,128)(2,1)S(1)} fusion(bf16[1024,1024]{1,0:T(8,128)(2,1)S(1)} %copy-done.7, bf16[1024,1024]{1,0:T(8,128)(2,1)S(1)} %copy-done.8, f32[2,512]{1,0:T(2,128)S(1)} %add_rsqrt_fusion.1, bf16[2,256,1024]{2,1,0:T(8,128)(2,1)S(1)} %collective-permute-done.1, bf16[2,256,1024]{2,1,0:T(8,128)(2,1)} %collective-permute-done), kind=kOutput, calls=%fused_computation.18 | convolution fusion | flops 4311744512 | bytes 10489856 | tf_op jit(solution)/shard_map/sbd,de->sbe/dot_general | solution.py:131
  46.4 0.5 fusion.61
  46.9 4.0 %pad_maximum_fusion.k_ref.v_ref = bf16[2,1024,2048]{2,1,0:T(8,128)(2,1)} fusion(bf16[2,256,2048]{2,1,0:T(8,128)(2,1)S(1)} %get-tuple-element.15, bf16[2,512,2048]{2,1,0:T(8,128)(2,1)S(1)} %convolution_convert_fusion.1, bf16[2,256,2048]{2,1,0:T(8,128)(2,1)S(1)} %get-tuple-element.14), kind=kLoop, calls=%fused_computation.1 | loop fusion | flops 25165824 | bytes 16777216 | tf_op jit(solution)/shard_map/concatenate | solution.py:134
  50.9 30.1 %shard_map.140 = bf16[2,512,1024]{2,1,0:T(8,128)(2,1)} custom-call(bf16[2,512,1024]{2,1,0:T(8,128)(2,1)} %fusion.17.q_ref, bf16[2,1024,2048]{2,1,0:T(8,128)(2,1)} %pad_maximum_fusion.k_ref.v_ref, bf16[2,1024,2048]{2,1,0:T(8,128)(2,1)} %pad_maximum_fusion.k_ref.v_ref, f32[2,2,256,768]{3,2,1,0:T(8,128)} %broadcast_select_fusion.b_ref), custom_call_target="tpu_custom_call" | custom-call | flops 6442450944 | bytes 15728640 | tf_op jit(solution)/shard_map/pallas_call | solution.py:66
  81.0 0.0 copy-start.10
  81.0 6.3 %convert_reduce_fusion = (f32[2,16,1024]{2,1,0:T(8,128)S(1)}, bf16[2,512,1024]{2,1,0:T(8,128)(2,1)}) fusion(bf16[2,512,1024]{2,1,0:T(8,128)(2,1)} %shard_map.140, bf16[1024,1024]{1,0:T(8,128)(2,1)S(1)} %copy-done, bf16[2,512,1024]{2,1,0:T(8,128)(2,1)} %param.15, pred[2,512]{1,0:T(4,128)(4,1)S(1)} %broadcast_compare_fusion.1), kind=kOutput, calls=%fused_computation.15 | convolution fusion | flops 2153742336 | bytes 8520704 | tf_op jit(solution)/shard_map/sbd,de->sbe/dot_general | solution.py:153
  87.4 14.8 %all_gather.3 = bf16[16,16,1024]{2,1,0:T(8,128)(2,1)S(1)} all-gather(bf16[2,16,1024]{2,1,0:T(8,128)(2,1)S(1)} %multiply_convert_fusion), channel_id=1, replica_groups=mesh['seq'=16,'head'=8] {'head'}, dimensions={0}, use_global_device_ids=true | all-gather | bytes 589824 | tf_op jit(solution)/shard_map/all_gather | solution.py:161
  102.2 0.2 fusion.30
  102.4 0.0 copy-start.3
  102.4 0.8 fusion.25
  103.2 0.9 fusion.39
  104.0 9.9 %all-to-all-start = ((bf16[16,16,1152]{2,1,0:T(8,128)(2,1)}), bf16[16,16,1152]{2,1,0:T(8,128)(2,1)S(1)}, u32[]{:S(2)}, u32[]{:S(2)}) async-start(bf16[16,16,1152]{2,1,0:T(8,128)(2,1)} %fusion.39), calls=%async_computation | async-start | bytes 1179648 | tf_op jit(solution)/shard_map/all_to_all | solution.py:172
  113.9 0.0 reduce-scatter.2.cloned.1.call-start
  114.0 0.6 dynamic_slice.18
  114.6 1.0 dynamic-slice_reduce_fusion
  115.6 0.1 reshape.237
  115.7 0.1 reduce_max.18
  115.8 0.7 multiply_compare_fusion
  116.5 0.2 fusion.40
  116.7 10.0 %all-to-all-done = bf16[16,16,1152]{2,1,0:T(8,128)(2,1)S(1)} async-done(((bf16[16,16,1152]{2,1,0:T(8,128)(2,1)}), bf16[16,16,1152]{2,1,0:T(8,128)(2,1)S(1)}, u32[]{:S(2)}, u32[]{:S(2)}) %all-to-all-start) | async-done | bytes 589856 | tf_op jit(solution)/shard_map/all_to_all | solution.py:172
  126.7 0.7 fusion.63
  127.4 1.8 copy.38
  129.3 0.1 reshape.241
  129.3 0.8 copy.48
  130.2 3.4 %convolution_convert_fusion.4 = bf16[512,512]{0,1:T(8,128)(2,1)S(1)} fusion(bf16[4096,512]{1,0:T(8,128)(2,1)} %param.24, bf16[28,4096]{1,0:T(8,128)(2,1)S(1)} %copy-done.3, f32[28]{0:T(128)S(1)} %add_rsqrt_fusion.3, s32[512]{0:T(512)S(1)} %reshape.241), kind=kOutput, calls=%fused_computation.39 | convolution fusion | flops 132755456 | bytes 4950128 | tf_op jit(solution)/shard_map/stv,ve->ste/dot_general | solution.py:200
  133.6 2.3 %fusion.64 = (f32[4,512]{1,0:T(4,128)S(1)}, f32[4,512,256]{1,2,0:T(8,128)}) fusion(f32[256]{0:T(256)S(1)} %reduce_max.18, pred[256]{0:T(512)(128)(4,1)S(1)} %multiply_compare_fusion, bf16[512,4,128]{0,2,1:T(8,128)(2,1)S(1)} %bitcast.58, bf16[256,4,128]{0,2,1:T(8,128)(2,1)S(1)} %bitcast.62), kind=kOutput, calls=%fused_computation.99 | convolution fusion | flops 136839424 | bytes 2893056 | tf_op jit(solution)/shard_map/sub | solution.py:28
  135.9 2.7 %convolution_convert_fusion.3 = bf16[4,128,512]{2,1,0:T(8,128)(2,1)} fusion(bf16[256,4,128]{0,2,1:T(8,128)(2,1)S(1)} %bitcast.61, f32[4,512,256]{1,2,0:T(8,128)} %get-tuple-element.25, f32[4,512]{1,0:T(4,128)S(1)} %get-tuple-element.24), kind=kOutput, calls=%fused_computation.37 | convolution fusion | flops 135528448 | bytes 2891776 | tf_op jit(solution)/shard_map/shtp,sphd->sthd/dot_general | solution.py:214
  138.6 2.4 %copy.43 = bf16[1,512,512]{2,0,1:T(2,128)(2,1)S(1)} copy(bf16[1,512,512]{1,2,0:T(8,128)(2,1)} %bitcast.59) | data formatting | bytes 1048576 | tf_op jit(solution)/shard_map/reshape | solution.py:217
  141.1 0.6 broadcast.190
  141.6 4.7 %reduce.15 = bf16[512,512]{1,0:T(8,128)(2,1)} reduce(bf16[512,1,512]{2,1,0:T(2,128)(2,1)S(1)} %bitcast.56, bf16[]{:T(256)} %broadcast.190), dimensions={1}, to_apply=%bitcast.45.reduce_sub_computation | reduce | bytes 1048578
  146.3 1.4 reshape.262
  147.7 14.2 %all_to_all.24 = bf16[16,2,8192]{2,1,0:T(2,128)(2,1)} all-to-all(bf16[16,2,8192]{2,1,0:T(2,128)(2,1)S(1)} %reshape.262), channel_id=1, replica_groups=mesh['seq'=16,'head'=8] {'seq'}, dimensions={0} | all-to-all | bytes 1048576 | tf_op jit(solution)/shard_map/all_to_all | solution.py:218
  161.9 2.2 %reshape.263 = bf16[512,1,512]{2,1,0:T(2,128)(2,1)S(1)} reshape(bf16[16,2,8192]{2,1,0:T(2,128)(2,1)} %all_to_all.24) | data formatting | bytes 1048576
  164.1 0.1 copy.47
  164.3 6.5 %convolution_convert_fusion = bf16[16,32,4096]{2,1,0:T(8,128)(2,1)} fusion(bf16[16,32,512]{2,1,0:T(8,128)(2,1)S(1)} %bitcast.60, bf16[512,4096]{1,0:T(8,128)(2,1)} %param.27), kind=kOutput, calls=%fused_computation.5 | convolution fusion | flops 2149580800 | bytes 8912896 | tf_op jit(solution)/shard_map/ste,ed->std/dot_general | solution.py:219
  170.7 0.0 reduce-scatter.2.cloned.1.call-update
  170.8 35.6 %reduce-scatter.2.cloned.1.call-done = bf16[16,32,512]{2,1,0:T(8,128)(2,1)} async-done(((bf16[16,32,4096]{2,1,0:T(8,128)(2,1)}), bf16[16,32,512]{2,1,0:T(8,128)(2,1)}) %reduce-scatter.2.cloned.1.call-update) | async-done | bytes 524304 | tf_op jit(solution)/shard_map/reduce_scatter | solution.py:222
  206.3 2.2 %fusion.28 = bf16[16,32,512]{2,1,0:T(8,128)(2,1)} fusion(bf16[16,32,512]{2,1,0:T(8,128)(2,1)} %reduce-scatter.2.cloned.1.call-done, s32[16,32]{1,0:T(8,128)S(1)} %copy-done.6, bf16[28,4096]{1,0:T(8,128)(2,1)S(1)} %copy-done.3, s32[]{:T(128)S(6)} %select_n.36), kind=kOutput, calls=%fused_computation.43 | convolution fusion | flops 16005120 | bytes 1089540 | tf_op jit(solution)/shard_map/stv,vd->std/dot_general | solution.py:191
  (24 shorter events, 0.1 us)
Async XLA Ops:
  7.2 73.8 %copy-start = (bf16[1024,1024]{1,0:T(8,128)(2,1)S(1)}, bf16[1024,1024]{1,0:T(8,128)(2,1)}, u32[]{:S(2)}) copy-start(bf16[1024,1024]{1,0:T(8,128)(2,1)} %param.21) | copy-start | bytes 6291460
  7.2 10.1 %copy-start.1 = (bf16[2,512,1024]{2,1,0:T(8,128)(2,1)S(1)}, bf16[2,512,1024]{2,1,0:T(8,128)(2,1)}, u32[]{:S(2)}) copy-start(bf16[2,512,1024]{2,1,0:T(8,128)(2,1)} %param.15) | copy-start | bytes 6291460
  7.2 10.7 %copy-start.11 = (s32[16]{0:T(128)S(1)}, s32[16]{0:T(128)}, u32[]{:S(2)}) copy-start(s32[16]{0:T(128)} %param.17) | copy-start | bytes 196
  7.2 11.7 %copy-start.6 = (s32[16,32]{1,0:T(8,128)S(1)}, s32[16,32]{1,0:T(8,128)}, u32[]{:S(2)}) copy-start(s32[16,32]{1,0:T(8,128)} %param.22) | copy-start | bytes 6148
  10.4 26.8 %collective-permute-start.1 = (bf16[2,256,1024]{2,1,0:T(8,128)(2,1)}, bf16[2,256,1024]{2,1,0:T(8,128)(2,1)S(1)}, u32[]{:S(2)}, u32[]{:S(2)}) collective-permute-start(bf16[2,256,1024]{2,1,0:T(8,128)(2,1)} %get-tuple-element.17), channel_id=1, source_target_pairs={{8,0},{16,8},{24,16},{32,24},{40,32},{48,40},{56,48},{64,56},{72,6... | collective-permute-start | bytes 3145736 | tf_op jit(solution)/shard_map/ppermute | solution.py:121
  11.7 26.8 %collective-permute-start = (bf16[2,256,1024]{2,1,0:T(8,128)(2,1)}, bf16[2,256,1024]{2,1,0:T(8,128)(2,1)}, u32[]{:S(2)}, u32[]{:S(2)}) collective-permute-start(bf16[2,256,1024]{2,1,0:T(8,128)(2,1)} %get-tuple-element.16), channel_id=1, source_target_pairs={{0,8},{8,16},{16,24},{24,32},{32,40},{40,48},{48,56},{56,64},{64,7... | collective-permute-start | bytes 3145736 | tf_op jit(solution)/shard_map/ppermute | solution.py:120
  18.9 8.2 %copy-start.7 = (bf16[1024,1024]{1,0:T(8,128)(2,1)S(1)}, bf16[1024,1024]{1,0:T(8,128)(2,1)}, u32[]{:S(2)}) copy-start(bf16[1024,1024]{1,0:T(8,128)(2,1)} %param.20) | copy-start | bytes 6291460
  18.9 8.2 %copy-start.8 = (bf16[1024,1024]{1,0:T(8,128)(2,1)S(1)}, bf16[1024,1024]{1,0:T(8,128)(2,1)}, u32[]{:S(2)}) copy-start(bf16[1024,1024]{1,0:T(8,128)(2,1)} %param.19) | copy-start | bytes 6291460
  25.0 2.4 %copy-start.2 = (bf16[2,512,1024]{2,1,0:T(8,128)(2,1)S(1)}, bf16[2,512,1024]{2,1,0:T(8,128)(2,1)}, u32[]{:S(2)}) copy-start(bf16[2,512,1024]{2,1,0:T(8,128)(2,1)} %param.15) | copy-start | bytes 6291460
  81.0 21.4 %copy-start.9 = (bf16[1024,512]{1,0:T(8,128)(2,1)S(1)}, bf16[1024,512]{1,0:T(8,128)(2,1)}, u32[]{:S(2)}) copy-start(bf16[1024,512]{1,0:T(8,128)(2,1)} %param.26) | copy-start | bytes 3145732
  81.0 21.4 %copy-start.10 = (bf16[1024,512]{1,0:T(8,128)(2,1)S(1)}, bf16[1024,512]{1,0:T(8,128)(2,1)}, u32[]{:S(2)}) copy-start(bf16[1024,512]{1,0:T(8,128)(2,1)} %param.25) | copy-start | bytes 3145732
  102.4 14.1 %copy-start.3 = (bf16[28,4096]{1,0:T(8,128)(2,1)S(1)}, bf16[28,4096]{1,0:T(8,128)(2,1)}, u32[]{:S(2)}) copy-start(bf16[28,4096]{1,0:T(8,128)(2,1)} %param.23) | copy-start | bytes 688132
  104.0 22.6 %all-to-all-start = ((bf16[16,16,1152]{2,1,0:T(8,128)(2,1)}), bf16[16,16,1152]{2,1,0:T(8,128)(2,1)S(1)}, u32[]{:S(2)}, u32[]{:S(2)}) async-start(bf16[16,16,1152]{2,1,0:T(8,128)(2,1)} %fusion.39), calls=%async_computation | async-start | bytes 1179648 | tf_op jit(solution)/shard_map/all_to_all | solution.py:172
  113.9 92.4 %reduce-scatter.2.cloned.1.call-start = ((), (), s32[]{:S(2)}) async-start(), calls=%async_computation.3 | async-start | bytes 4718592 | tf_op jit(solution)/shard_map/reduce_scatter | solution.py:222
  130.2 3.5 %copy-start.5 = (bf16[1,256,512]{1,2,0:T(8,128)(2,1)S(1)}, bf16[1,256,512]{1,2,0:T(8,128)(2,1)}, u32[]{:S(2)}) copy-start(bf16[1,256,512]{1,2,0:T(8,128)(2,1)} %copy.48) | copy-start | bytes 786436
  133.6 2.3 %copy-start.4 = (bf16[1,256,512]{1,2,0:T(8,128)(2,1)S(1)}, bf16[1,256,512]{1,2,0:T(8,128)(2,1)}, u32[]{:S(2)}) copy-start(bf16[1,256,512]{1,2,0:T(8,128)(2,1)} %copy.38) | copy-start | bytes 786436
Sparse Core Ops, SparseCore 0:
  170.9 35.4 reduce-scatter.1

commit v7 on v6

--- a/solution.py
+++ b/solution.py
@@ -11,6 +11,7 @@
 HD = 32
 QBLOCK = 256
 HGROUP = 512
+DEC_SCALE = 128 ** (-0.5)
 
 
 epsilon = 1e-05
@@ -86,6 +87,40 @@
     )(query_enc, keyval, keyval, full_bias)
 
 
+def cross_kernel(q_ref, k_ref, v_ref, b_ref, o_ref):
+    s = lax.dot_general(
+        q_ref[0], k_ref[0], (((1,), (1,)), ((), ())), preferred_element_type=jnp.float32
+    )
+    s = s * DEC_SCALE + b_ref[0]
+    m = jnp.max(s, axis=1, keepdims=True)
+    p = jnp.exp(s - m)
+    total = jnp.sum(p, axis=1, keepdims=True)
+    pv = jnp.dot(p.astype(jnp.bfloat16), v_ref[0], preferred_element_type=jnp.float32)
+    o_ref[0] = (pv / total).astype(o_ref.dtype)
+
+
+def cross_attention(query_one, received, mem_bias, heads_here, dec_head):
+    _, all_tok, width = query_one.shape
+    mem_len = received.shape[1]
+    return pl.pallas_call(
+        cross_kernel,
+        out_shape=jax.ShapeDtypeStruct(query_one.shape, jnp.bfloat16),
+        grid=(heads_here,),
+        in_specs=[
+            pl.BlockSpec((1, all_tok, dec_head), lambda h: (0, 0, h)),
+            pl.BlockSpec((1, mem_len, dec_head), lambda h: (0, 0, h)),
+            pl.BlockSpec((1, mem_len, dec_head), lambda h: (0, 0, heads_here + h)),
+            pl.BlockSpec((1, 1, mem_len), lambda h: (0, 0, 0)),
+        ],
+        out_specs=pl.BlockSpec((1, all_tok, dec_head), lambda h: (0, 0, h)),
+        cost_estimate=pl.CostEstimate(
+            flops=all_tok * mem_len * width * 4,
+            transcendentals=all_tok * mem_len * heads_here,
+            bytes_accessed=all_tok * width * 4 + mem_len * width * 4,
+        ),
+    )(query_one, received, received, mem_bias)
+
+
 def per_device(
     spectra,
     key_bias,
@@ -200,21 +235,8 @@
     query_one = jnp.einsum(
         "stv,ve->ste", onehot_one, query_table, preferred_element_type=jnp.float32
     ).astype(jnp.bfloat16)
-    all_tok = query_one.shape[1]
-    query_heads = query_one.reshape(1, all_tok, heads_here, dec_head)
-    key_heads = memory[:, :, :local_width].reshape(1, mem_len, heads_here, dec_head)
-    value_heads = memory[:, :, local_width:].reshape(1, mem_len, heads_here, dec_head)
-    scores = (
-        jnp.einsum("sthd,sphd->shtp", query_heads, key_heads, preferred_element_type=jnp.float32)
-        * dec_head ** (-0.5)
-        + pooled_bias[:, None, None, :]
-    )
-    scores = jnp.where(mem_valid[:, None, None, :], scores, masked_score)
-    weights = softmax_rows(scores)
-    context_one = jnp.einsum(
-        "shtp,sphd->sthd", weights, value_heads, preferred_element_type=jnp.float32
-    ).astype(jnp.bfloat16)
-    context_one = context_one.reshape(1, all_tok, local_width)
+    mem_bias = jnp.where(mem_valid, pooled_bias, masked_score)[:, None, :]
+    context_one = cross_attention(query_one, received, mem_bias, heads_here, dec_head)
     dec_context = lax.all_to_all(context_one, "seq", 1, 0, tiled=True)
     partial_sums = jnp.einsum(
         "ste,ed->std", dec_context, dec_out, preferred_element_type=jnp.float32

time: 216 us -> 212 us (0.981)
  local copies, waits for them, and re-layouts: 16.2 us -> 11.9 us
  Pallas kernels: 30.1 us -> 34.4 us
  waiting for transfers between devices: 51.8 us -> 49.1 us
    pallas_call x0 -> x1, Pallas kernels: none -> 4.24 us  [cross_attention(): pl.pallas_call(cross_kernel, out_shape=jax.ShapeDtypeStruct(query_one.sha...]
    ppermute x1, waiting for transfers between devices: 4.97 us -> 0.95 us  [per_device(): high_edge = lax.ppermute(spectra[:, :half_span], 'seq', backward)]
    dot_general x1 -> x0, matrix products: 2.7 us -> none  [per_device(): jnp.einsum('shtp,sphd->sthd', weights, value_heads, preferred_element_typ...]
    dot_general x1, matrix products: 4.86 us -> 7.55 us  [per_device(): jnp.einsum('sbd,de->sbe', normed, kv_weights, preferred_element_type=jnp....]
    slice x2 -> x0, local copies, waits for them, and re-layouts: 2.55 us -> none  [the longest x1 1.81 us: per_device(): memory[:, :, local_width:].reshape(1, mem_len, heads_here, dec_head)]
    reshape x1 -> x0, local copies, waits for them, and re-layouts: 2.41 us -> none  [per_device(): context_one = context_one.reshape(1, all_tok, local_width)]
    sub x1 -> x0, matrix products: 2.29 us -> none  [softmax_rows(): weights = jnp.exp(scores - row_top)]
    unnamed x29 -> x24, local copies, waits for them, and re-layouts: 5.6 us -> 4.41 us
  transfers between devices with their start and end apart: 4 -> 4, of which waited for: 4 -> 4; matrix products, arithmetic and copies ran while one was open for 8% -> 10% of each run, Pallas kernels for 0% -> 0%
where the time goes in v7:
time: 212 us; the launch traced here: 211 us
  waiting for transfers between devices  49.1 us (23%)
  matrix products  39.8 us (19%)
  Pallas kernels  34.4 us (16%)
  blocking collectives  28.7 us (14%)
  starting transfers between devices  16.7 us (8%)
  other arithmetic  16.5 us (8%)
  between operations  14.3 us (7%)
  local copies, waits for them, and re-layouts  11.9 us (6%)
    reduce_scatter x1, waiting for transfers between devices, per_device(): lax.psum_scatter(partial_sums.astype(jnp.bfloat16), 'head', scatter_dimen...  35.6 us
    pallas_call x1, Pallas kernels, band_attention(): pl.pallas_call(band_kernel, out_shape=jax.ShapeDtypeStruct(query_enc.shap...  30.1 us
    all_gather x1, blocking collectives, per_device(): spectra_all = lax.all_gather(pooled, 'head', axis=0, tiled=True)  14.6 us
    all_to_all x1, blocking collectives, per_device(): dec_context = lax.all_to_all(context_one, 'seq', 1, 0, tiled=True)  14.2 us
    all_to_all x1, waiting for transfers between devices, per_device(): received = lax.all_to_all(payload, 'seq', 0, 1, tiled=True)  11.3 us
    all_to_all x1, starting transfers between devices, per_device(): received = lax.all_to_all(payload, 'seq', 0, 1, tiled=True)  9.86 us
    dot_general x1, matrix products, per_device(): jnp.einsum('sbd,de->sbe', normed, kv_weights, preferred_element_type=jnp....  7.55 us
    dot_general x1, matrix products, per_device(): jnp.einsum('ste,ed->std', dec_context, dec_out, preferred_element_type=jn...  6.47 us
  transfers between devices with their start and end apart: 4, of which 4 were waited for; matrix products, arithmetic and copies ran while one was open for 10% of the time, Pallas kernels for 0%

profile of v7, /device:TPU:0, one launch (start us, length us, event | category | flops | bytes accessed | tf_op | source)
XLA Modules:
  0.0 211.4 jit_solution(2561953183694703576)
XLA Ops:
  7.2 0.0 copy-start
  7.2 0.0 copy-start.1
  7.2 0.0 copy-start.9
  7.2 0.0 copy-start.4
  7.2 3.2 %fusion.53 = (bf16[2,256,1024]{2,1,0:T(8,128)(2,1)}, bf16[2,256,1024]{2,1,0:T(8,128)(2,1)}) fusion(bf16[2,512,1024]{2,1,0:T(8,128)(2,1)} %param.15), kind=kLoop, calls=%fused_computation.85 | loop fusion | bytes 4194304 | tf_op jit(solution)/shard_map/slice | solution.py:155
  10.4 1.3 collective-permute-start.1
  11.7 5.5 %collective-permute-start = (bf16[2,256,1024]{2,1,0:T(8,128)(2,1)}, bf16[2,256,1024]{2,1,0:T(8,128)(2,1)}, u32[]{:S(2)}, u32[]{:S(2)}) collective-permute-start(bf16[2,256,1024]{2,1,0:T(8,128)(2,1)} %get-tuple-element.16), channel_id=1, source_target_pairs={{0,8},{8,16},{16,24},{24,32},{32,40},{40,48},{48,56},{56,64},{64,7... | collective-permute-start | bytes 3145736 | tf_op jit(solution)/shard_map/ppermute | solution.py:155
  17.3 0.0 copy-done.1
  17.3 0.5 fusion.2
  17.8 0.1 fusion.33
  17.9 0.0 copy-done.9
  17.9 0.1 dynamic_slice.15
  18.0 0.6 dynamic_slice.18
  18.6 1.0 dynamic-slice_reduce_fusion
  19.6 0.8 and_select_fusion
  20.5 0.0 copy-done.4
  20.5 0.1 reshape.203
  20.6 5.9 %fusion.16.q_ref = bf16[2,512,1024]{2,1,0:T(8,128)(2,1)} fusion(bf16[1024,1024]{1,0:T(8,128)(2,1)} %param.18, bf16[2,512,1024]{2,1,0:T(8,128)(2,1)} %param.15, f32[2,512]{1,0:T(2,128)S(1)} %add_rsqrt_fusion.2), kind=kOutput, calls=%fused_computation.28 | convolution fusion | flops 2151677952 | bytes 6295552 | tf_op jit(solution)/shard_map/sbd,de->sbe/dot_general | solution.py:159
  26.5 2.0 broadcast_select_fusion.b_ref
  28.6 0.1 reduce_max.11
  28.7 0.1 broadcast_compare_fusion.1
  28.8 0.0 copy-start.5
  28.8 0.0 copy-start.6
  28.8 7.5 %convolution_convert_fusion.1 = bf16[2,512,2048]{2,1,0:T(8,128)(2,1)S(1)} fusion(bf16[1024,1024]{1,0:T(8,128)(2,1)} %param.20, bf16[1024,1024]{1,0:T(8,128)(2,1)} %param.19, bf16[2,512,1024]{2,1,0:T(8,128)(2,1)} %param.15, f32[2,512]{1,0:T(2,128)S(1)} %add_rsqrt_fusion.2), kind=kOutput, calls=%fused_computation.16 | convolution fusion | flops 4308598784 | bytes 10489856 | tf_op jit(solution)/shard_map/sbd,de->sbe/dot_general | solution.py:162
  36.3 1.0 collective-permute-done.1
  37.3 1.3 collective-permute-done
  38.6 1.7 fusion
  40.3 0.0 copy-done.5
  40.3 0.0 copy-done.6
  40.3 6.3 %convolution_convert_fusion.2 = bf16[2,512,2048]{2,1,0:T(8,128)(2,1)S(1)} fusion(bf16[1024,1024]{1,0:T(8,128)(2,1)S(1)} %copy-done.5, bf16[1024,1024]{1,0:T(8,128)(2,1)S(1)} %copy-done.6, f32[2,512]{1,0:T(2,128)S(1)} %add_rsqrt_fusion.1, bf16[2,256,1024]{2,1,0:T(8,128)(2,1)S(1)} %collective-permute-done.1, bf16[2,256,1024]{2,1,0:T(8,128)(2,1)} %collective-permute-done), kind=kOutput, calls=%fused_computation.17 | convolution fusion | flops 4311744512 | bytes 10489856 | tf_op jit(solution)/shard_map/sbd,de->sbe/dot_general | solution.py:166
  46.6 0.5 fusion.52
  47.1 4.0 %pad_maximum_fusion.k_ref.v_ref = bf16[2,1024,2048]{2,1,0:T(8,128)(2,1)} fusion(bf16[2,256,2048]{2,1,0:T(8,128)(2,1)S(1)} %get-tuple-element.15, bf16[2,512,2048]{2,1,0:T(8,128)(2,1)S(1)} %convolution_convert_fusion.1, bf16[2,256,2048]{2,1,0:T(8,128)(2,1)S(1)} %get-tuple-element.14), kind=kLoop, calls=%fused_computation | loop fusion | flops 25165824 | bytes 16777216 | tf_op jit(solution)/shard_map/concatenate | solution.py:169
  51.1 30.1 %shard_map.140 = bf16[2,512,1024]{2,1,0:T(8,128)(2,1)} custom-call(bf16[2,512,1024]{2,1,0:T(8,128)(2,1)} %fusion.16.q_ref, bf16[2,1024,2048]{2,1,0:T(8,128)(2,1)} %pad_maximum_fusion.k_ref.v_ref, bf16[2,1024,2048]{2,1,0:T(8,128)(2,1)} %pad_maximum_fusion.k_ref.v_ref, f32[2,2,256,768]{3,2,1,0:T(8,128)} %broadcast_select_fusion.b_ref), custom_call_target="tpu_custom_call" | custom-call | flops 6442450944 | bytes 15728640 | tf_op jit(solution)/shard_map/pallas_call | solution.py:67
  81.2 0.0 copy-done
  81.2 0.0 copy-start.7
  81.2 0.0 copy-start.8
  81.3 6.3 %convert_reduce_fusion = (f32[2,16,1024]{2,1,0:T(8,128)S(1)}, bf16[2,512,1024]{2,1,0:T(8,128)(2,1)}) fusion(bf16[2,512,1024]{2,1,0:T(8,128)(2,1)} %shard_map.140, bf16[1024,1024]{1,0:T(8,128)(2,1)S(1)} %copy-done, bf16[2,512,1024]{2,1,0:T(8,128)(2,1)} %param.15, pred[2,512]{1,0:T(4,128)(4,1)S(1)} %broadcast_compare_fusion.1), kind=kOutput, calls=%fused_computation.14 | convolution fusion | flops 2153742336 | bytes 8520704 | tf_op jit(solution)/shard_map/sbd,de->sbe/dot_general | solution.py:188
  87.6 14.6 %all_gather.3 = bf16[16,16,1024]{2,1,0:T(8,128)(2,1)S(1)} all-gather(bf16[2,16,1024]{2,1,0:T(8,128)(2,1)S(1)} %multiply_convert_fusion), channel_id=1, replica_groups=mesh['seq'=16,'head'=8] {'head'}, dimensions={0}, use_global_device_ids=true | all-gather | bytes 589824 | tf_op jit(solution)/shard_map/all_gather | solution.py:196
  102.2 0.2 fusion.29
  102.3 0.0 copy-done.7
  102.4 0.0 copy-done.8
  102.4 0.8 fusion.23
  103.1 0.9 fusion.34
  104.0 9.9 %all-to-all-start = ((bf16[16,16,1152]{2,1,0:T(8,128)(2,1)}), bf16[16,16,1152]{2,1,0:T(8,128)(2,1)S(1)}, u32[]{:S(2)}, u32[]{:S(2)}) async-start(bf16[16,16,1152]{2,1,0:T(8,128)(2,1)} %fusion.34), calls=%async_computation | async-start | bytes 1179648 | tf_op jit(solution)/shard_map/all_to_all | solution.py:207
  113.9 0.0 reduce-scatter.2.cloned.1.call-start
  113.9 0.0 copy-done.3
  113.9 0.2 fusion.35
  114.1 1.2 compare_select_fusion.b_ref
  115.3 11.3 %all-to-all-done = bf16[16,16,1152]{2,1,0:T(8,128)(2,1)S(1)} async-done(((bf16[16,16,1152]{2,1,0:T(8,128)(2,1)}), bf16[16,16,1152]{2,1,0:T(8,128)(2,1)S(1)}, u32[]{:S(2)}, u32[]{:S(2)}) %all-to-all-start) | async-done | bytes 589856 | tf_op jit(solution)/shard_map/all_to_all | solution.py:207
  126.7 0.1 reshape.206
  126.7 4.2 %fusion.27.q_ref = bf16[1,512,512]{2,1,0:T(8,128)(2,1)} fusion(bf16[4096,512]{1,0:T(8,128)(2,1)} %param.24, bf16[28,4096]{1,0:T(8,128)(2,1)S(1)} %copy-done.3, f32[28]{0:T(128)S(1)} %add_rsqrt_fusion.3, s32[512]{0:T(512)S(1)} %reshape.206), kind=kOutput, calls=%fused_computation.38 | convolution fusion | flops 132755456 | bytes 4950128 | tf_op jit(solution)/shard_map/stv,ve->ste/dot_general | solution.py:235
  131.0 0.0 copy-done.2
  131.0 4.2 %shard_map.141 = bf16[1,512,512]{2,1,0:T(8,128)(2,1)} custom-call(bf16[1,512,512]{2,1,0:T(8,128)(2,1)} %fusion.27.q_ref, bf16[1,256,1152]{2,1,0:T(8,128)(2,1)} %bitcast.49, bf16[1,256,1152]{2,1,0:T(8,128)(2,1)} %bitcast.50, f32[1,1,256]{2,1,0:T(1,128)} %compare_select_fusion.b_ref), custom_call_target="tpu_custom_call" | custom-call | flops 268435456 | bytes 1572864 | tf_op jit(solution)/shard_map/pallas_call | solution.py:105
  135.2 1.9 copy.26
  137.1 0.6 broadcast.192
  137.7 4.7 %reduce.11 = bf16[512,512]{1,0:T(8,128)(2,1)} reduce(bf16[512,1,512]{2,1,0:T(2,128)(2,1)S(1)} %bitcast.52, bf16[]{:T(256)} %broadcast.192), dimensions={1}, to_apply=%bitcast.48.reduce_sub_computation | reduce | bytes 1048578
  142.3 1.4 reshape.227
  143.8 14.2 %all_to_all.24 = bf16[16,2,8192]{2,1,0:T(2,128)(2,1)} all-to-all(bf16[16,2,8192]{2,1,0:T(2,128)(2,1)S(1)} %reshape.227), channel_id=1, replica_groups=mesh['seq'=16,'head'=8] {'seq'}, dimensions={0} | all-to-all | bytes 1048576 | tf_op jit(solution)/shard_map/all_to_all | solution.py:240
  157.9 2.2 %reshape.228 = bf16[512,1,512]{2,1,0:T(2,128)(2,1)S(1)} reshape(bf16[16,2,8192]{2,1,0:T(2,128)(2,1)} %all_to_all.24) | data formatting | bytes 1048576
  160.2 0.1 copy.24
  160.3 6.5 %convolution_convert_fusion = bf16[16,32,4096]{2,1,0:T(8,128)(2,1)} fusion(bf16[16,32,512]{2,1,0:T(8,128)(2,1)S(1)} %bitcast.53, bf16[512,4096]{1,0:T(8,128)(2,1)} %param.27), kind=kOutput, calls=%fused_computation.4 | convolution fusion | flops 2149580800 | bytes 8912896 | tf_op jit(solution)/shard_map/ste,ed->std/dot_general | solution.py:241
  166.8 0.0 reduce-scatter.2.cloned.1.call-update
  166.8 35.6 %reduce-scatter.2.cloned.1.call-done = bf16[16,32,512]{2,1,0:T(8,128)(2,1)} async-done(((bf16[16,32,4096]{2,1,0:T(8,128)(2,1)}), bf16[16,32,512]{2,1,0:T(8,128)(2,1)}) %reduce-scatter.2.cloned.1.call-update) | async-done | bytes 524304 | tf_op jit(solution)/shard_map/reduce_scatter | solution.py:244
  202.4 2.2 %fusion.26 = bf16[16,32,512]{2,1,0:T(8,128)(2,1)} fusion(bf16[16,32,512]{2,1,0:T(8,128)(2,1)} %reduce-scatter.2.cloned.1.call-done, s32[16,32]{1,0:T(8,128)S(1)} %copy-done.4, bf16[28,4096]{1,0:T(8,128)(2,1)S(1)} %copy-done.3, s32[]{:T(128)S(6)} %select_n.44), kind=kOutput, calls=%fused_computation.37 | convolution fusion | flops 16005120 | bytes 1089540 | tf_op jit(solution)/shard_map/stv,vd->std/dot_general | solution.py:226
  (16 shorter events, 0.1 us)
Async XLA Ops:
  7.2 74.1 %copy-start = (bf16[1024,1024]{1,0:T(8,128)(2,1)S(1)}, bf16[1024,1024]{1,0:T(8,128)(2,1)}, u32[]{:S(2)}) copy-start(bf16[1024,1024]{1,0:T(8,128)(2,1)} %param.21) | copy-start | bytes 6291460
  7.2 10.1 %copy-start.1 = (bf16[2,512,1024]{2,1,0:T(8,128)(2,1)S(1)}, bf16[2,512,1024]{2,1,0:T(8,128)(2,1)}, u32[]{:S(2)}) copy-start(bf16[2,512,1024]{2,1,0:T(8,128)(2,1)} %param.15) | copy-start | bytes 6291460
  7.2 10.7 %copy-start.9 = (s32[16]{0:T(128)S(1)}, s32[16]{0:T(128)}, u32[]{:S(2)}) copy-start(s32[16]{0:T(128)} %param.17) | copy-start | bytes 196
  7.2 13.3 %copy-start.4 = (s32[16,32]{1,0:T(8,128)S(1)}, s32[16,32]{1,0:T(8,128)}, u32[]{:S(2)}) copy-start(s32[16,32]{1,0:T(8,128)} %param.22) | copy-start | bytes 6148
  10.4 26.8 %collective-permute-start.1 = (bf16[2,256,1024]{2,1,0:T(8,128)(2,1)}, bf16[2,256,1024]{2,1,0:T(8,128)(2,1)S(1)}, u32[]{:S(2)}, u32[]{:S(2)}) collective-permute-start(bf16[2,256,1024]{2,1,0:T(8,128)(2,1)} %get-tuple-element.17), channel_id=1, source_target_pairs={{8,0},{16,8},{24,16},{32,24},{40,32},{48,40},{56,48},{64,56},{72,6... | collective-permute-start | bytes 3145736 | tf_op jit(solution)/shard_map/ppermute | solution.py:156
  11.7 26.8 %collective-permute-start = (bf16[2,256,1024]{2,1,0:T(8,128)(2,1)}, bf16[2,256,1024]{2,1,0:T(8,128)(2,1)}, u32[]{:S(2)}, u32[]{:S(2)}) collective-permute-start(bf16[2,256,1024]{2,1,0:T(8,128)(2,1)} %get-tuple-element.16), channel_id=1, source_target_pairs={{0,8},{8,16},{16,24},{24,32},{32,40},{40,48},{48,56},{56,64},{64,7... | collective-permute-start | bytes 3145736 | tf_op jit(solution)/shard_map/ppermute | solution.py:155
  28.8 11.5 %copy-start.5 = (bf16[1024,1024]{1,0:T(8,128)(2,1)S(1)}, bf16[1024,1024]{1,0:T(8,128)(2,1)}, u32[]{:S(2)}) copy-start(bf16[1024,1024]{1,0:T(8,128)(2,1)} %param.20) | copy-start | bytes 6291460
  28.8 11.5 %copy-start.6 = (bf16[1024,1024]{1,0:T(8,128)(2,1)S(1)}, bf16[1024,1024]{1,0:T(8,128)(2,1)}, u32[]{:S(2)}) copy-start(bf16[1024,1024]{1,0:T(8,128)(2,1)} %param.19) | copy-start | bytes 6291460
  81.2 21.1 %copy-start.7 = (bf16[1024,512]{1,0:T(8,128)(2,1)S(1)}, bf16[1024,512]{1,0:T(8,128)(2,1)}, u32[]{:S(2)}) copy-start(bf16[1024,512]{1,0:T(8,128)(2,1)} %param.26) | copy-start | bytes 3145732
  81.2 21.1 %copy-start.8 = (bf16[1024,512]{1,0:T(8,128)(2,1)S(1)}, bf16[1024,512]{1,0:T(8,128)(2,1)}, u32[]{:S(2)}) copy-start(bf16[1024,512]{1,0:T(8,128)(2,1)} %param.25) | copy-start | bytes 3145732
  102.2 11.8 %copy-start.3 = (bf16[28,4096]{1,0:T(8,128)(2,1)S(1)}, bf16[28,4096]{1,0:T(8,128)(2,1)}, u32[]{:S(2)}) copy-start(bf16[28,4096]{1,0:T(8,128)(2,1)} %param.23) | copy-start | bytes 688132
  104.0 22.6 %all-to-all-start = ((bf16[16,16,1152]{2,1,0:T(8,128)(2,1)}), bf16[16,16,1152]{2,1,0:T(8,128)(2,1)S(1)}, u32[]{:S(2)}, u32[]{:S(2)}) async-start(bf16[16,16,1152]{2,1,0:T(8,128)(2,1)} %fusion.34), calls=%async_computation | async-start | bytes 1179648 | tf_op jit(solution)/shard_map/all_to_all | solution.py:207
  113.9 88.5 %reduce-scatter.2.cloned.1.call-start = ((), (), s32[]{:S(2)}) async-start(), calls=%async_computation.3 | async-start | bytes 4718592 | tf_op jit(solution)/shard_map/reduce_scatter | solution.py:244
  126.6 4.4 %copy-start.2 = (bf16[16,16,1152]{2,1,0:T(8,128)(2,1)}, bf16[16,16,1152]{2,1,0:T(8,128)(2,1)S(1)}, u32[]{:S(2)}) copy-start(bf16[16,16,1152]{2,1,0:T(8,128)(2,1)S(1)} %all-to-all-done) | copy-start | bytes 1769476
Sparse Core Ops, SparseCore 0:
  166.9 35.4 reduce-scatter.1

commit v8 on v7

--- a/solution.py
+++ b/solution.py
@@ -226,18 +226,14 @@
     own_part = jnp.einsum(
         "stv,vd->std", onehot, own_table, preferred_element_type=jnp.float32
     ).astype(jnp.bfloat16)
-    onehot_one = (
-        ids_one[:, :, None] == jnp.arange(vocab, dtype=jnp.int32)[None, None, :]
-    ).astype(jnp.bfloat16)
     query_table = jnp.einsum(
         "vd,de->ve", rms_rows(embedding), dec_query, preferred_element_type=jnp.float32
     ).astype(jnp.bfloat16)
-    query_one = jnp.einsum(
-        "stv,ve->ste", onehot_one, query_table, preferred_element_type=jnp.float32
-    ).astype(jnp.bfloat16)
+    query_one = jnp.take(query_table, ids_one[0], axis=0)[None]
     mem_bias = jnp.where(mem_valid, pooled_bias, masked_score)[:, None, :]
     context_one = cross_attention(query_one, received, mem_bias, heads_here, dec_head)
-    dec_context = lax.all_to_all(context_one, "seq", 1, 0, tiled=True)
+    context_one = context_one.reshape(seq_count, tok_count, local_width)
+    dec_context = lax.all_to_all(context_one, "seq", 0, 0, tiled=True)
     partial_sums = jnp.einsum(
         "ste,ed->std", dec_context, dec_out, preferred_element_type=jnp.float32
     )

time: 212 us -> 201 us (0.948)
  waiting for transfers between devices: 49.1 us -> 45.2 us
  local copies, waits for them, and re-layouts: 11.9 us -> 9.73 us
    unnamed x1 -> x0, other arithmetic: 4.66 us -> none
    unnamed x24 -> x30, local copies, waits for them, and re-layouts: 4.41 us -> 0.08 us
  transfers between devices with their start and end apart: 4 -> 4, of which waited for: 4 -> 2; matrix products, arithmetic and copies ran while one was open for 10% -> 14% of each run, Pallas kernels for 0% -> 0%
where the time goes in v8:
time: 201 us; the launch traced here: 200 us
  waiting for transfers between devices  45.2 us (22%)
  matrix products  38.6 us (19%)
  Pallas kernels  34.4 us (17%)
  blocking collectives  28.8 us (14%)
  starting transfers between devices  14.8 us (7%)
  other arithmetic  14.5 us (7%)
  between operations  14.3 us (7%)
  local copies, waits for them, and re-layouts  9.73 us (5%)
    reduce_scatter x1, waiting for transfers between devices, per_device(): lax.psum_scatter(partial_sums.astype(jnp.bfloat16), 'head', scatter_dimen...  35.6 us
    pallas_call x1, Pallas kernels, band_attention(): pl.pallas_call(band_kernel, out_shape=jax.ShapeDtypeStruct(query_enc.shap...  30.2 us
    all_to_all x1, blocking collectives, per_device(): dec_context = lax.all_to_all(context_one, 'seq', 0, 0, tiled=True)  14.4 us
    all_gather x1, blocking collectives, per_device(): spectra_all = lax.all_gather(pooled, 'head', axis=0, tiled=True)  14.3 us
    all_to_all x1, waiting for transfers between devices, per_device(): received = lax.all_to_all(payload, 'seq', 0, 1, tiled=True)  9.62 us
    all_to_all x1, starting transfers between devices, per_device(): received = lax.all_to_all(payload, 'seq', 0, 1, tiled=True)  7.93 us
    dot_general x1, matrix products, per_device(): jnp.einsum('sbd,de->sbe', normed, kv_weights, preferred_element_type=jnp....  7.54 us
    dot_general x1, matrix products, per_device(): jnp.einsum('ste,ed->std', dec_context, dec_out, preferred_element_type=jn...  6.46 us
  transfers between devices with their start and end apart: 4, of which 2 were waited for; matrix products, arithmetic and copies ran while one was open for 14% of the time, Pallas kernels for 0%

profile of v8, /device:TPU:0, one launch (start us, length us, event | category | flops | bytes accessed | tf_op | source)
XLA Modules:
  0.0 200.3 jit_solution(15937979371821004722)
XLA Ops:
  7.2 0.0 copy-start
  7.2 0.0 copy-start.1
  7.2 0.0 copy-start.14
  7.2 0.0 copy-start.3
  7.2 0.0 copy-start.5
  7.2 3.2 %fusion.49 = (bf16[2,256,1024]{2,1,0:T(8,128)(2,1)}, bf16[2,256,1024]{2,1,0:T(8,128)(2,1)}) fusion(bf16[2,512,1024]{2,1,0:T(8,128)(2,1)} %param.15), kind=kLoop, calls=%fused_computation.87 | loop fusion | bytes 4194304 | tf_op jit(solution)/shard_map/slice | solution.py:155
  10.4 1.3 collective-permute-start.1
  11.7 5.5 %collective-permute-start = (bf16[2,256,1024]{2,1,0:T(8,128)(2,1)}, bf16[2,256,1024]{2,1,0:T(8,128)(2,1)}, u32[]{:S(2)}, u32[]{:S(2)}) collective-permute-start(bf16[2,256,1024]{2,1,0:T(8,128)(2,1)} %get-tuple-element.16), channel_id=1, source_target_pairs={{0,8},{8,16},{16,24},{24,32},{32,40},{40,48},{48,56},{56,64},{64,7... | collective-permute-start | bytes 3145736 | tf_op jit(solution)/shard_map/ppermute | solution.py:155
  17.3 0.0 copy-done.1
  17.3 0.5 fusion.2
  17.8 0.8 fusion.32
  18.6 0.0 copy-done.14
  18.6 0.1 dynamic_slice.15
  18.7 0.6 dynamic_slice.18
  19.3 1.7 dynamic-slice_reduce_fusion
  20.9 0.8 and_select_fusion
  21.8 0.6 broadcast_compare_fusion.1
  22.4 0.0 copy-done.3
  22.4 0.7 fusion.34
  23.1 0.0 copy-done.5
  23.1 0.6 copy.19
  23.8 0.8 reshape.235
  24.6 0.0 copy-start.4
  24.6 6.0 %fusion.16.q_ref = bf16[2,512,1024]{2,1,0:T(8,128)(2,1)} fusion(bf16[1024,1024]{1,0:T(8,128)(2,1)} %param.18, bf16[2,512,1024]{2,1,0:T(8,128)(2,1)} %param.15, f32[2,512]{1,0:T(2,128)S(1)} %add_rsqrt_fusion.2), kind=kOutput, calls=%fused_computation.29 | convolution fusion | flops 2151677952 | bytes 6295552 | tf_op jit(solution)/shard_map/sbd,de->sbe/dot_general | solution.py:159
  30.6 0.0 copy-done.4
  30.6 2.0 %broadcast_select_fusion.b_ref = f32[2,2,256,768]{3,2,1,0:T(8,128)} fusion(f32[2,2,768]{2,1,0:T(2,128)S(1)} %copy.18, pred[256,768]{1,0:T(8,128)(4,1)S(1)} %copy-done.4), kind=kLoop, calls=%fused_computation.30 | loop fusion | flops 786432 | bytes 3354624 | tf_op jit(solution)/shard_map/jit(_where)/select_n | solution.py:184
  32.6 0.1 reduce_max.11
  32.7 1.2 compare_select_fusion.2.b_ref
  33.9 7.5 %convolution_convert_fusion.1 = bf16[2,512,2048]{2,1,0:T(8,128)(2,1)S(1)} fusion(bf16[1024,1024]{1,0:T(8,128)(2,1)} %param.20, bf16[1024,1024]{1,0:T(8,128)(2,1)} %param.19, bf16[2,512,1024]{2,1,0:T(8,128)(2,1)} %param.15, f32[2,512]{1,0:T(2,128)S(1)} %add_rsqrt_fusion.2), kind=kOutput, calls=%fused_computation.17 | convolution fusion | flops 4308598784 | bytes 10489856 | tf_op jit(solution)/shard_map/sbd,de->sbe/dot_general | solution.py:162
  41.4 0.0 collective-permute-done.1
  41.4 0.0 collective-permute-done
  41.4 1.7 fusion
  43.2 0.0 copy-done.10
  43.2 0.0 copy-done.11
  43.2 6.3 %convolution_convert_fusion.2 = bf16[2,512,2048]{2,1,0:T(8,128)(2,1)S(1)} fusion(bf16[1024,1024]{1,0:T(8,128)(2,1)S(1)} %copy-done.10, bf16[1024,1024]{1,0:T(8,128)(2,1)S(1)} %copy-done.11, f32[2,512]{1,0:T(2,128)S(1)} %add_rsqrt_fusion.1, bf16[2,256,1024]{2,1,0:T(8,128)(2,1)S(1)} %collective-permute-done.1, bf16[2,256,1024]{2,1,0:T(8,128)(2,1)} %collective-permute-done), kind=kOutput, calls=%fused_computation.18 | convolution fusion | flops 4311744512 | bytes 10489856 | tf_op jit(solution)/shard_map/sbd,de->sbe/dot_general | solution.py:166
  49.5 0.5 fusion.48
  50.0 4.0 %pad_maximum_fusion.k_ref.v_ref = bf16[2,1024,2048]{2,1,0:T(8,128)(2,1)} fusion(bf16[2,256,2048]{2,1,0:T(8,128)(2,1)S(1)} %get-tuple-element.15, bf16[2,512,2048]{2,1,0:T(8,128)(2,1)S(1)} %convolution_convert_fusion.1, bf16[2,256,2048]{2,1,0:T(8,128)(2,1)S(1)} %get-tuple-element.14), kind=kLoop, calls=%fused_computation.1 | loop fusion | flops 25165824 | bytes 16777216 | tf_op jit(solution)/shard_map/concatenate | solution.py:169
  54.0 30.2 %shard_map.140 = bf16[2,512,1024]{2,1,0:T(8,128)(2,1)} custom-call(bf16[2,512,1024]{2,1,0:T(8,128)(2,1)} %fusion.16.q_ref, bf16[2,1024,2048]{2,1,0:T(8,128)(2,1)} %pad_maximum_fusion.k_ref.v_ref, bf16[2,1024,2048]{2,1,0:T(8,128)(2,1)} %pad_maximum_fusion.k_ref.v_ref, f32[2,2,256,768]{3,2,1,0:T(8,128)} %broadcast_select_fusion.b_ref), custom_call_target="tpu_custom_call" | custom-call | flops 6442450944 | bytes 15728640 | tf_op jit(solution)/shard_map/pallas_call | solution.py:67
  84.2 0.0 copy-done
  84.2 0.0 copy-done.8
  84.2 0.0 copy-start.12
  84.2 0.0 copy-start.13
  84.2 6.3 %convert_reduce_fusion = (f32[2,16,1024]{2,1,0:T(8,128)S(1)}, bf16[2,512,1024]{2,1,0:T(8,128)(2,1)}) fusion(bf16[2,512,1024]{2,1,0:T(8,128)(2,1)} %shard_map.140, bf16[1024,1024]{1,0:T(8,128)(2,1)S(1)} %copy-done, bf16[2,512,1024]{2,1,0:T(8,128)(2,1)} %param.15, pred[2,512]{1,0:T(4,128)(4,1)S(1)} %copy-done.8), kind=kOutput, calls=%fused_computation.15 | convolution fusion | flops 2153742336 | bytes 8520704 | tf_op jit(solution)/shard_map/sbd,de->sbe/dot_general | solution.py:188
  90.5 14.3 %all_gather.3 = bf16[16,16,1024]{2,1,0:T(8,128)(2,1)S(1)} all-gather(bf16[2,16,1024]{2,1,0:T(8,128)(2,1)S(1)} %multiply_convert_fusion), channel_id=1, replica_groups=mesh['seq'=16,'head'=8] {'head'}, dimensions={0}, use_global_device_ids=true | all-gather | bytes 589824 | tf_op jit(solution)/shard_map/all_gather | solution.py:196
  104.9 0.2 fusion.28
  105.1 0.0 copy-done.12
  105.1 0.0 copy-done.13
  105.1 0.8 fusion.23
  105.9 0.0 copy-done.7
  105.9 0.9 fusion.33
  106.7 7.9 %all-to-all-start = ((bf16[16,16,1152]{2,1,0:T(8,128)(2,1)}), bf16[16,16,1152]{2,1,0:T(8,128)(2,1)S(1)}, u32[]{:S(2)}, u32[]{:S(2)}) async-start(bf16[16,16,1152]{2,1,0:T(8,128)(2,1)} %fusion.33), calls=%async_computation | async-start | bytes 1179648 | tf_op jit(solution)/shard_map/all_to_all | solution.py:207
  114.7 0.0 reduce-scatter.2.cloned.1.call-start
  114.7 3.1 %convolution_convert_fusion.4 = bf16[28,512]{1,0:T(8,128)(2,1)S(1)} fusion(bf16[4096,512]{1,0:T(8,128)(2,1)} %param.24, bf16[28,4096]{1,0:T(8,128)(2,1)S(1)} %copy-done.3, f32[28]{0:T(128)S(1)} %add_rsqrt_fusion.3), kind=kOutput, calls=%fused_computation.40 | convolution fusion | flops 117798912 | bytes 4452464 | tf_op jit(solution)/shard_map/vd,de->ve/dot_general | solution.py:229
  117.8 9.6 %all-to-all-done = bf16[16,16,1152]{2,1,0:T(8,128)(2,1)S(1)} async-done(((bf16[16,16,1152]{2,1,0:T(8,128)(2,1)}), bf16[16,16,1152]{2,1,0:T(8,128)(2,1)S(1)}, u32[]{:S(2)}, u32[]{:S(2)}) %all-to-all-start) | async-done | bytes 589856 | tf_op jit(solution)/shard_map/all_to_all | solution.py:207
  127.4 0.1 reshape.240
  127.6 0.1 reshape.239
  127.6 2.0 gather_fusion
  129.6 0.9 bitcast_select_fusion.q_ref
  130.5 4.2 %shard_map.141 = bf16[1,512,512]{2,1,0:T(8,128)(2,1)} custom-call(bf16[1,512,512]{2,1,0:T(8,128)(2,1)} %bitcast_select_fusion.q_ref, bf16[1,256,1152]{2,1,0:T(8,128)(2,1)} %bitcast.47, bf16[1,256,1152]{2,1,0:T(8,128)(2,1)} %bitcast.48, f32[1,1,256]{2,1,0:T(1,128)} %compare_select_fusion.2.b_ref), custom_call_target="tpu_custom_call" | custom-call | flops 268435456 | bytes 1572864 | tf_op jit(solution)/shard_map/pallas_call | solution.py:105
  134.8 14.4 %all_to_all.17 = bf16[16,32,512]{2,1,0:T(8,128)(2,1)S(1)} all-to-all(bf16[16,32,512]{2,1,0:T(8,128)(2,1)} %bitcast.49), channel_id=1, replica_groups=mesh['seq'=16,'head'=8] {'seq'}, dimensions={0} | all-to-all | bytes 1048576 | tf_op jit(solution)/shard_map/all_to_all | solution.py:236
  149.2 6.5 %convolution_convert_fusion = bf16[16,32,4096]{2,1,0:T(8,128)(2,1)} fusion(bf16[16,32,512]{2,1,0:T(8,128)(2,1)S(1)} %all_to_all.17, bf16[512,4096]{1,0:T(8,128)(2,1)} %param.27), kind=kOutput, calls=%fused_computation.5 | convolution fusion | flops 2149580800 | bytes 8912896 | tf_op jit(solution)/shard_map/ste,ed->std/dot_general | solution.py:237
  155.7 0.0 reduce-scatter.2.cloned.1.call-update
  155.7 35.6 %reduce-scatter.2.cloned.1.call-done = bf16[16,32,512]{2,1,0:T(8,128)(2,1)} async-done(((bf16[16,32,4096]{2,1,0:T(8,128)(2,1)}), bf16[16,32,512]{2,1,0:T(8,128)(2,1)}) %reduce-scatter.2.cloned.1.call-update) | async-done | bytes 524304 | tf_op jit(solution)/shard_map/reduce_scatter | solution.py:240
  191.3 2.2 %fusion.26 = bf16[16,32,512]{2,1,0:T(8,128)(2,1)} fusion(bf16[16,32,512]{2,1,0:T(8,128)(2,1)} %reduce-scatter.2.cloned.1.call-done, s32[16,32]{1,0:T(8,128)S(1)} %copy-done.6, bf16[28,4096]{1,0:T(8,128)(2,1)S(1)} %copy-done.3, s32[]{:T(128)S(6)} %select_n.71), kind=kOutput, calls=%fused_computation.37 | convolution fusion | flops 16005120 | bytes 1089540 | tf_op jit(solution)/shard_map/stv,vd->std/dot_general | solution.py:226
  (27 shorter events, 0.2 us)
Async XLA Ops:
  7.2 77.0 %copy-start = (bf16[1024,1024]{1,0:T(8,128)(2,1)S(1)}, bf16[1024,1024]{1,0:T(8,128)(2,1)}, u32[]{:S(2)}) copy-start(bf16[1024,1024]{1,0:T(8,128)(2,1)} %param.21) | copy-start | bytes 6291460
  7.2 10.1 %copy-start.1 = (bf16[2,512,1024]{2,1,0:T(8,128)(2,1)S(1)}, bf16[2,512,1024]{2,1,0:T(8,128)(2,1)}, u32[]{:S(2)}) copy-start(bf16[2,512,1024]{2,1,0:T(8,128)(2,1)} %param.15) | copy-start | bytes 6291460
  7.2 11.4 %copy-start.14 = (s32[16]{0:T(128)S(1)}, s32[16]{0:T(128)}, u32[]{:S(2)}) copy-start(s32[16]{0:T(128)} %param.17) | copy-start | bytes 196
  7.2 15.2 %copy-start.3 = (bf16[28,4096]{1,0:T(8,128)(2,1)S(1)}, bf16[28,4096]{1,0:T(8,128)(2,1)}, u32[]{:S(2)}) copy-start(bf16[28,4096]{1,0:T(8,128)(2,1)} %param.23) | copy-start | bytes 688132
  7.2 15.9 %copy-start.5 = (s32[16,32]{1,0:T(8,128)S(1)}, s32[16,32]{1,0:T(8,128)}, u32[]{:S(2)}) copy-start(s32[16,32]{1,0:T(8,128)} %param.22) | copy-start | bytes 6148
  10.4 31.0 %collective-permute-start.1 = (bf16[2,256,1024]{2,1,0:T(8,128)(2,1)}, bf16[2,256,1024]{2,1,0:T(8,128)(2,1)S(1)}, u32[]{:S(2)}, u32[]{:S(2)}) collective-permute-start(bf16[2,256,1024]{2,1,0:T(8,128)(2,1)} %get-tuple-element.17), channel_id=1, source_target_pairs={{8,0},{16,8},{24,16},{32,24},{40,32},{48,40},{56,48},{64,56},{72,6... | collective-permute-start | bytes 3145736 | tf_op jit(solution)/shard_map/ppermute | solution.py:156
  11.7 29.7 %collective-permute-start = (bf16[2,256,1024]{2,1,0:T(8,128)(2,1)}, bf16[2,256,1024]{2,1,0:T(8,128)(2,1)}, u32[]{:S(2)}, u32[]{:S(2)}) collective-permute-start(bf16[2,256,1024]{2,1,0:T(8,128)(2,1)} %get-tuple-element.16), channel_id=1, source_target_pairs={{0,8},{8,16},{16,24},{24,32},{32,40},{40,48},{48,56},{56,64},{64,7... | collective-permute-start | bytes 3145736 | tf_op jit(solution)/shard_map/ppermute | solution.py:155
  24.6 6.0 %copy-start.4 = (pred[256,768]{1,0:T(8,128)(4,1)S(1)}, pred[256,768]{1,0:T(8,128)(4,1)}, u32[]{:S(2)}) copy-start(pred[256,768]{1,0:T(8,128)(4,1)} %fusion.32) | copy-start | bytes 589828
  33.9 9.3 %copy-start.10 = (bf16[1024,1024]{1,0:T(8,128)(2,1)S(1)}, bf16[1024,1024]{1,0:T(8,128)(2,1)}, u32[]{:S(2)}) copy-start(bf16[1024,1024]{1,0:T(8,128)(2,1)} %param.20) | copy-start | bytes 6291460
  33.9 9.3 %copy-start.11 = (bf16[1024,1024]{1,0:T(8,128)(2,1)S(1)}, bf16[1024,1024]{1,0:T(8,128)(2,1)}, u32[]{:S(2)}) copy-start(bf16[1024,1024]{1,0:T(8,128)(2,1)} %param.19) | copy-start | bytes 6291460
  54.0 30.2 %copy-start.8 = (pred[2,512]{1,0:T(4,128)(4,1)S(1)}, pred[2,512]{1,0:T(4,128)(4,1)}, u32[]{:S(2)}) copy-start(pred[2,512]{1,0:T(4,128)(4,1)} %broadcast_compare_fusion.1) | copy-start | bytes 3076
  84.2 20.9 %copy-start.12 = (bf16[1024,512]{1,0:T(8,128)(2,1)S(1)}, bf16[1024,512]{1,0:T(8,128)(2,1)}, u32[]{:S(2)}) copy-start(bf16[1024,512]{1,0:T(8,128)(2,1)} %param.26) | copy-start | bytes 3145732
  84.2 20.9 %copy-start.13 = (bf16[1024,512]{1,0:T(8,128)(2,1)S(1)}, bf16[1024,512]{1,0:T(8,128)(2,1)}, u32[]{:S(2)}) copy-start(bf16[1024,512]{1,0:T(8,128)(2,1)} %param.25) | copy-start | bytes 3145732
  90.5 15.3 %copy-start.7 = (bf16[16,1,32]{2,1,0:T(2,128)(2,1)S(1)}, bf16[16,1,32]{2,1,0:T(2,128)(2,1)}, u32[]{:S(2)}) copy-start(bf16[16,1,32]{2,1,0:T(2,128)(2,1)} %copy.19) | copy-start | bytes 3076
  104.9 9.8 %copy-start.9 = (f32[28]{0:T(128)S(1)}, f32[28]{0:T(128)}, u32[]{:S(2)}) copy-start(f32[28]{0:T(128)} %fusion.34) | copy-start | bytes 340
  106.7 20.7 %all-to-all-start = ((bf16[16,16,1152]{2,1,0:T(8,128)(2,1)}), bf16[16,16,1152]{2,1,0:T(8,128)(2,1)S(1)}, u32[]{:S(2)}, u32[]{:S(2)}) async-start(bf16[16,16,1152]{2,1,0:T(8,128)(2,1)} %fusion.33), calls=%async_computation | async-start | bytes 1179648 | tf_op jit(solution)/shard_map/all_to_all | solution.py:207
  114.7 76.6 %reduce-scatter.2.cloned.1.call-start = ((), (), s32[]{:S(2)}) async-start(), calls=%async_computation.3 | async-start | bytes 4718592 | tf_op jit(solution)/shard_map/reduce_scatter | solution.py:240
  127.4 3.1 %copy-start.2 = (bf16[16,16,1152]{2,1,0:T(8,128)(2,1)}, bf16[16,16,1152]{2,1,0:T(8,128)(2,1)S(1)}, u32[]{:S(2)}) copy-start(bf16[16,16,1152]{2,1,0:T(8,128)(2,1)S(1)} %all-to-all-done) | copy-start | bytes 1769476
  155.7 35.6 %copy-start.6 = (s32[16,32]{1,0:T(8,128)S(1)}, s32[16,32]{1,0:T(8,128)}, u32[]{:S(2)}) copy-start(s32[16,32]{1,0:T(8,128)} %param.22) | copy-start | bytes 6148
Sparse Core Ops, SparseCore 0:
  155.8 35.4 reduce-scatter.1

commit v9 on v8

--- a/solution.py
+++ b/solution.py
@@ -30,49 +30,60 @@
     return (weights / jnp.sum(weights, axis=-1, keepdims=True)).astype(jnp.bfloat16)
 
 
-def band_kernel(q_ref, k_ref, v_ref, b_ref, o_ref):
-    qb = pl.program_id(2)
-    q0 = pl.multiple_of(qb * QBLOCK, QBLOCK)
-    kwin = QBLOCK + WINDOW
-    bias = b_ref[0, 0]
+def band_kernel(q_ref, km_ref, vm_ref, ke_ref, ve_ref, bm_ref, be_ref, o_ref):
+    bias_mid = bm_ref[0, 0]
+    bias_edge = be_ref[0, 0]
     lane = lax.broadcasted_iota(jnp.int32, (1, 128), 1)
     low = lane < 64
+    dims = (((1,), (1,)), ((), ()))
     for pair in range(HGROUP // 128):
         cols = slice(pair * 128, (pair + 1) * 128)
         q = q_ref[0, :, cols] * 0.125
-        k = k_ref[0, pl.ds(q0, kwin), cols]
-        v = v_ref[0, pl.ds(q0, kwin), cols]
+        key_mid = km_ref[0, :, cols]
+        key_edge = ke_ref[0, :, cols]
         out = None
         for half in range(2):
             sel = low if half == 0 else jnp.logical_not(low)
             qh = jnp.where(sel, q, jnp.zeros_like(q))
-            s = lax.dot_general(
-                qh, k, (((1,), (1,)), ((), ())), preferred_element_type=jnp.float32
-            ) + bias
-            m = jnp.max(s, axis=1, keepdims=True)
-            p = jnp.exp(s - m)
-            total = jnp.sum(p, axis=1, keepdims=True)
-            pv = jnp.dot(p.astype(jnp.bfloat16), v, preferred_element_type=jnp.float32)
+            s_mid = lax.dot_general(qh, key_mid, dims, preferred_element_type=jnp.float32)
+            s_mid = s_mid + bias_mid
+            s_edge = lax.dot_general(qh, key_edge, dims, preferred_element_type=jnp.float32)
+            s_edge = s_edge + bias_edge
+            m = jnp.maximum(
+                jnp.max(s_mid, axis=1, keepdims=True), jnp.max(s_edge, axis=1, keepdims=True)
+            )
+            p_mid = jnp.exp(s_mid - m)
+            p_edge = jnp.exp(s_edge - m)
+            total = jnp.sum(p_mid, axis=1, keepdims=True) + jnp.sum(p_edge, axis=1, keepdims=True)
+            pv = jnp.dot(
+                p_mid.astype(jnp.bfloat16), vm_ref[0, :, cols], preferred_element_type=jnp.float32
+            ) + jnp.dot(
+                p_edge.astype(jnp.bfloat16), ve_ref[0, :, cols], preferred_element_type=jnp.float32
+            )
             pv = pv / total
             out = pv if out is None else jnp.where(low, out, pv)
         o_ref[0, :, cols] = out.astype(o_ref.dtype)
 
 
-def band_attention(query_enc, keyval, full_bias):
-    spec_dev, bin_dev, width = query_enc.shape
-    key_span = keyval.shape[1]
+def band_attention(qkv, keyval_edges, bias_mid, bias_edge):
+    spec_dev, bin_dev, triple = qkv.shape
+    width = triple // 3
+    edge_rows = keyval_edges.shape[1] // 2
     groups = width // HGROUP
     qblocks = bin_dev // QBLOCK
-    kwin = QBLOCK + WINDOW
+    kwin = bin_dev + edge_rows
     return pl.pallas_call(
         band_kernel,
-        out_shape=jax.ShapeDtypeStruct(query_enc.shape, jnp.bfloat16),
+        out_shape=jax.ShapeDtypeStruct((spec_dev, bin_dev, width), jnp.bfloat16),
         grid=(spec_dev, groups, qblocks),
         in_specs=[
             pl.BlockSpec((1, QBLOCK, HGROUP), lambda s, g, b: (s, b, g)),
-            pl.BlockSpec((1, key_span, HGROUP), lambda s, g, b: (s, 0, g)),
-            pl.BlockSpec((1, key_span, HGROUP), lambda s, g, b: (s, 0, groups + g)),
-            pl.BlockSpec((1, 1, QBLOCK, kwin), lambda s, g, b: (s, b, 0, 0)),
+            pl.BlockSpec((1, bin_dev, HGROUP), lambda s, g, b: (s, 0, groups + g)),
+            pl.BlockSpec((1, bin_dev, HGROUP), lambda s, g, b: (s, 0, 2 * groups + g)),
+            pl.BlockSpec((1, edge_rows, HGROUP), lambda s, g, b: (s, b, g)),
+            pl.BlockSpec((1, edge_rows, HGROUP), lambda s, g, b: (s, b, groups + g)),
+            pl.BlockSpec((1, 1, QBLOCK, bin_dev), lambda s, g, b: (s, b, 0, 0)),
+            pl.BlockSpec((1, 1, QBLOCK, edge_rows), lambda s, g, b: (s, b, 0, 0)),
         ],
         out_specs=pl.BlockSpec((1, QBLOCK, HGROUP), lambda s, g, b: (s, b, g)),
         compiler_params=pltpu.CompilerParams(
@@ -81,10 +92,10 @@
         cost_estimate=pl.CostEstimate(
             flops=spec_dev * bin_dev * kwin * width * 8,
             transcendentals=spec_dev * bin_dev * kwin * HE,
-            bytes_accessed=spec_dev * (bin_dev * width * 4 + key_span * width * 4)
-            + full_bias.size * 4,
-        ),
-    )(query_enc, keyval, keyval, full_bias)
+            bytes_accessed=spec_dev * bin_dev * width * 10
+            + (bias_mid.size + bias_edge.size) * 4,
+        ),
+    )(qkv, qkv, qkv, keyval_edges, keyval_edges, bias_mid, bias_edge)
 
 
 def cross_kernel(q_ref, k_ref, v_ref, b_ref, o_ref):
@@ -148,6 +159,7 @@
         bias_pad, (first_spec, first_bin), (spec_dev, bin_dev + 2 * half_span)
     )
     kv_weights = jnp.concatenate([enc_key, enc_value], axis=1)
+    qkv_weights = jnp.concatenate([enc_query, enc_key, enc_value], axis=1)
 
     count = lax.axis_size("seq")
     forward = [(i, i + 1) for i in range(count - 1)]
@@ -156,33 +168,31 @@
     high_edge = lax.ppermute(spectra[:, :half_span], "seq", backward)
 
     normed = rms_rows(spectra)
-    query_enc = jnp.einsum(
-        "sbd,de->sbe", normed, enc_query, preferred_element_type=jnp.float32
-    ).astype(jnp.bfloat16)
-    keyval_mid = jnp.einsum(
-        "sbd,de->sbe", normed, kv_weights, preferred_element_type=jnp.float32
+    qkv = jnp.einsum(
+        "sbd,de->sbe", normed, qkv_weights, preferred_element_type=jnp.float32
     ).astype(jnp.bfloat16)
     edges = rms_rows(jnp.concatenate([low_edge, high_edge], axis=1))
     keyval_edges = jnp.einsum(
         "sbd,de->sbe", edges, kv_weights, preferred_element_type=jnp.float32
     ).astype(jnp.bfloat16)
-    keyval = jnp.concatenate(
-        [keyval_edges[:, :half_span], keyval_mid, keyval_edges[:, half_span:]], axis=1
-    )
     key_span = bin_dev + 2 * half_span
-    kwin = QBLOCK + WINDOW
     key_cols = first_bin - half_span + jnp.arange(key_span, dtype=jnp.int32)
     col_ok = (key_cols[None, :] >= 0) & (key_cols[None, :] < my_counts[:, None])
     col_bias = jnp.where(col_ok, my_bias, masked_score)
-    windows = jnp.stack(
-        [col_bias[:, b * QBLOCK : b * QBLOCK + kwin] for b in range(bin_dev // QBLOCK)], axis=1
-    )
-    offset = (
-        jnp.arange(kwin, dtype=jnp.int32)[None, :] - jnp.arange(QBLOCK, dtype=jnp.int32)[:, None]
-    )
-    band = (offset >= 0) & (offset <= WINDOW)
-    full_bias = jnp.where(band[None, None], windows[:, :, None, :], masked_score)
-    context = band_attention(query_enc, keyval, full_bias)
+    qblocks = bin_dev // QBLOCK
+    block_ix = jnp.arange(qblocks, dtype=jnp.int32)[:, None, None]
+    query_local = block_ix * QBLOCK + jnp.arange(QBLOCK, dtype=jnp.int32)[None, :, None]
+    key_mid = half_span + jnp.arange(bin_dev, dtype=jnp.int32)[None, None, :]
+    key_edge = jnp.arange(half_span, dtype=jnp.int32)[None, None, :] + block_ix * (
+        key_span - half_span
+    )
+    band_mid = (key_mid - query_local >= 0) & (key_mid - query_local <= WINDOW)
+    band_edge = (key_edge - query_local >= 0) & (key_edge - query_local <= WINDOW)
+    col_mid = col_bias[:, half_span : half_span + bin_dev]
+    col_edge = col_bias.reshape(spec_dev, key_span // half_span, half_span)[:, :: qblocks + 1]
+    bias_mid = jnp.where(band_mid[None], col_mid[:, None, None, :], masked_score)
+    bias_edge = jnp.where(band_edge[None], col_edge[:, :, None, :], masked_score)
+    context = band_attention(qkv, keyval_edges, bias_mid, bias_edge)
 
     query_rows = first_bin + jnp.arange(bin_dev, dtype=jnp.int32)
     attended = jnp.einsum("sbd,de->sbe", context, enc_out, preferred_element_type=jnp.float32)

time: 201 us -> 198 us (0.985)
  waiting for transfers between devices: 45.2 us -> 49.7 us
  local copies, waits for them, and re-layouts: 9.73 us -> 6.29 us
  other arithmetic: 14.5 us -> 11.2 us
    ppermute x1, waiting for transfers between devices: 0.01 us -> 4.42 us  [per_device(): high_edge = lax.ppermute(spectra[:, :half_span], 'seq', backward)]
    concatenate x1 -> x0, other arithmetic: 3.96 us -> none  [per_device(): jnp.concatenate([keyval_edges[:, :half_span], keyval_mid, keyval_edges[:,...]
    dot_general x2 -> x1, matrix products: 13.5 us -> 13 us  [per_device(): jnp.einsum('sbd,de->sbe', normed, qkv_weights, preferred_element_type=jnp...]
  transfers between devices with their start and end apart: 4 -> 4, of which waited for: 2 -> 3; matrix products, arithmetic and copies ran while one was open for 14% -> 12% of each run, Pallas kernels for 0% -> 0%
where the time goes in v9:
time: 198 us; the launch traced here: 197 us
  waiting for transfers between devices  49.7 us (25%)
  matrix products  39.8 us (20%)
  Pallas kernels  33.9 us (17%)
  blocking collectives  28.7 us (14%)
  between operations  14.3 us (7%)
  starting transfers between devices  13.4 us (7%)
  other arithmetic  11.2 us (6%)
  local copies, waits for them, and re-layouts  6.29 us (3%)
    reduce_scatter x1, waiting for transfers between devices, per_device(): lax.psum_scatter(partial_sums.astype(jnp.bfloat16), 'head', scatter_dimen...  35.6 us
    pallas_call x1, Pallas kernels, band_attention(): pl.pallas_call(band_kernel, out_shape=jax.ShapeDtypeStruct((spec_dev, bin...  29.6 us
    all_to_all x1, blocking collectives, per_device(): dec_context = lax.all_to_all(context_one, 'seq', 0, 0, tiled=True)  14.4 us
    all_gather x1, blocking collectives, per_device(): spectra_all = lax.all_gather(pooled, 'head', axis=0, tiled=True)  14.3 us
    dot_general x1, matrix products, per_device(): jnp.einsum('sbd,de->sbe', normed, qkv_weights, preferred_element_type=jnp...  13 us
    all_to_all x1, waiting for transfers between devices, per_device(): received = lax.all_to_all(payload, 'seq', 0, 1, tiled=True)  9.62 us
    dot_general x1, matrix products, per_device(): jnp.einsum('sbd,de->sbe', edges, kv_weights, preferred_element_type=jnp.f...  8.04 us
    all_to_all x1, starting transfers between devices, per_device(): received = lax.all_to_all(payload, 'seq', 0, 1, tiled=True)  7.65 us
  transfers between devices with their start and end apart: 4, of which 3 were waited for; matrix products, arithmetic and copies ran while one was open for 12% of the time, Pallas kernels for 0%

profile of v9, /device:TPU:0, one launch (start us, length us, event | category | flops | bytes accessed | tf_op | source)
XLA Modules:
  0.0 197.3 jit_solution(14466333959690847560)
XLA Ops:
  7.2 0.0 copy-start
  7.2 0.0 copy-start.9
  7.2 0.0 copy-start.3
  7.2 0.0 copy-start.4
  7.2 0.0 copy-start.2
  7.2 3.2 %fusion.52 = (bf16[2,256,1024]{2,1,0:T(8,128)(2,1)}, bf16[2,256,1024]{2,1,0:T(8,128)(2,1)}) fusion(bf16[2,512,1024]{2,1,0:T(8,128)(2,1)} %param.15), kind=kLoop, calls=%fused_computation.97 | loop fusion | bytes 4194304 | tf_op jit(solution)/shard_map/slice | solution.py:167
  10.4 4.4 %collective-permute-start = (bf16[2,256,1024]{2,1,0:T(8,128)(2,1)}, bf16[2,256,1024]{2,1,0:T(8,128)(2,1)}, u32[]{:S(2)}, u32[]{:S(2)}) collective-permute-start(bf16[2,256,1024]{2,1,0:T(8,128)(2,1)} %get-tuple-element.14), channel_id=1, source_target_pairs={{0,8},{8,16},{16,24},{24,32},{32,40},{40,48},{48,56},{56,64},{64,7... | collective-permute-start | bytes 3145736 | tf_op jit(solution)/shard_map/ppermute | solution.py:167
  14.9 1.3 collective-permute-start.1
  16.2 0.0 copy-done.9
  16.2 0.1 dynamic_slice.15
  16.3 0.0 copy-done.3
  16.3 0.1 and_select_fusion
  16.5 2.1 %fusion.8 = f32[2,512]{1,0:T(2,128)S(1)} fusion(bf16[2,512,1024]{2,1,0:T(8,128)(2,1)} %param.15), kind=kLoop, calls=%fused_computation.16 | loop fusion | flops 3144704 | bytes 2101248 | tf_op jit(solution)/shard_map/reduce_sum | solution.py:23
  18.5 0.1 dynamic-slice_reduce_fusion
  18.6 0.6 dynamic_slice.18
  19.3 0.1 iota_add_fusion.1
  19.3 0.2 fusion.41
  19.5 0.3 fusion.35
  19.9 0.1 broadcast_compare_fusion.1
  19.9 0.0 copy-done.4
  19.9 0.0 copy-done.2
  20.0 0.2 fusion.37
  20.1 0.1 reshape.294
  20.2 1.2 broadcast_select_fusion.1.be_ref
  21.4 1.6 broadcast_select_fusion.bm_ref
  23.0 0.1 reduce_max.11
  23.1 1.2 compare_select_fusion.2.b_ref
  24.3 0.0 copy-start.5
  24.3 0.0 copy-start.6
  24.3 13.0 %fusion.5.q_ref.km_ref.vm_ref = bf16[2,512,3072]{2,1,0:T(8,128)(2,1)} fusion(bf16[1024,1024]{1,0:T(8,128)(2,1)} %param.20, bf16[1024,1024]{1,0:T(8,128)(2,1)} %param.19, bf16[1024,1024]{1,0:T(8,128)(2,1)} %param.18, bf16[2,512,1024]{2,1,0:T(8,128)(2,1)} %param.15, f32[2,512]{1,0:T(2,128)S(1)} %add_rsqrt_fusion.2), kind=kOutput, calls=%fused_computation.11 | convolution fusion | flops 6467616768 | bytes 14684160 | tf_op jit(solution)/shard_map/sbd,de->sbe/dot_general | solution.py:171
  37.3 0.0 collective-permute-done
  37.3 4.4 %collective-permute-done.1 = bf16[2,256,1024]{2,1,0:T(8,128)(2,1)} collective-permute-done((bf16[2,256,1024]{2,1,0:T(8,128)(2,1)}, bf16[2,256,1024]{2,1,0:T(8,128)(2,1)}, u32[]{:S(2)}, u32[]{:S(2)}) %collective-permute-start.1) | collective-permute-done | bytes 1048608 | tf_op jit(solution)/shard_map/ppermute | solution.py:168
  41.7 2.0 %fusion.6 = f32[2,512]{1,0:T(2,128)S(1)} fusion(bf16[2,256,1024]{2,1,0:T(8,128)(2,1)} %collective-permute-done.1, bf16[2,256,1024]{2,1,0:T(8,128)(2,1)} %collective-permute-done), kind=kLoop, calls=%fused_computation.14 | loop fusion | flops 6290432 | bytes 2101248 | tf_op jit(solution)/shard_map/reduce_sum | solution.py:23
  43.7 0.0 copy-done.5
  43.8 0.0 copy-done.6
  43.8 8.0 %fusion.16.ke_ref.ve_ref = bf16[2,512,2048]{2,1,0:T(8,128)(2,1)} fusion(bf16[1024,1024]{1,0:T(8,128)(2,1)S(1)} %copy-done.5, bf16[1024,1024]{1,0:T(8,128)(2,1)S(1)} %copy-done.6, f32[2,512]{1,0:T(2,128)S(1)} %add_rsqrt_fusion.1, bf16[2,256,1024]{2,1,0:T(8,128)(2,1)} %collective-permute-done.1, bf16[2,256,1024]{2,1,0:T(8,128)(2,1)} %collective-permute-done), kind=kOutput, calls=%fused_computation.26 | convolution fusion | flops 4311744512 | bytes 10489856 | tf_op jit(solution)/shard_map/sbd,de->sbe/dot_general | solution.py:175
  51.8 29.6 %shard_map.140 = bf16[2,512,1024]{2,1,0:T(8,128)(2,1)} custom-call(bf16[2,512,3072]{2,1,0:T(8,128)(2,1)} %fusion.5.q_ref.km_ref.vm_ref, bf16[2,512,3072]{2,1,0:T(8,128)(2,1)} %fusion.5.q_ref.km_ref.vm_ref, bf16[2,512,3072]{2,1,0:T(8,128)(2,1)} %fusion.5.q_ref.km_ref.vm_ref, bf16[2,512,2048]{2,1,0:T(8,128)(2,1)} %fusion.16.ke_ref.ve_ref, ...), custom_call_target="tpu_custom_call" | custom-call | flops 6442450944 | bytes 13631488 | tf_op jit(solution)/shard_map/pallas_call | solution.py:75
  81.4 0.0 copy-done
  81.4 0.0 copy-start.7
  81.4 0.0 copy-start.8
  81.5 6.3 %convert_reduce_fusion = (f32[2,16,1024]{2,1,0:T(8,128)S(1)}, bf16[2,512,1024]{2,1,0:T(8,128)(2,1)}) fusion(bf16[2,512,1024]{2,1,0:T(8,128)(2,1)} %shard_map.140, bf16[1024,1024]{1,0:T(8,128)(2,1)S(1)} %copy-done, bf16[2,512,1024]{2,1,0:T(8,128)(2,1)} %param.15, pred[2,512]{1,0:T(4,128)(4,1)S(1)} %broadcast_compare_fusion.1), kind=kOutput, calls=%fused_computation.24 | convolution fusion | flops 2153742336 | bytes 8520704 | tf_op jit(solution)/shard_map/sbd,de->sbe/dot_general | solution.py:198
  87.8 14.3 %all_gather.3 = bf16[16,16,1024]{2,1,0:T(8,128)(2,1)S(1)} all-gather(bf16[2,16,1024]{2,1,0:T(8,128)(2,1)S(1)} %multiply_convert_fusion), channel_id=1, replica_groups=mesh['seq'=16,'head'=8] {'head'}, dimensions={0}, use_global_device_ids=true | all-gather | bytes 589824 | tf_op jit(solution)/shard_map/all_gather | solution.py:206
  102.1 0.2 fusion.33
  102.3 0.0 copy-done.7
  102.3 0.0 copy-done.8
  102.3 0.8 fusion.28
  103.1 0.9 fusion.36
  103.9 7.6 %all-to-all-start = ((bf16[16,16,1152]{2,1,0:T(8,128)(2,1)}), bf16[16,16,1152]{2,1,0:T(8,128)(2,1)S(1)}, u32[]{:S(2)}, u32[]{:S(2)}) async-start(bf16[16,16,1152]{2,1,0:T(8,128)(2,1)} %fusion.36), calls=%async_computation | async-start | bytes 1179648 | tf_op jit(solution)/shard_map/all_to_all | solution.py:217
  111.6 0.0 reduce-scatter.2.cloned.1.call-start
  111.7 3.1 %convolution_convert_fusion.2 = bf16[28,512]{1,0:T(8,128)(2,1)S(1)} fusion(bf16[4096,512]{1,0:T(8,128)(2,1)} %param.24, bf16[28,4096]{1,0:T(8,128)(2,1)S(1)} %copy-done.2, f32[28]{0:T(128)S(1)} %add_rsqrt_fusion.3), kind=kOutput, calls=%fused_computation.47 | convolution fusion | flops 117798912 | bytes 4452464 | tf_op jit(solution)/shard_map/vd,de->ve/dot_general | solution.py:239
  114.7 9.6 %all-to-all-done = bf16[16,16,1152]{2,1,0:T(8,128)(2,1)S(1)} async-done(((bf16[16,16,1152]{2,1,0:T(8,128)(2,1)}), bf16[16,16,1152]{2,1,0:T(8,128)(2,1)S(1)}, u32[]{:S(2)}, u32[]{:S(2)}) %all-to-all-start) | async-done | bytes 589856 | tf_op jit(solution)/shard_map/all_to_all | solution.py:217
  124.3 0.0 copy-start.1
  124.3 0.1 reshape.299
  124.5 0.1 reshape.298
  124.6 2.0 gather_fusion
  126.5 0.9 bitcast_select_fusion.q_ref
  127.5 0.0 copy-done.1
  127.5 4.2 %shard_map.141 = bf16[1,512,512]{2,1,0:T(8,128)(2,1)} custom-call(bf16[1,512,512]{2,1,0:T(8,128)(2,1)} %bitcast_select_fusion.q_ref, bf16[1,256,1152]{2,1,0:T(8,128)(2,1)} %bitcast.44, bf16[1,256,1152]{2,1,0:T(8,128)(2,1)} %bitcast.45, f32[1,1,256]{2,1,0:T(1,128)} %compare_select_fusion.2.b_ref), custom_call_target="tpu_custom_call" | custom-call | flops 268435456 | bytes 1572864 | tf_op jit(solution)/shard_map/pallas_call | solution.py:116
  131.7 14.4 %all_to_all.17 = bf16[16,32,512]{2,1,0:T(8,128)(2,1)S(1)} all-to-all(bf16[16,32,512]{2,1,0:T(8,128)(2,1)} %bitcast.46), channel_id=1, replica_groups=mesh['seq'=16,'head'=8] {'seq'}, dimensions={0} | all-to-all | bytes 1048576 | tf_op jit(solution)/shard_map/all_to_all | solution.py:246
  146.1 6.5 %convolution_convert_fusion = bf16[16,32,4096]{2,1,0:T(8,128)(2,1)} fusion(bf16[16,32,512]{2,1,0:T(8,128)(2,1)S(1)} %all_to_all.17, bf16[512,4096]{1,0:T(8,128)(2,1)} %param.27), kind=kOutput, calls=%fused_computation.10 | convolution fusion | flops 2149580800 | bytes 8912896 | tf_op jit(solution)/shard_map/ste,ed->std/dot_general | solution.py:247
  152.6 0.0 reduce-scatter.2.cloned.1.call-update
  152.6 35.6 %reduce-scatter.2.cloned.1.call-done = bf16[16,32,512]{2,1,0:T(8,128)(2,1)} async-done(((bf16[16,32,4096]{2,1,0:T(8,128)(2,1)}), bf16[16,32,512]{2,1,0:T(8,128)(2,1)}) %reduce-scatter.2.cloned.1.call-update) | async-done | bytes 524304 | tf_op jit(solution)/shard_map/reduce_scatter | solution.py:250
  188.3 2.2 %fusion.31 = bf16[16,32,512]{2,1,0:T(8,128)(2,1)} fusion(bf16[16,32,512]{2,1,0:T(8,128)(2,1)} %reduce-scatter.2.cloned.1.call-done, s32[16,32]{1,0:T(8,128)S(1)} %copy-done.4, bf16[28,4096]{1,0:T(8,128)(2,1)S(1)} %copy-done.2, s32[]{:T(128)S(6)} %select_n.76), kind=kOutput, calls=%fused_computation.44 | convolution fusion | flops 16005120 | bytes 1089540 | tf_op jit(solution)/shard_map/stv,vd->std/dot_general | solution.py:236
  (21 shorter events, 0.2 us)
Async XLA Ops:
  7.2 74.3 %copy-start = (bf16[1024,1024]{1,0:T(8,128)(2,1)S(1)}, bf16[1024,1024]{1,0:T(8,128)(2,1)}, u32[]{:S(2)}) copy-start(bf16[1024,1024]{1,0:T(8,128)(2,1)} %param.21) | copy-start | bytes 6291460
  7.2 9.1 %copy-start.9 = (s32[16]{0:T(128)S(1)}, s32[16]{0:T(128)}, u32[]{:S(2)}) copy-start(s32[16]{0:T(128)} %param.17) | copy-start | bytes 196
  7.2 9.1 %copy-start.3 = (f32[16,8192]{1,0:T(8,128)S(1)}, f32[16,8192]{1,0:T(8,128)}, u32[]{:S(2)}) copy-start(f32[16,8192]{1,0:T(8,128)} %param.16) | copy-start | bytes 1572868
  7.2 12.7 %copy-start.4 = (s32[16,32]{1,0:T(8,128)S(1)}, s32[16,32]{1,0:T(8,128)}, u32[]{:S(2)}) copy-start(s32[16,32]{1,0:T(8,128)} %param.22) | copy-start | bytes 6148
  7.2 12.7 %copy-start.2 = (bf16[28,4096]{1,0:T(8,128)(2,1)S(1)}, bf16[28,4096]{1,0:T(8,128)(2,1)}, u32[]{:S(2)}) copy-start(bf16[28,4096]{1,0:T(8,128)(2,1)} %param.23) | copy-start | bytes 688132
  10.4 26.8 %collective-permute-start = (bf16[2,256,1024]{2,1,0:T(8,128)(2,1)}, bf16[2,256,1024]{2,1,0:T(8,128)(2,1)}, u32[]{:S(2)}, u32[]{:S(2)}) collective-permute-start(bf16[2,256,1024]{2,1,0:T(8,128)(2,1)} %get-tuple-element.14), channel_id=1, source_target_pairs={{0,8},{8,16},{16,24},{24,32},{32,40},{40,48},{48,56},{56,64},{64,7... | collective-permute-start | bytes 3145736 | tf_op jit(solution)/shard_map/ppermute | solution.py:167
  14.9 26.8 %collective-permute-start.1 = (bf16[2,256,1024]{2,1,0:T(8,128)(2,1)}, bf16[2,256,1024]{2,1,0:T(8,128)(2,1)}, u32[]{:S(2)}, u32[]{:S(2)}) collective-permute-start(bf16[2,256,1024]{2,1,0:T(8,128)(2,1)} %get-tuple-element.15), channel_id=1, source_target_pairs={{8,0},{16,8},{24,16},{32,24},{40,32},{48,40},{56,48},{64,56},{72,6... | collective-permute-start | bytes 3145736 | tf_op jit(solution)/shard_map/ppermute | solution.py:168
  24.3 19.5 %copy-start.5 = (bf16[1024,1024]{1,0:T(8,128)(2,1)S(1)}, bf16[1024,1024]{1,0:T(8,128)(2,1)}, u32[]{:S(2)}) copy-start(bf16[1024,1024]{1,0:T(8,128)(2,1)} %param.20) | copy-start | bytes 6291460
  24.3 19.5 %copy-start.6 = (bf16[1024,1024]{1,0:T(8,128)(2,1)S(1)}, bf16[1024,1024]{1,0:T(8,128)(2,1)}, u32[]{:S(2)}) copy-start(bf16[1024,1024]{1,0:T(8,128)(2,1)} %param.19) | copy-start | bytes 6291460
  81.4 20.9 %copy-start.7 = (bf16[1024,512]{1,0:T(8,128)(2,1)S(1)}, bf16[1024,512]{1,0:T(8,128)(2,1)}, u32[]{:S(2)}) copy-start(bf16[1024,512]{1,0:T(8,128)(2,1)} %param.26) | copy-start | bytes 3145732
  81.4 20.9 %copy-start.8 = (bf16[1024,512]{1,0:T(8,128)(2,1)S(1)}, bf16[1024,512]{1,0:T(8,128)(2,1)}, u32[]{:S(2)}) copy-start(bf16[1024,512]{1,0:T(8,128)(2,1)} %param.25) | copy-start | bytes 3145732
  103.9 20.4 %all-to-all-start = ((bf16[16,16,1152]{2,1,0:T(8,128)(2,1)}), bf16[16,16,1152]{2,1,0:T(8,128)(2,1)S(1)}, u32[]{:S(2)}, u32[]{:S(2)}) async-start(bf16[16,16,1152]{2,1,0:T(8,128)(2,1)} %fusion.36), calls=%async_computation | async-start | bytes 1179648 | tf_op jit(solution)/shard_map/all_to_all | solution.py:217
  111.6 76.7 %reduce-scatter.2.cloned.1.call-start = ((), (), s32[]{:S(2)}) async-start(), calls=%async_computation.3 | async-start | bytes 4718592 | tf_op jit(solution)/shard_map/reduce_scatter | solution.py:250
  124.3 3.1 %copy-start.1 = (bf16[16,16,1152]{2,1,0:T(8,128)(2,1)}, bf16[16,16,1152]{2,1,0:T(8,128)(2,1)S(1)}, u32[]{:S(2)}) copy-start(bf16[16,16,1152]{2,1,0:T(8,128)(2,1)S(1)} %all-to-all-done) | copy-start | bytes 1769476
Sparse Core Ops, SparseCore 0:
  152.7 35.4 reduce-scatter.1

commit v10 on v9

--- a/solution.py
+++ b/solution.py
@@ -10,7 +10,7 @@
 POOL = 32
 HD = 32
 QBLOCK = 256
-HGROUP = 512
+HGROUP = 1024
 DEC_SCALE = 128 ** (-0.5)
 
 
@@ -30,7 +30,10 @@
     return (weights / jnp.sum(weights, axis=-1, keepdims=True)).astype(jnp.bfloat16)
 
 
-def band_kernel(q_ref, km_ref, vm_ref, ke_ref, ve_ref, bm_ref, be_ref, o_ref):
+def band_kernel(
+    q_ref, km_ref, vm_ref, ke_ref, ve_ref, bm_ref, be_ref, eo_ref, sp_ref, rv_ref, pm_ref,
+    e_ref, p_ref, ctx
+):
     bias_mid = bm_ref[0, 0]
     bias_edge = be_ref[0, 0]
     lane = lax.broadcasted_iota(jnp.int32, (1, 128), 1)
@@ -62,41 +65,63 @@
             )
             pv = pv / total
             out = pv if out is None else jnp.where(low, out, pv)
-        o_ref[0, :, cols] = out.astype(o_ref.dtype)
-
-
-def band_attention(qkv, keyval_edges, bias_mid, bias_edge):
+        ctx[:, cols] = out.astype(jnp.bfloat16)
+    attended = jnp.dot(ctx[...], eo_ref[...], preferred_element_type=jnp.float32)
+    rows = sp_ref[0].astype(jnp.float32) + attended
+    encoded = jnp.where(rv_ref[0] > 0, rows, 0.0).astype(jnp.bfloat16)
+    e_ref[0] = encoded
+    p_ref[0] = jnp.dot(pm_ref[...], encoded, preferred_element_type=jnp.float32)
+
+
+def band_attention(qkv, keyval_edges, bias_mid, bias_edge, enc_out, spectra, row_valid):
     spec_dev, bin_dev, triple = qkv.shape
     width = triple // 3
     edge_rows = keyval_edges.shape[1] // 2
     groups = width // HGROUP
     qblocks = bin_dev // QBLOCK
     kwin = bin_dev + edge_rows
+    pooled_rows = QBLOCK // POOL
+    pool_matrix = (
+        jnp.arange(QBLOCK, dtype=jnp.int32)[None, :] // POOL
+        == jnp.arange(pooled_rows, dtype=jnp.int32)[:, None]
+    ).astype(jnp.bfloat16) * (1.0 / POOL)
     return pl.pallas_call(
         band_kernel,
-        out_shape=jax.ShapeDtypeStruct((spec_dev, bin_dev, width), jnp.bfloat16),
-        grid=(spec_dev, groups, qblocks),
+        out_shape=(
+            jax.ShapeDtypeStruct((spec_dev, bin_dev, width), jnp.bfloat16),
+            jax.ShapeDtypeStruct((spec_dev, bin_dev // POOL, width), jnp.float32),
+        ),
+        grid=(spec_dev, qblocks),
         in_specs=[
-            pl.BlockSpec((1, QBLOCK, HGROUP), lambda s, g, b: (s, b, g)),
-            pl.BlockSpec((1, bin_dev, HGROUP), lambda s, g, b: (s, 0, groups + g)),
-            pl.BlockSpec((1, bin_dev, HGROUP), lambda s, g, b: (s, 0, 2 * groups + g)),
-            pl.BlockSpec((1, edge_rows, HGROUP), lambda s, g, b: (s, b, g)),
-            pl.BlockSpec((1, edge_rows, HGROUP), lambda s, g, b: (s, b, groups + g)),
-            pl.BlockSpec((1, 1, QBLOCK, bin_dev), lambda s, g, b: (s, b, 0, 0)),
-            pl.BlockSpec((1, 1, QBLOCK, edge_rows), lambda s, g, b: (s, b, 0, 0)),
+            pl.BlockSpec((1, QBLOCK, HGROUP), lambda s, b: (s, b, 0)),
+            pl.BlockSpec((1, bin_dev, HGROUP), lambda s, b: (s, 0, groups)),
+            pl.BlockSpec((1, bin_dev, HGROUP), lambda s, b: (s, 0, 2 * groups)),
+            pl.BlockSpec((1, edge_rows, HGROUP), lambda s, b: (s, b, 0)),
+            pl.BlockSpec((1, edge_rows, HGROUP), lambda s, b: (s, b, groups)),
+            pl.BlockSpec((1, 1, QBLOCK, bin_dev), lambda s, b: (s, b, 0, 0)),
+            pl.BlockSpec((1, 1, QBLOCK, edge_rows), lambda s, b: (s, b, 0, 0)),
+            pl.BlockSpec((width, width), lambda s, b: (0, 0)),
+            pl.BlockSpec((1, QBLOCK, width), lambda s, b: (s, b, 0)),
+            pl.BlockSpec((1, QBLOCK, 1), lambda s, b: (s, b, 0)),
+            pl.BlockSpec((pooled_rows, QBLOCK), lambda s, b: (0, 0)),
         ],
-        out_specs=pl.BlockSpec((1, QBLOCK, HGROUP), lambda s, g, b: (s, b, g)),
-        compiler_params=pltpu.CompilerParams(
-            dimension_semantics=("arbitrary", "arbitrary", "arbitrary")
-        ),
+        out_specs=(
+            pl.BlockSpec((1, QBLOCK, width), lambda s, b: (s, b, 0)),
+            pl.BlockSpec((1, pooled_rows, width), lambda s, b: (s, b, 0)),
+        ),
+        scratch_shapes=[pltpu.VMEM((QBLOCK, width), jnp.bfloat16)],
+        compiler_params=pltpu.CompilerParams(dimension_semantics=("arbitrary", "arbitrary")),
         cost_estimate=pl.CostEstimate(
-            flops=spec_dev * bin_dev * kwin * width * 8,
+            flops=spec_dev * bin_dev * (kwin * width * 8 + width * width * 2),
             transcendentals=spec_dev * bin_dev * kwin * HE,
-            bytes_accessed=spec_dev * bin_dev * width * 10
-            + (bias_mid.size + bias_edge.size) * 4,
-        ),
-    )(qkv, qkv, qkv, keyval_edges, keyval_edges, bias_mid, bias_edge)
-
+            bytes_accessed=spec_dev * bin_dev * width * 14
+            + (bias_mid.size + bias_edge.size) * 4
+            + width * width * 2,
+        ),
+    )(
+        qkv, qkv, qkv, keyval_edges, keyval_edges, bias_mid, bias_edge,
+        enc_out, spectra, row_valid, pool_matrix,
+    )
 
 def cross_kernel(q_ref, k_ref, v_ref, b_ref, o_ref):
     s = lax.dot_general(
@@ -192,17 +217,12 @@
     col_edge = col_bias.reshape(spec_dev, key_span // half_span, half_span)[:, :: qblocks + 1]
     bias_mid = jnp.where(band_mid[None], col_mid[:, None, None, :], masked_score)
     bias_edge = jnp.where(band_edge[None], col_edge[:, :, None, :], masked_score)
-    context = band_attention(qkv, keyval_edges, bias_mid, bias_edge)
-
     query_rows = first_bin + jnp.arange(bin_dev, dtype=jnp.int32)
-    attended = jnp.einsum("sbd,de->sbe", context, enc_out, preferred_element_type=jnp.float32)
-    valid_rows = (query_rows[None, :] < my_counts[:, None])[:, :, None]
-    encoded = jnp.where(valid_rows, spectra.astype(jnp.float32) + attended, 0.0).astype(
-        jnp.bfloat16
-    )
-    pooled = jnp.mean(
-        encoded.astype(jnp.float32).reshape(spec_dev, bin_dev // POOL, POOL, model_width), axis=2
-    ).astype(jnp.bfloat16)
+    row_valid = (query_rows[None, :] < my_counts[:, None]).astype(jnp.int32)[:, :, None]
+    encoded, pooled_sums = band_attention(
+        qkv, keyval_edges, bias_mid, bias_edge, enc_out, spectra, row_valid
+    )
+    pooled = pooled_sums.astype(jnp.bfloat16)
     spectra_all = lax.all_gather(pooled, "head", axis=0, tiled=True)
     mem_weights = jnp.concatenate([mem_key, mem_value], axis=1)
     local_width = mem_key.shape[1]

time: 198 us -> 198 us (level)
  matrix products: 39.8 us -> 34.2 us
  Pallas kernels: 33.9 us -> 37.6 us
    dot_general x1 -> x0, matrix products: 6.33 us -> none  [per_device(): jnp.einsum('sbd,de->sbe', context, enc_out, preferred_element_type=jnp.fl...]
    pallas_call x1, Pallas kernels: 29.6 us -> 33.4 us  [band_attention(): pl.pallas_call(band_kernel, out_shape=(jax.ShapeDtypeStruct((spec_dev, bi...]
where the time goes in v10:
time: 198 us; the launch traced here: 197 us
  waiting for transfers between devices  50.3 us (25%)
  Pallas kernels  37.6 us (19%)
  matrix products  34.2 us (17%)
  blocking collectives  28.7 us (14%)
  between operations  14.3 us (7%)
  starting transfers between devices  13.4 us (7%)
  other arithmetic  11.9 us (6%)
  local copies, waits for them, and re-layouts  6.59 us (3%)
    reduce_scatter x1, waiting for transfers between devices, per_device(): lax.psum_scatter(partial_sums.astype(jnp.bfloat16), 'head', scatter_dimen...  35.6 us
    pallas_call x1, Pallas kernels, band_attention(): pl.pallas_call(band_kernel, out_shape=(jax.ShapeDtypeStruct((spec_dev, bi...  33.4 us
    all_to_all x1, blocking collectives, per_device(): dec_context = lax.all_to_all(context_one, 'seq', 0, 0, tiled=True)  14.4 us
    all_gather x1, blocking collectives, per_device(): spectra_all = lax.all_gather(pooled, 'head', axis=0, tiled=True)  14.3 us
    dot_general x1, matrix products, per_device(): jnp.einsum('sbd,de->sbe', normed, qkv_weights, preferred_element_type=jnp...  12.4 us
    all_to_all x1, waiting for transfers between devices, per_device(): received = lax.all_to_all(payload, 'seq', 0, 1, tiled=True)  9.63 us
    dot_general x1, matrix products, per_device(): jnp.einsum('sbd,de->sbe', edges, kv_weights, preferred_element_type=jnp.f...  8.1 us
    all_to_all x1, starting transfers between devices, per_device(): received = lax.all_to_all(payload, 'seq', 0, 1, tiled=True)  7.63 us
  transfers between devices with their start and end apart: 4, of which 3 were waited for; matrix products, arithmetic and copies ran while one was open for 12% of the time, Pallas kernels for 0%

profile of v10, /device:TPU:0, one launch (start us, length us, event | category | flops | bytes accessed | tf_op | source)
XLA Modules:
  0.0 197.1 jit_solution(4095019800117292506)
XLA Ops:
  7.2 0.0 copy-start
  7.2 0.0 copy-start.8
  7.2 0.0 copy-start.3
  7.2 0.0 copy-start.4
  7.2 0.0 copy-start.2
  7.2 3.2 %fusion.47 = (bf16[2,256,1024]{2,1,0:T(8,128)(2,1)}, bf16[2,256,1024]{2,1,0:T(8,128)(2,1)}) fusion(bf16[2,512,1024]{2,1,0:T(8,128)(2,1)} %sp_ref.1), kind=kLoop, calls=%fused_computation.96 | loop fusion | bytes 4194304 | tf_op jit(solution)/shard_map/slice | solution.py:192
  10.4 4.4 %collective-permute-start = (bf16[2,256,1024]{2,1,0:T(8,128)(2,1)}, bf16[2,256,1024]{2,1,0:T(8,128)(2,1)}, u32[]{:S(2)}, u32[]{:S(2)}) collective-permute-start(bf16[2,256,1024]{2,1,0:T(8,128)(2,1)} %get-tuple-element.18), channel_id=1, source_target_pairs={{0,8},{8,16},{16,24},{24,32},{32,40},{40,48},{48,56},{56,64},{64,7... | collective-permute-start | bytes 3145736 | tf_op jit(solution)/shard_map/ppermute | solution.py:192
  14.9 1.3 collective-permute-start.1
  16.2 0.0 copy-done.8
  16.2 0.1 dynamic_slice.15
  16.3 0.0 copy-done.3
  16.3 0.1 and_select_fusion
  16.5 0.0 copy-done
  16.5 0.5 fusion.6
  17.0 0.1 dynamic-slice_reduce_fusion
  17.1 0.7 dynamic_slice.18
  17.8 0.1 iota_add_fusion.2
  17.8 0.2 fusion.35
  18.0 0.3 fusion.29
  18.3 0.9 compare_convert_fusion.rv_ref
  19.3 0.6 fusion.41.pm_ref
  19.9 0.0 copy-done.4
  19.9 0.0 copy-done.2
  19.9 0.2 fusion.31
  20.1 0.1 reshape.341
  20.2 1.1 broadcast_select_fusion.1.be_ref
  21.3 1.6 broadcast_select_fusion.bm_ref
  22.9 0.1 reduce_max.11
  23.0 1.3 compare_select_fusion.2.b_ref
  24.2 0.0 copy-start.5
  24.2 0.0 copy-start.6
  24.2 12.4 %fusion.5.q_ref.km_ref.vm_ref = bf16[2,512,3072]{2,1,0:T(8,128)(2,1)} fusion(bf16[1024,1024]{1,0:T(8,128)(2,1)} %param.20, bf16[1024,1024]{1,0:T(8,128)(2,1)} %param.19, bf16[1024,1024]{1,0:T(8,128)(2,1)} %param.18, bf16[2,512,1024]{2,1,0:T(8,128)(2,1)S(1)} %copy-done, f32[2,512]{1,0:T(2,128)S(1)} %add_rsqrt_fusion.2), kind=kOutput, calls=%fused_computation.8 | convolution fusion | flops 6467616768 | bytes 14684160 | tf_op jit(solution)/shard_map/sbd,de->sbe/dot_general | solution.py:196
  36.6 0.0 collective-permute-done
  36.6 5.1 %collective-permute-done.1 = bf16[2,256,1024]{2,1,0:T(8,128)(2,1)} collective-permute-done((bf16[2,256,1024]{2,1,0:T(8,128)(2,1)}, bf16[2,256,1024]{2,1,0:T(8,128)(2,1)}, u32[]{:S(2)}, u32[]{:S(2)}) %collective-permute-start.1) | collective-permute-done | bytes 1048608 | tf_op jit(solution)/shard_map/ppermute | solution.py:193
  41.7 2.0 %fusion.8 = f32[2,512]{1,0:T(2,128)S(1)} fusion(bf16[2,256,1024]{2,1,0:T(8,128)(2,1)} %collective-permute-done.1, bf16[2,256,1024]{2,1,0:T(8,128)(2,1)} %collective-permute-done), kind=kLoop, calls=%fused_computation.15 | loop fusion | flops 6290432 | bytes 2101248 | tf_op jit(solution)/shard_map/reduce_sum | solution.py:23
  43.7 0.0 copy-done.5
  43.8 0.0 copy-done.6
  43.8 8.1 %fusion.14.ke_ref.ve_ref = bf16[2,512,2048]{2,1,0:T(8,128)(2,1)} fusion(bf16[1024,1024]{1,0:T(8,128)(2,1)S(1)} %copy-done.5, bf16[1024,1024]{1,0:T(8,128)(2,1)S(1)} %copy-done.6, f32[2,512]{1,0:T(2,128)S(1)} %add_rsqrt_fusion.1, bf16[2,256,1024]{2,1,0:T(8,128)(2,1)} %collective-permute-done.1, bf16[2,256,1024]{2,1,0:T(8,128)(2,1)} %collective-permute-done), kind=kOutput, calls=%fused_computation.22 | convolution fusion | flops 4311744512 | bytes 10489856 | tf_op jit(solution)/shard_map/sbd,de->sbe/dot_general | solution.py:200
  51.9 0.0 copy-start.7
  51.9 33.4 %shard_map.140 = (bf16[2,512,1024]{2,1,0:T(8,128)(2,1)}, f32[2,16,1024]{2,1,0:T(8,128)}) custom-call(bf16[2,512,3072]{2,1,0:T(8,128)(2,1)} %fusion.5.q_ref.km_ref.vm_ref, bf16[2,512,3072]{2,1,0:T(8,128)(2,1)} %fusion.5.q_ref.km_ref.vm_ref, bf16[2,512,3072]{2,1,0:T(8,128)(2,1)} %fusion.5.q_ref.km_ref.vm_ref, bf16[2,512,2048]{2,1,0:T(8,128)(2,1)} %fusion.14.ke_ref.ve_ref, ...), custom_call_target="tpu_custom_call" | custom-call | flops 8589934592 | bytes 19922944 | tf_op jit(solution)/shard_map/pallas_call | solution.py:88
  85.2 0.9 convert_element_type.103
  86.1 14.3 %all_gather.3 = bf16[16,16,1024]{2,1,0:T(8,128)(2,1)S(1)} all-gather(bf16[2,16,1024]{2,1,0:T(8,128)(2,1)S(1)} %convert_element_type.103), channel_id=1, replica_groups=mesh['seq'=16,'head'=8] {'head'}, dimensions={0}, use_global_device_ids=true | all-gather | bytes 589824 | tf_op jit(solution)/shard_map/all_gather | solution.py:226
  100.5 0.2 fusion.27
  100.6 0.0 copy-done.7
  100.6 2.0 %fusion.22 = bf16[16,16,1024]{2,1,0:T(8,128)(2,1)S(1)} fusion(bf16[1024,512]{1,0:T(8,128)(2,1)S(1)} %copy-done.7, bf16[1024,512]{1,0:T(8,128)(2,1)} %param.25, bf16[16,16,1024]{2,1,0:T(8,128)(2,1)S(1)} %all_gather.3, f32[16,16]{1,0:T(8,128)S(1)} %add_rsqrt_fusion), kind=kOutput, calls=%fused_computation.34 | convolution fusion | flops 542113792 | bytes 3146752 | tf_op jit(solution)/shard_map/spd,de->spe/dot_general | solution.py:229
  102.6 0.9 fusion.30
  103.5 7.6 %all-to-all-start = ((bf16[16,16,1152]{2,1,0:T(8,128)(2,1)}), bf16[16,16,1152]{2,1,0:T(8,128)(2,1)S(1)}, u32[]{:S(2)}, u32[]{:S(2)}) async-start(bf16[16,16,1152]{2,1,0:T(8,128)(2,1)} %fusion.30), calls=%async_computation | async-start | bytes 1179648 | tf_op jit(solution)/shard_map/all_to_all | solution.py:237
  111.1 0.0 reduce-scatter.2.cloned.1.call-start
  111.2 3.1 %convolution_convert_fusion.2 = bf16[28,512]{1,0:T(8,128)(2,1)S(1)} fusion(bf16[4096,512]{1,0:T(8,128)(2,1)} %param.24, bf16[28,4096]{1,0:T(8,128)(2,1)S(1)} %copy-done.2, f32[28]{0:T(128)S(1)} %add_rsqrt_fusion.3), kind=kOutput, calls=%fused_computation.41 | convolution fusion | flops 117798912 | bytes 4452464 | tf_op jit(solution)/shard_map/vd,de->ve/dot_general | solution.py:259
  114.3 9.6 %all-to-all-done = bf16[16,16,1152]{2,1,0:T(8,128)(2,1)S(1)} async-done(((bf16[16,16,1152]{2,1,0:T(8,128)(2,1)}), bf16[16,16,1152]{2,1,0:T(8,128)(2,1)S(1)}, u32[]{:S(2)}, u32[]{:S(2)}) %all-to-all-start) | async-done | bytes 589856 | tf_op jit(solution)/shard_map/all_to_all | solution.py:237
  123.9 0.0 copy-start.1
  123.9 0.1 reshape.344
  124.0 0.1 reshape.343
  124.1 2.2 %gather_fusion = bf16[512,512]{1,0:T(8,128)(2,1)S(1)} fusion(bf16[28,512]{1,0:T(8,128)(2,1)S(1)} %convolution_convert_fusion.2, s32[1024]{0:T(1024)S(1)} %pad_clamp_fusion), kind=kCustom, calls=%fused_computation | custom fusion | bytes 1050624 | tf_op jit(solution)/shard_map/jit(_take)/gather | solution.py:262
  126.3 0.9 bitcast_select_fusion.q_ref
  127.2 0.0 copy-done.1
  127.2 4.2 %shard_map.141 = bf16[1,512,512]{2,1,0:T(8,128)(2,1)} custom-call(bf16[1,512,512]{2,1,0:T(8,128)(2,1)} %bitcast_select_fusion.q_ref, bf16[1,256,1152]{2,1,0:T(8,128)(2,1)} %bitcast.33, bf16[1,256,1152]{2,1,0:T(8,128)(2,1)} %bitcast.34, f32[1,1,256]{2,1,0:T(1,128)} %compare_select_fusion.2.b_ref), custom_call_target="tpu_custom_call" | custom-call | flops 268435456 | bytes 1572864 | tf_op jit(solution)/shard_map/pallas_call | solution.py:141
  131.5 14.4 %all_to_all.17 = bf16[16,32,512]{2,1,0:T(8,128)(2,1)S(1)} all-to-all(bf16[16,32,512]{2,1,0:T(8,128)(2,1)} %bitcast.35), channel_id=1, replica_groups=mesh['seq'=16,'head'=8] {'seq'}, dimensions={0} | all-to-all | bytes 1048576 | tf_op jit(solution)/shard_map/all_to_all | solution.py:266
  145.9 6.5 %convolution_convert_fusion = bf16[16,32,4096]{2,1,0:T(8,128)(2,1)} fusion(bf16[16,32,512]{2,1,0:T(8,128)(2,1)S(1)} %all_to_all.17, bf16[512,4096]{1,0:T(8,128)(2,1)} %param.27), kind=kOutput, calls=%fused_computation.7 | convolution fusion | flops 2149580800 | bytes 8912896 | tf_op jit(solution)/shard_map/ste,ed->std/dot_general | solution.py:267
  152.4 0.0 reduce-scatter.2.cloned.1.call-update
  152.4 35.6 %reduce-scatter.2.cloned.1.call-done = bf16[16,32,512]{2,1,0:T(8,128)(2,1)} async-done(((bf16[16,32,4096]{2,1,0:T(8,128)(2,1)}), bf16[16,32,512]{2,1,0:T(8,128)(2,1)}) %reduce-scatter.2.cloned.1.call-update) | async-done | bytes 524304 | tf_op jit(solution)/shard_map/reduce_scatter | solution.py:270
  188.0 2.2 %fusion.25 = bf16[16,32,512]{2,1,0:T(8,128)(2,1)} fusion(bf16[16,32,512]{2,1,0:T(8,128)(2,1)} %reduce-scatter.2.cloned.1.call-done, s32[16,32]{1,0:T(8,128)S(1)} %copy-done.4, bf16[28,4096]{1,0:T(8,128)(2,1)S(1)} %copy-done.2, s32[]{:T(128)S(6)} %select_n.82), kind=kOutput, calls=%fused_computation.38 | convolution fusion | flops 16005120 | bytes 1089540 | tf_op jit(solution)/shard_map/stv,vd->std/dot_general | solution.py:256
  (21 shorter events, 0.2 us)
Async XLA Ops:
  7.2 9.3 %copy-start = (bf16[2,512,1024]{2,1,0:T(8,128)(2,1)S(1)}, bf16[2,512,1024]{2,1,0:T(8,128)(2,1)}, u32[]{:S(2)}) copy-start(bf16[2,512,1024]{2,1,0:T(8,128)(2,1)} %sp_ref.1) | copy-start | bytes 6291460
  7.2 9.1 %copy-start.8 = (s32[16]{0:T(128)S(1)}, s32[16]{0:T(128)}, u32[]{:S(2)}) copy-start(s32[16]{0:T(128)} %param.17) | copy-start | bytes 196
  7.2 9.1 %copy-start.3 = (f32[16,8192]{1,0:T(8,128)S(1)}, f32[16,8192]{1,0:T(8,128)}, u32[]{:S(2)}) copy-start(f32[16,8192]{1,0:T(8,128)} %param.16) | copy-start | bytes 1572868
  7.2 12.7 %copy-start.4 = (s32[16,32]{1,0:T(8,128)S(1)}, s32[16,32]{1,0:T(8,128)}, u32[]{:S(2)}) copy-start(s32[16,32]{1,0:T(8,128)} %param.22) | copy-start | bytes 6148
  7.2 12.7 %copy-start.2 = (bf16[28,4096]{1,0:T(8,128)(2,1)S(1)}, bf16[28,4096]{1,0:T(8,128)(2,1)}, u32[]{:S(2)}) copy-start(bf16[28,4096]{1,0:T(8,128)(2,1)} %param.23) | copy-start | bytes 688132
  10.4 26.2 %collective-permute-start = (bf16[2,256,1024]{2,1,0:T(8,128)(2,1)}, bf16[2,256,1024]{2,1,0:T(8,128)(2,1)}, u32[]{:S(2)}, u32[]{:S(2)}) collective-permute-start(bf16[2,256,1024]{2,1,0:T(8,128)(2,1)} %get-tuple-element.18), channel_id=1, source_target_pairs={{0,8},{8,16},{16,24},{24,32},{32,40},{40,48},{48,56},{56,64},{64,7... | collective-permute-start | bytes 3145736 | tf_op jit(solution)/shard_map/ppermute | solution.py:192
  14.9 26.8 %collective-permute-start.1 = (bf16[2,256,1024]{2,1,0:T(8,128)(2,1)}, bf16[2,256,1024]{2,1,0:T(8,128)(2,1)}, u32[]{:S(2)}, u32[]{:S(2)}) collective-permute-start(bf16[2,256,1024]{2,1,0:T(8,128)(2,1)} %get-tuple-element.19), channel_id=1, source_target_pairs={{8,0},{16,8},{24,16},{32,24},{40,32},{48,40},{56,48},{64,56},{72,6... | collective-permute-start | bytes 3145736 | tf_op jit(solution)/shard_map/ppermute | solution.py:193
  24.2 19.5 %copy-start.5 = (bf16[1024,1024]{1,0:T(8,128)(2,1)S(1)}, bf16[1024,1024]{1,0:T(8,128)(2,1)}, u32[]{:S(2)}) copy-start(bf16[1024,1024]{1,0:T(8,128)(2,1)} %param.20) | copy-start | bytes 6291460
  24.2 19.5 %copy-start.6 = (bf16[1024,1024]{1,0:T(8,128)(2,1)S(1)}, bf16[1024,1024]{1,0:T(8,128)(2,1)}, u32[]{:S(2)}) copy-start(bf16[1024,1024]{1,0:T(8,128)(2,1)} %param.19) | copy-start | bytes 6291460
  51.9 48.8 %copy-start.7 = (bf16[1024,512]{1,0:T(8,128)(2,1)S(1)}, bf16[1024,512]{1,0:T(8,128)(2,1)}, u32[]{:S(2)}) copy-start(bf16[1024,512]{1,0:T(8,128)(2,1)} %param.26) | copy-start | bytes 3145732
  103.5 20.4 %all-to-all-start = ((bf16[16,16,1152]{2,1,0:T(8,128)(2,1)}), bf16[16,16,1152]{2,1,0:T(8,128)(2,1)S(1)}, u32[]{:S(2)}, u32[]{:S(2)}) async-start(bf16[16,16,1152]{2,1,0:T(8,128)(2,1)} %fusion.30), calls=%async_computation | async-start | bytes 1179648 | tf_op jit(solution)/shard_map/all_to_all | solution.py:237
  111.1 76.9 %reduce-scatter.2.cloned.1.call-start = ((), (), s32[]{:S(2)}) async-start(), calls=%async_computation.3 | async-start | bytes 4718592 | tf_op jit(solution)/shard_map/reduce_scatter | solution.py:270
  123.9 3.4 %copy-start.1 = (bf16[16,16,1152]{2,1,0:T(8,128)(2,1)}, bf16[16,16,1152]{2,1,0:T(8,128)(2,1)S(1)}, u32[]{:S(2)}) copy-start(bf16[16,16,1152]{2,1,0:T(8,128)(2,1)S(1)} %all-to-all-done) | copy-start | bytes 1769476
Sparse Core Ops, SparseCore 0:
  152.5 35.4 reduce-scatter.1

commit v11 on v10

--- a/solution.py
+++ b/solution.py
@@ -31,8 +31,7 @@
 
 
 def band_kernel(
-    q_ref, km_ref, vm_ref, ke_ref, ve_ref, bm_ref, be_ref, eo_ref, sp_ref, rv_ref, pm_ref,
-    e_ref, p_ref, ctx
+    q_ref, km_ref, vm_ref, ke_ref, ve_ref, bm_ref, be_ref, eo_ref, sp_ref, lim_ref, e_ref, p_ref, ctx
 ):
     bias_mid = bm_ref[0, 0]
     bias_edge = be_ref[0, 0]
@@ -68,12 +67,21 @@
         ctx[:, cols] = out.astype(jnp.bfloat16)
     attended = jnp.dot(ctx[...], eo_ref[...], preferred_element_type=jnp.float32)
     rows = sp_ref[0].astype(jnp.float32) + attended
-    encoded = jnp.where(rv_ref[0] > 0, rows, 0.0).astype(jnp.bfloat16)
+    local_row = pl.program_id(1) * QBLOCK + lax.broadcasted_iota(jnp.int32, (QBLOCK, 1), 0)
+    encoded = jnp.where(local_row < lim_ref[pl.program_id(0)], rows, 0.0).astype(jnp.bfloat16)
     e_ref[0] = encoded
-    p_ref[0] = jnp.dot(pm_ref[...], encoded, preferred_element_type=jnp.float32)
-
-
-def band_attention(qkv, keyval_edges, bias_mid, bias_edge, enc_out, spectra, row_valid):
+    pooled_rows = QBLOCK // POOL
+    pool_matrix = jnp.where(
+        lax.broadcasted_iota(jnp.int32, (pooled_rows, QBLOCK), 1) // POOL
+        == lax.broadcasted_iota(jnp.int32, (pooled_rows, QBLOCK), 0),
+        1.0 / POOL,
+        0.0,
+    ).astype(jnp.bfloat16)
+    pooled = jnp.dot(pool_matrix, encoded, preferred_element_type=jnp.float32)
+    p_ref[0] = pooled.astype(p_ref.dtype)
+
+
+def band_attention(qkv, keyval_edges, bias_mid, bias_edge, enc_out, spectra, row_limit):
     spec_dev, bin_dev, triple = qkv.shape
     width = triple // 3
     edge_rows = keyval_edges.shape[1] // 2
@@ -81,15 +89,11 @@
     qblocks = bin_dev // QBLOCK
     kwin = bin_dev + edge_rows
     pooled_rows = QBLOCK // POOL
-    pool_matrix = (
-        jnp.arange(QBLOCK, dtype=jnp.int32)[None, :] // POOL
-        == jnp.arange(pooled_rows, dtype=jnp.int32)[:, None]
-    ).astype(jnp.bfloat16) * (1.0 / POOL)
     return pl.pallas_call(
         band_kernel,
         out_shape=(
             jax.ShapeDtypeStruct((spec_dev, bin_dev, width), jnp.bfloat16),
-            jax.ShapeDtypeStruct((spec_dev, bin_dev // POOL, width), jnp.float32),
+            jax.ShapeDtypeStruct((spec_dev, bin_dev // POOL, width), jnp.bfloat16),
         ),
         grid=(spec_dev, qblocks),
         in_specs=[
@@ -102,8 +106,7 @@
             pl.BlockSpec((1, 1, QBLOCK, edge_rows), lambda s, b: (s, b, 0, 0)),
             pl.BlockSpec((width, width), lambda s, b: (0, 0)),
             pl.BlockSpec((1, QBLOCK, width), lambda s, b: (s, b, 0)),
-            pl.BlockSpec((1, QBLOCK, 1), lambda s, b: (s, b, 0)),
-            pl.BlockSpec((pooled_rows, QBLOCK), lambda s, b: (0, 0)),
+            pl.BlockSpec(memory_space=pltpu.SMEM),
         ],
         out_specs=(
             pl.BlockSpec((1, QBLOCK, width), lambda s, b: (s, b, 0)),
@@ -120,7 +123,7 @@
         ),
     )(
         qkv, qkv, qkv, keyval_edges, keyval_edges, bias_mid, bias_edge,
-        enc_out, spectra, row_valid, pool_matrix,
+        enc_out, spectra, row_limit,
     )
 
 def cross_kernel(q_ref, k_ref, v_ref, b_ref, o_ref):
@@ -217,12 +220,10 @@
     col_edge = col_bias.reshape(spec_dev, key_span // half_span, half_span)[:, :: qblocks + 1]
     bias_mid = jnp.where(band_mid[None], col_mid[:, None, None, :], masked_score)
     bias_edge = jnp.where(band_edge[None], col_edge[:, :, None, :], masked_score)
-    query_rows = first_bin + jnp.arange(bin_dev, dtype=jnp.int32)
-    row_valid = (query_rows[None, :] < my_counts[:, None]).astype(jnp.int32)[:, :, None]
-    encoded, pooled_sums = band_attention(
-        qkv, keyval_edges, bias_mid, bias_edge, enc_out, spectra, row_valid
-    )
-    pooled = pooled_sums.astype(jnp.bfloat16)
+    row_limit = my_counts - first_bin
+    encoded, pooled = band_attention(
+        qkv, keyval_edges, bias_mid, bias_edge, enc_out, spectra, row_limit
+    )
     spectra_all = lax.all_gather(pooled, "head", axis=0, tiled=True)
     mem_weights = jnp.concatenate([mem_key, mem_value], axis=1)
     local_width = mem_key.shape[1]

time: 198 us -> 197 us (level)
  transfers between devices with their start and end apart: 4 -> 4, of which waited for: 3 -> 4; matrix products, arithmetic and copies ran while one was open for 12% -> 11% of each run, Pallas kernels for 0% -> 0%
where the time goes in v11:
time: 197 us; the launch traced here: 196 us
  waiting for transfers between devices  51.5 us (26%)
  Pallas kernels  37.5 us (19%)
  matrix products  34.2 us (17%)
  blocking collectives  29 us (15%)
  between operations  14.3 us (7%)
  starting transfers between devices  13.4 us (7%)
  other arithmetic  10.1 us (5%)
  local copies, waits for them, and re-layouts  6.42 us (3%)
    reduce_scatter x1, waiting for transfers between devices, per_device(): lax.psum_scatter(partial_sums.astype(jnp.bfloat16), 'head', scatter_dimen...  35.7 us
    pallas_call x1, Pallas kernels, band_attention(): pl.pallas_call(band_kernel, out_shape=(jax.ShapeDtypeStruct((spec_dev, bi...  33.3 us
    all_gather x1, blocking collectives, per_device(): spectra_all = lax.all_gather(pooled, 'head', axis=0, tiled=True)  14.5 us
    all_to_all x1, blocking collectives, per_device(): dec_context = lax.all_to_all(context_one, 'seq', 0, 0, tiled=True)  14.4 us
    dot_general x1, matrix products, per_device(): jnp.einsum('sbd,de->sbe', normed, qkv_weights, preferred_element_type=jnp...  12.4 us
    all_to_all x1, waiting for transfers between devices, per_device(): received = lax.all_to_all(payload, 'seq', 0, 1, tiled=True)  9.63 us
    dot_general x1, matrix products, per_device(): jnp.einsum('sbd,de->sbe', edges, kv_weights, preferred_element_type=jnp.f...  8.1 us
    all_to_all x1, starting transfers between devices, per_device(): received = lax.all_to_all(payload, 'seq', 0, 1, tiled=True)  7.63 us
  transfers between devices with their start and end apart: 4, of which 4 were waited for; matrix products, arithmetic and copies ran while one was open for 11% of the time, Pallas kernels for 0%

profile of v11, /device:TPU:0, one launch (start us, length us, event | category | flops | bytes accessed | tf_op | source)
XLA Modules:
  0.0 196.3 jit_solution(5790158977354870040)
XLA Ops:
  7.2 0.0 copy-start
  7.2 0.0 copy-start.5
  7.2 0.0 copy-start.3
  7.2 0.0 copy-start.4
  7.2 0.0 copy-start.2
  7.2 3.2 %fusion.46 = (bf16[2,256,1024]{2,1,0:T(8,128)(2,1)}, bf16[2,256,1024]{2,1,0:T(8,128)(2,1)}) fusion(bf16[2,512,1024]{2,1,0:T(8,128)(2,1)} %sp_ref.1), kind=kLoop, calls=%fused_computation.89 | loop fusion | bytes 4194304 | tf_op jit(solution)/shard_map/slice | solution.py:195
  10.4 4.4 %collective-permute-start = (bf16[2,256,1024]{2,1,0:T(8,128)(2,1)}, bf16[2,256,1024]{2,1,0:T(8,128)(2,1)}, u32[]{:S(2)}, u32[]{:S(2)}) collective-permute-start(bf16[2,256,1024]{2,1,0:T(8,128)(2,1)} %get-tuple-element.20), channel_id=1, source_target_pairs={{0,8},{8,16},{16,24},{24,32},{32,40},{40,48},{48,56},{56,64},{64,7... | collective-permute-start | bytes 3145736 | tf_op jit(solution)/shard_map/ppermute | solution.py:195
  14.9 1.3 collective-permute-start.1
  16.2 0.0 copy-done.5
  16.2 0.7 broadcast_subtract_fusion
  16.9 0.0 copy-done.3
  16.9 0.1 and_select_fusion
  17.0 0.0 copy-done
  17.0 0.5 fusion.6
  17.5 0.1 dynamic-slice_reduce_fusion
  17.6 0.6 dynamic_slice.18
  18.2 0.1 iota_add_fusion.1
  18.3 0.2 fusion.35
  18.5 0.3 fusion.29
  18.8 0.0 copy-done.4
  18.9 0.0 copy-done.2
  18.9 0.2 fusion.31
  19.1 0.1 reshape.255
  19.1 1.1 broadcast_select_fusion.1.be_ref
  20.2 1.6 broadcast_select_fusion.bm_ref
  21.8 0.1 reduce_max.11
  21.9 1.2 compare_select_fusion.2.b_ref
  23.1 0.0 copy-start.6
  23.1 0.0 copy-start.7
  23.1 12.4 %fusion.5.q_ref.km_ref.vm_ref = bf16[2,512,3072]{2,1,0:T(8,128)(2,1)} fusion(bf16[1024,1024]{1,0:T(8,128)(2,1)} %param.20, bf16[1024,1024]{1,0:T(8,128)(2,1)} %param.19, bf16[1024,1024]{1,0:T(8,128)(2,1)} %param.18, bf16[2,512,1024]{2,1,0:T(8,128)(2,1)S(1)} %copy-done, f32[2,512]{1,0:T(2,128)S(1)} %add_rsqrt_fusion.2), kind=kOutput, calls=%fused_computation.8 | convolution fusion | flops 6467616768 | bytes 14684160 | tf_op jit(solution)/shard_map/sbd,de->sbe/dot_general | solution.py:199
  35.5 1.1 collective-permute-done
  36.6 5.1 %collective-permute-done.1 = bf16[2,256,1024]{2,1,0:T(8,128)(2,1)} collective-permute-done((bf16[2,256,1024]{2,1,0:T(8,128)(2,1)}, bf16[2,256,1024]{2,1,0:T(8,128)(2,1)}, u32[]{:S(2)}, u32[]{:S(2)}) %collective-permute-start.1) | collective-permute-done | bytes 1048608 | tf_op jit(solution)/shard_map/ppermute | solution.py:196
  41.7 2.0 %fusion.8 = f32[2,512]{1,0:T(2,128)S(1)} fusion(bf16[2,256,1024]{2,1,0:T(8,128)(2,1)} %collective-permute-done.1, bf16[2,256,1024]{2,1,0:T(8,128)(2,1)} %collective-permute-done), kind=kLoop, calls=%fused_computation.15 | loop fusion | flops 6290432 | bytes 2101248 | tf_op jit(solution)/shard_map/reduce_sum | solution.py:23
  43.7 0.0 copy-done.6
  43.8 0.0 copy-done.7
  43.8 8.1 %fusion.14.ke_ref.ve_ref = bf16[2,512,2048]{2,1,0:T(8,128)(2,1)} fusion(bf16[1024,1024]{1,0:T(8,128)(2,1)S(1)} %copy-done.6, bf16[1024,1024]{1,0:T(8,128)(2,1)S(1)} %copy-done.7, f32[2,512]{1,0:T(2,128)S(1)} %add_rsqrt_fusion.1, bf16[2,256,1024]{2,1,0:T(8,128)(2,1)} %collective-permute-done.1, bf16[2,256,1024]{2,1,0:T(8,128)(2,1)} %collective-permute-done), kind=kOutput, calls=%fused_computation.22 | convolution fusion | flops 4311744512 | bytes 10489856 | tf_op jit(solution)/shard_map/sbd,de->sbe/dot_general | solution.py:203
  51.9 0.0 copy-start.8
  51.9 33.3 %shard_map.140 = (bf16[2,512,1024]{2,1,0:T(8,128)(2,1)}, bf16[2,16,1024]{2,1,0:T(8,128)(2,1)}) custom-call(bf16[2,512,3072]{2,1,0:T(8,128)(2,1)} %fusion.5.q_ref.km_ref.vm_ref, bf16[2,512,3072]{2,1,0:T(8,128)(2,1)} %fusion.5.q_ref.km_ref.vm_ref, bf16[2,512,3072]{2,1,0:T(8,128)(2,1)} %fusion.5.q_ref.km_ref.vm_ref, ...), custom_call_target="tpu_custom_call" | custom-call | flops 8589934592 | bytes 19922944 | tf_op jit(solution)/shard_map/pallas_call | solution.py:92
  85.1 14.5 %all_gather.3 = bf16[16,16,1024]{2,1,0:T(8,128)(2,1)S(1)} all-gather(bf16[2,16,1024]{2,1,0:T(8,128)(2,1)} %get-tuple-element.17), channel_id=1, replica_groups=mesh['seq'=16,'head'=8] {'head'}, dimensions={0}, use_global_device_ids=true | all-gather | bytes 589824 | tf_op jit(solution)/shard_map/all_gather | solution.py:227
  99.7 0.2 fusion.27
  99.9 0.0 copy-done.8
  99.9 2.0 %fusion.22 = bf16[16,16,1024]{2,1,0:T(8,128)(2,1)S(1)} fusion(bf16[1024,512]{1,0:T(8,128)(2,1)S(1)} %copy-done.8, bf16[1024,512]{1,0:T(8,128)(2,1)} %param.25, bf16[16,16,1024]{2,1,0:T(8,128)(2,1)S(1)} %all_gather.3, f32[16,16]{1,0:T(8,128)S(1)} %add_rsqrt_fusion), kind=kOutput, calls=%fused_computation.34 | convolution fusion | flops 542113792 | bytes 3146752 | tf_op jit(solution)/shard_map/spd,de->spe/dot_general | solution.py:230
  101.9 0.9 fusion.30
  102.7 7.6 %all-to-all-start = ((bf16[16,16,1152]{2,1,0:T(8,128)(2,1)}), bf16[16,16,1152]{2,1,0:T(8,128)(2,1)S(1)}, u32[]{:S(2)}, u32[]{:S(2)}) async-start(bf16[16,16,1152]{2,1,0:T(8,128)(2,1)} %fusion.30), calls=%async_computation | async-start | bytes 1179648 | tf_op jit(solution)/shard_map/all_to_all | solution.py:238
  110.4 0.0 reduce-scatter.2.cloned.1.call-start
  110.4 3.1 %convolution_convert_fusion.2 = bf16[28,512]{1,0:T(8,128)(2,1)S(1)} fusion(bf16[4096,512]{1,0:T(8,128)(2,1)} %param.24, bf16[28,4096]{1,0:T(8,128)(2,1)S(1)} %copy-done.2, f32[28]{0:T(128)S(1)} %add_rsqrt_fusion.3), kind=kOutput, calls=%fused_computation.41 | convolution fusion | flops 117798912 | bytes 4452464 | tf_op jit(solution)/shard_map/vd,de->ve/dot_general | solution.py:260
  113.5 9.6 %all-to-all-done = bf16[16,16,1152]{2,1,0:T(8,128)(2,1)S(1)} async-done(((bf16[16,16,1152]{2,1,0:T(8,128)(2,1)}), bf16[16,16,1152]{2,1,0:T(8,128)(2,1)S(1)}, u32[]{:S(2)}, u32[]{:S(2)}) %all-to-all-start) | async-done | bytes 589856 | tf_op jit(solution)/shard_map/all_to_all | solution.py:238
  123.1 0.0 copy-start.1
  123.1 0.1 reshape.258
  123.2 0.1 reshape.257
  123.3 2.2 %gather_fusion = bf16[512,512]{1,0:T(8,128)(2,1)S(1)} fusion(bf16[28,512]{1,0:T(8,128)(2,1)S(1)} %convolution_convert_fusion.2, s32[1024]{0:T(1024)S(1)} %pad_clamp_fusion), kind=kCustom, calls=%fused_computation | custom fusion | bytes 1050624 | tf_op jit(solution)/shard_map/jit(_take)/gather | solution.py:263
  125.5 0.9 bitcast_select_fusion.q_ref
  126.5 0.0 copy-done.1
  126.5 4.2 %shard_map.141 = bf16[1,512,512]{2,1,0:T(8,128)(2,1)} custom-call(bf16[1,512,512]{2,1,0:T(8,128)(2,1)} %bitcast_select_fusion.q_ref, bf16[1,256,1152]{2,1,0:T(8,128)(2,1)} %bitcast.33, bf16[1,256,1152]{2,1,0:T(8,128)(2,1)} %bitcast.34, f32[1,1,256]{2,1,0:T(1,128)} %compare_select_fusion.2.b_ref), custom_call_target="tpu_custom_call" | custom-call | flops 268435456 | bytes 1572864 | tf_op jit(solution)/shard_map/pallas_call | solution.py:144
  130.7 14.4 %all_to_all.17 = bf16[16,32,512]{2,1,0:T(8,128)(2,1)S(1)} all-to-all(bf16[16,32,512]{2,1,0:T(8,128)(2,1)} %bitcast.35), channel_id=1, replica_groups=mesh['seq'=16,'head'=8] {'seq'}, dimensions={0} | all-to-all | bytes 1048576 | tf_op jit(solution)/shard_map/all_to_all | solution.py:267
  145.1 6.5 %convolution_convert_fusion = bf16[16,32,4096]{2,1,0:T(8,128)(2,1)} fusion(bf16[16,32,512]{2,1,0:T(8,128)(2,1)S(1)} %all_to_all.17, bf16[512,4096]{1,0:T(8,128)(2,1)} %param.27), kind=kOutput, calls=%fused_computation.7 | convolution fusion | flops 2149580800 | bytes 8912896 | tf_op jit(solution)/shard_map/ste,ed->std/dot_general | solution.py:268
  151.6 0.0 reduce-scatter.2.cloned.1.call-update
  151.6 35.7 %reduce-scatter.2.cloned.1.call-done = bf16[16,32,512]{2,1,0:T(8,128)(2,1)} async-done(((bf16[16,32,4096]{2,1,0:T(8,128)(2,1)}), bf16[16,32,512]{2,1,0:T(8,128)(2,1)}) %reduce-scatter.2.cloned.1.call-update) | async-done | bytes 524304 | tf_op jit(solution)/shard_map/reduce_scatter | solution.py:271
  187.3 2.2 %fusion.25 = bf16[16,32,512]{2,1,0:T(8,128)(2,1)} fusion(bf16[16,32,512]{2,1,0:T(8,128)(2,1)} %reduce-scatter.2.cloned.1.call-done, s32[16,32]{1,0:T(8,128)S(1)} %copy-done.4, bf16[28,4096]{1,0:T(8,128)(2,1)S(1)} %copy-done.2, s32[]{:T(128)S(6)} %select_n.71), kind=kOutput, calls=%fused_computation.38 | convolution fusion | flops 16005120 | bytes 1089540 | tf_op jit(solution)/shard_map/stv,vd->std/dot_general | solution.py:257
  (19 shorter events, 0.2 us)
Async XLA Ops:
  7.2 9.9 %copy-start = (bf16[2,512,1024]{2,1,0:T(8,128)(2,1)S(1)}, bf16[2,512,1024]{2,1,0:T(8,128)(2,1)}, u32[]{:S(2)}) copy-start(bf16[2,512,1024]{2,1,0:T(8,128)(2,1)} %sp_ref.1) | copy-start | bytes 6291460
  7.2 9.1 %copy-start.5 = (s32[16]{0:T(128)S(1)}, s32[16]{0:T(128)}, u32[]{:S(2)}) copy-start(s32[16]{0:T(128)} %param.17) | copy-start | bytes 196
  7.2 9.7 %copy-start.3 = (f32[16,8192]{1,0:T(8,128)S(1)}, f32[16,8192]{1,0:T(8,128)}, u32[]{:S(2)}) copy-start(f32[16,8192]{1,0:T(8,128)} %param.16) | copy-start | bytes 1572868
  7.2 11.6 %copy-start.4 = (s32[16,32]{1,0:T(8,128)S(1)}, s32[16,32]{1,0:T(8,128)}, u32[]{:S(2)}) copy-start(s32[16,32]{1,0:T(8,128)} %param.22) | copy-start | bytes 6148
  7.2 11.7 %copy-start.2 = (bf16[28,4096]{1,0:T(8,128)(2,1)S(1)}, bf16[28,4096]{1,0:T(8,128)(2,1)}, u32[]{:S(2)}) copy-start(bf16[28,4096]{1,0:T(8,128)(2,1)} %param.23) | copy-start | bytes 688132
  10.4 26.2 %collective-permute-start = (bf16[2,256,1024]{2,1,0:T(8,128)(2,1)}, bf16[2,256,1024]{2,1,0:T(8,128)(2,1)}, u32[]{:S(2)}, u32[]{:S(2)}) collective-permute-start(bf16[2,256,1024]{2,1,0:T(8,128)(2,1)} %get-tuple-element.20), channel_id=1, source_target_pairs={{0,8},{8,16},{16,24},{24,32},{32,40},{40,48},{48,56},{56,64},{64,7... | collective-permute-start | bytes 3145736 | tf_op jit(solution)/shard_map/ppermute | solution.py:195
  14.9 26.8 %collective-permute-start.1 = (bf16[2,256,1024]{2,1,0:T(8,128)(2,1)}, bf16[2,256,1024]{2,1,0:T(8,128)(2,1)}, u32[]{:S(2)}, u32[]{:S(2)}) collective-permute-start(bf16[2,256,1024]{2,1,0:T(8,128)(2,1)} %get-tuple-element.21), channel_id=1, source_target_pairs={{8,0},{16,8},{24,16},{32,24},{40,32},{48,40},{56,48},{64,56},{72,6... | collective-permute-start | bytes 3145736 | tf_op jit(solution)/shard_map/ppermute | solution.py:196
  23.1 20.6 %copy-start.6 = (bf16[1024,1024]{1,0:T(8,128)(2,1)S(1)}, bf16[1024,1024]{1,0:T(8,128)(2,1)}, u32[]{:S(2)}) copy-start(bf16[1024,1024]{1,0:T(8,128)(2,1)} %param.20) | copy-start | bytes 6291460
  23.1 20.6 %copy-start.7 = (bf16[1024,1024]{1,0:T(8,128)(2,1)S(1)}, bf16[1024,1024]{1,0:T(8,128)(2,1)}, u32[]{:S(2)}) copy-start(bf16[1024,1024]{1,0:T(8,128)(2,1)} %param.19) | copy-start | bytes 6291460
  51.9 48.0 %copy-start.8 = (bf16[1024,512]{1,0:T(8,128)(2,1)S(1)}, bf16[1024,512]{1,0:T(8,128)(2,1)}, u32[]{:S(2)}) copy-start(bf16[1024,512]{1,0:T(8,128)(2,1)} %param.26) | copy-start | bytes 3145732
  102.7 20.4 %all-to-all-start = ((bf16[16,16,1152]{2,1,0:T(8,128)(2,1)}), bf16[16,16,1152]{2,1,0:T(8,128)(2,1)S(1)}, u32[]{:S(2)}, u32[]{:S(2)}) async-start(bf16[16,16,1152]{2,1,0:T(8,128)(2,1)} %fusion.30), calls=%async_computation | async-start | bytes 1179648 | tf_op jit(solution)/shard_map/all_to_all | solution.py:238
  110.4 76.9 %reduce-scatter.2.cloned.1.call-start = ((), (), s32[]{:S(2)}) async-start(), calls=%async_computation.3 | async-start | bytes 4718592 | tf_op jit(solution)/shard_map/reduce_scatter | solution.py:271
  123.1 3.4 %copy-start.1 = (bf16[16,16,1152]{2,1,0:T(8,128)(2,1)}, bf16[16,16,1152]{2,1,0:T(8,128)(2,1)S(1)}, u32[]{:S(2)}) copy-start(bf16[16,16,1152]{2,1,0:T(8,128)(2,1)S(1)} %all-to-all-done) | copy-start | bytes 1769476
Sparse Core Ops, SparseCore 0:
  151.7 35.4 reduce-scatter.1

commit v12 on v11

--- a/solution.py
+++ b/solution.py
@@ -199,6 +199,12 @@
     qkv = jnp.einsum(
         "sbd,de->sbe", normed, qkv_weights, preferred_element_type=jnp.float32
     ).astype(jnp.bfloat16)
+    query_table = jnp.einsum(
+        "vd,de->ve", rms_rows(embedding), dec_query, preferred_element_type=jnp.float32
+    ).astype(jnp.bfloat16)
+    query_table, low_edge, high_edge = lax.optimization_barrier(
+        (query_table, low_edge, high_edge)
+    )
     edges = rms_rows(jnp.concatenate([low_edge, high_edge], axis=1))
     keyval_edges = jnp.einsum(
         "sbd,de->sbe", edges, kv_weights, preferred_element_type=jnp.float32
@@ -257,9 +263,6 @@
     own_part = jnp.einsum(
         "stv,vd->std", onehot, own_table, preferred_element_type=jnp.float32
     ).astype(jnp.bfloat16)
-    query_table = jnp.einsum(
-        "vd,de->ve", rms_rows(embedding), dec_query, preferred_element_type=jnp.float32
-    ).astype(jnp.bfloat16)
     query_one = jnp.take(query_table, ids_one[0], axis=0)[None]
     mem_bias = jnp.where(mem_valid, pooled_bias, masked_score)[:, None, :]
     context_one = cross_attention(query_one, received, mem_bias, heads_here, dec_head)

time: 197 us -> 195 us (0.990)
  matrix products: 34.2 us -> 28.3 us
  waiting for transfers between devices: 51.5 us -> 53.6 us
    ppermute x1, waiting for transfers between devices: 1.1 us -> 4.11 us  [per_device(): low_edge = lax.ppermute(spectra[:, bin_dev - half_span:], 'seq', forward)]
    dot_general x1, matrix products: 3.05 us -> 0.86 us  [per_device(): jnp.einsum('vd,de->ve', rms_rows(embedding), dec_query, preferred_element...]
    dot_general x1, matrix products: 12.4 us -> 10.4 us  [per_device(): jnp.einsum('sbd,de->sbe', normed, qkv_weights, preferred_element_type=jnp...]
  transfers between devices with their start and end apart: 4 -> 4, of which waited for: 4 -> 4; matrix products, arithmetic and copies ran while one was open for 11% -> 10% of each run, Pallas kernels for 0% -> 0%
where the time goes in v12:
time: 195 us; the launch traced here: 194 us
  waiting for transfers between devices  53.6 us (27%)
  Pallas kernels  37.7 us (19%)
  blocking collectives  29 us (15%)
  matrix products  28.3 us (15%)
  between operations  14.3 us (7%)
  starting transfers between devices  13.4 us (7%)
  other arithmetic  10.5 us (5%)
  local copies, waits for them, and re-layouts  7.52 us (4%)
    reduce_scatter x1, waiting for transfers between devices, per_device(): lax.psum_scatter(partial_sums.astype(jnp.bfloat16), 'head', scatter_dimen...  35.6 us
    pallas_call x1, Pallas kernels, band_attention(): pl.pallas_call(band_kernel, out_shape=(jax.ShapeDtypeStruct((spec_dev, bi...  33.5 us
    all_gather x1, blocking collectives, per_device(): spectra_all = lax.all_gather(pooled, 'head', axis=0, tiled=True)  14.5 us
    all_to_all x1, blocking collectives, per_device(): dec_context = lax.all_to_all(context_one, 'seq', 0, 0, tiled=True)  14.4 us
    dot_general x1, matrix products, per_device(): jnp.einsum('sbd,de->sbe', normed, qkv_weights, preferred_element_type=jnp...  10.4 us
    all_to_all x1, waiting for transfers between devices, per_device(): received = lax.all_to_all(payload, 'seq', 0, 1, tiled=True)  9.63 us
    all_to_all x1, starting transfers between devices, per_device(): received = lax.all_to_all(payload, 'seq', 0, 1, tiled=True)  8.51 us
    dot_general x1, matrix products, per_device(): jnp.einsum('sbd,de->sbe', edges, kv_weights, preferred_element_type=jnp.f...  7.57 us
  transfers between devices with their start and end apart: 4, of which 4 were waited for; matrix products, arithmetic and copies ran while one was open for 10% of the time, Pallas kernels for 0%

profile of v12, /device:TPU:0, one launch (start us, length us, event | category | flops | bytes accessed | tf_op | source)
XLA Modules:
  0.0 194.3 jit_solution(137349014658818716)
XLA Ops:
  7.2 0.0 copy-start
  7.2 0.0 copy-start.5
  7.2 0.0 copy-start.3
  7.2 0.0 copy-start.4
  7.2 3.2 %fusion.46 = (bf16[2,256,1024]{2,1,0:T(8,128)(2,1)}, bf16[2,256,1024]{2,1,0:T(8,128)(2,1)}) fusion(bf16[2,512,1024]{2,1,0:T(8,128)(2,1)} %sp_ref.1), kind=kLoop, calls=%fused_computation.89 | loop fusion | bytes 4194304 | tf_op jit(solution)/shard_map/slice | solution.py:196
  10.4 3.5 %collective-permute-start = (bf16[2,256,1024]{2,1,0:T(8,128)(2,1)}, bf16[2,256,1024]{2,1,0:T(8,128)(2,1)S(1)}, u32[]{:S(2)}, u32[]{:S(2)}) collective-permute-start(bf16[2,256,1024]{2,1,0:T(8,128)(2,1)} %get-tuple-element.27), channel_id=1, source_target_pairs={{0,8},{8,16},{16,24},{24,32},{32,40},{40,48},{48,56},{56,64},{64,7... | collective-permute-start | bytes 3145736 | tf_op jit(solution)/shard_map/ppermute | solution.py:195
  14.0 1.3 collective-permute-start.1
  15.3 0.0 copy-done.5
  15.3 0.7 broadcast_subtract_fusion
  16.0 0.8 and_select_fusion
  16.8 0.0 copy-done
  16.9 0.5 fusion.6
  17.4 0.0 copy-start.2
  17.4 0.1 iota_add_fusion.1
  17.4 0.2 fusion.35
  17.6 0.3 fusion.29
  18.0 0.0 copy-done.3
  18.0 0.0 copy-start.6
  18.0 0.0 copy-start.7
  18.0 0.2 fusion.31
  18.2 0.0 copy-done.4
  18.2 1.1 broadcast_select_fusion.1.be_ref
  19.3 1.6 broadcast_select_fusion.bm_ref
  20.9 0.0 copy-done.2
  20.9 0.9 convolution_convert_fusion.2
  21.8 0.0 copy-done.6
  21.8 0.4 copy-done.7
  22.1 0.0 copy-start.8
  22.1 10.4 %fusion.5.q_ref.km_ref.vm_ref = bf16[2,512,3072]{2,1,0:T(8,128)(2,1)} fusion(bf16[1024,1024]{1,0:T(8,128)(2,1)S(1)} %copy-done.7, bf16[1024,1024]{1,0:T(8,128)(2,1)} %param.19, bf16[1024,1024]{1,0:T(8,128)(2,1)S(1)} %copy-done.6, bf16[2,512,1024]{2,1,0:T(8,128)(2,1)S(1)} %copy-done, f32[2,512]{1,0:T(2,128)S(1)} %add_rsqrt_fusion.2), kind=kOutput, calls=%fused_computation.8 | convolution fusion | flops 6467616768 | bytes 14684160 | tf_op jit(solution)/shard_map/sbd,de->sbe/dot_general | solution.py:199
  32.5 4.1 %collective-permute-done = bf16[2,256,1024]{2,1,0:T(8,128)(2,1)S(1)} collective-permute-done((bf16[2,256,1024]{2,1,0:T(8,128)(2,1)}, bf16[2,256,1024]{2,1,0:T(8,128)(2,1)S(1)}, u32[]{:S(2)}, u32[]{:S(2)}) %collective-permute-start) | collective-permute-done | bytes 1048608 | tf_op jit(solution)/shard_map/ppermute | solution.py:195
  36.6 4.2 %collective-permute-done.1 = bf16[2,256,1024]{2,1,0:T(8,128)(2,1)} collective-permute-done((bf16[2,256,1024]{2,1,0:T(8,128)(2,1)}, bf16[2,256,1024]{2,1,0:T(8,128)(2,1)}, u32[]{:S(2)}, u32[]{:S(2)}) %collective-permute-start.1) | collective-permute-done | bytes 1048608 | tf_op jit(solution)/shard_map/ppermute | solution.py:196
  40.8 1.7 fusion.8
  42.5 0.0 copy-done.8
  42.5 7.6 %fusion.14.ke_ref.ve_ref = bf16[2,512,2048]{2,1,0:T(8,128)(2,1)} fusion(bf16[1024,1024]{1,0:T(8,128)(2,1)S(1)} %copy-done.7, bf16[1024,1024]{1,0:T(8,128)(2,1)S(1)} %copy-done.8, f32[2,512]{1,0:T(2,128)S(1)} %add_rsqrt_fusion.1, bf16[2,256,1024]{2,1,0:T(8,128)(2,1)} %collective-permute-done.1, bf16[2,256,1024]{2,1,0:T(8,128)(2,1)S(1)} %collective-permute-done), kind=kOutput, calls=%fused_computation.22 | convolution fusion | flops 4311744512 | bytes 10489856 | tf_op jit(solution)/shard_map/sbd,de->sbe/dot_general | solution.py:209
  50.1 0.0 copy-start.9
  50.1 0.0 copy-start.10
  50.1 33.5 %shard_map.140 = (bf16[2,512,1024]{2,1,0:T(8,128)(2,1)}, bf16[2,16,1024]{2,1,0:T(8,128)(2,1)}) custom-call(bf16[2,512,3072]{2,1,0:T(8,128)(2,1)} %fusion.5.q_ref.km_ref.vm_ref, bf16[2,512,3072]{2,1,0:T(8,128)(2,1)} %fusion.5.q_ref.km_ref.vm_ref, bf16[2,512,3072]{2,1,0:T(8,128)(2,1)} %fusion.5.q_ref.km_ref.vm_ref, ...), custom_call_target="tpu_custom_call" | custom-call | flops 8589934592 | bytes 19922944 | tf_op jit(solution)/shard_map/pallas_call | solution.py:92
  83.6 14.5 %all_gather.3 = bf16[16,16,1024]{2,1,0:T(8,128)(2,1)S(1)} all-gather(bf16[2,16,1024]{2,1,0:T(8,128)(2,1)} %get-tuple-element.22), channel_id=1, replica_groups=mesh['seq'=16,'head'=8] {'head'}, dimensions={0}, use_global_device_ids=true | all-gather | bytes 589824 | tf_op jit(solution)/shard_map/all_gather | solution.py:233
  98.1 0.2 fusion.27
  98.3 0.0 copy-done.9
  98.3 0.0 copy-done.10
  98.3 0.8 fusion.22
  99.1 0.9 fusion.30
  100.0 8.5 %all-to-all-start = ((bf16[16,16,1152]{2,1,0:T(8,128)(2,1)}), bf16[16,16,1152]{2,1,0:T(8,128)(2,1)S(1)}, u32[]{:S(2)}, u32[]{:S(2)}) async-start(bf16[16,16,1152]{2,1,0:T(8,128)(2,1)} %fusion.30), calls=%async_computation | async-start | bytes 1179648 | tf_op jit(solution)/shard_map/all_to_all | solution.py:244
  108.5 0.0 reduce-scatter.2.cloned.1.call-start
  108.5 0.6 dynamic_slice.18
  109.1 1.0 dynamic-slice_reduce_fusion
  110.2 0.1 reshape.255
  110.2 0.1 reduce_max.11
  110.4 1.2 compare_select_fusion.2.b_ref
  111.6 9.6 %all-to-all-done = bf16[16,16,1152]{2,1,0:T(8,128)(2,1)S(1)} async-done(((bf16[16,16,1152]{2,1,0:T(8,128)(2,1)}), bf16[16,16,1152]{2,1,0:T(8,128)(2,1)S(1)}, u32[]{:S(2)}, u32[]{:S(2)}) %all-to-all-start) | async-done | bytes 589856 | tf_op jit(solution)/shard_map/all_to_all | solution.py:244
  121.2 0.0 copy-start.1
  121.2 0.1 reshape.258
  121.4 0.1 reshape.257
  121.5 2.0 %gather_fusion = bf16[512,512]{1,0:T(8,128)(2,1)S(1)} fusion(bf16[28,512]{1,0:T(8,128)(2,1)S(1)} %convolution_convert_fusion.2, s32[1024]{0:T(1024)S(1)} %pad_clamp_fusion), kind=kCustom, calls=%fused_computation | custom fusion | bytes 1050624 | tf_op jit(solution)/shard_map/jit(_take)/gather | solution.py:266
  123.4 0.9 bitcast_select_fusion.q_ref
  124.4 0.0 copy-done.1
  124.4 4.2 %shard_map.141 = bf16[1,512,512]{2,1,0:T(8,128)(2,1)} custom-call(bf16[1,512,512]{2,1,0:T(8,128)(2,1)} %bitcast_select_fusion.q_ref, bf16[1,256,1152]{2,1,0:T(8,128)(2,1)} %bitcast.33, bf16[1,256,1152]{2,1,0:T(8,128)(2,1)} %bitcast.34, f32[1,1,256]{2,1,0:T(1,128)} %compare_select_fusion.2.b_ref), custom_call_target="tpu_custom_call" | custom-call | flops 268435456 | bytes 1572864 | tf_op jit(solution)/shard_map/pallas_call | solution.py:144
  128.6 14.4 %all_to_all.17 = bf16[16,32,512]{2,1,0:T(8,128)(2,1)S(1)} all-to-all(bf16[16,32,512]{2,1,0:T(8,128)(2,1)} %bitcast.35), channel_id=1, replica_groups=mesh['seq'=16,'head'=8] {'seq'}, dimensions={0} | all-to-all | bytes 1048576 | tf_op jit(solution)/shard_map/all_to_all | solution.py:270
  143.0 6.5 %convolution_convert_fusion = bf16[16,32,4096]{2,1,0:T(8,128)(2,1)} fusion(bf16[16,32,512]{2,1,0:T(8,128)(2,1)S(1)} %all_to_all.17, bf16[512,4096]{1,0:T(8,128)(2,1)} %param.27), kind=kOutput, calls=%fused_computation.7 | convolution fusion | flops 2149580800 | bytes 8912896 | tf_op jit(solution)/shard_map/ste,ed->std/dot_general | solution.py:271
  149.6 0.0 reduce-scatter.2.cloned.1.call-update
  149.6 35.6 %reduce-scatter.2.cloned.1.call-done = bf16[16,32,512]{2,1,0:T(8,128)(2,1)} async-done(((bf16[16,32,4096]{2,1,0:T(8,128)(2,1)}), bf16[16,32,512]{2,1,0:T(8,128)(2,1)}) %reduce-scatter.2.cloned.1.call-update) | async-done | bytes 524304 | tf_op jit(solution)/shard_map/reduce_scatter | solution.py:274
  185.2 2.2 %fusion.25 = bf16[16,32,512]{2,1,0:T(8,128)(2,1)} fusion(bf16[16,32,512]{2,1,0:T(8,128)(2,1)} %reduce-scatter.2.cloned.1.call-done, s32[16,32]{1,0:T(8,128)S(1)} %copy-done.4, bf16[28,4096]{1,0:T(8,128)(2,1)S(1)} %copy-done.3, s32[]{:T(128)S(6)} %select_n.71), kind=kOutput, calls=%fused_computation.38 | convolution fusion | flops 16005120 | bytes 1089540 | tf_op jit(solution)/shard_map/stv,vd->std/dot_general | solution.py:263
  (19 shorter events, 0.2 us)
Async XLA Ops:
  7.2 9.7 %copy-start = (bf16[2,512,1024]{2,1,0:T(8,128)(2,1)S(1)}, bf16[2,512,1024]{2,1,0:T(8,128)(2,1)}, u32[]{:S(2)}) copy-start(bf16[2,512,1024]{2,1,0:T(8,128)(2,1)} %sp_ref.1) | copy-start | bytes 6291460
  7.2 8.2 %copy-start.5 = (s32[16]{0:T(128)S(1)}, s32[16]{0:T(128)}, u32[]{:S(2)}) copy-start(s32[16]{0:T(128)} %param.17) | copy-start | bytes 196
  7.2 10.8 %copy-start.3 = (bf16[28,4096]{1,0:T(8,128)(2,1)S(1)}, bf16[28,4096]{1,0:T(8,128)(2,1)}, u32[]{:S(2)}) copy-start(bf16[28,4096]{1,0:T(8,128)(2,1)} %param.23) | copy-start | bytes 688132
  7.2 11.0 %copy-start.4 = (s32[16,32]{1,0:T(8,128)S(1)}, s32[16,32]{1,0:T(8,128)}, u32[]{:S(2)}) copy-start(s32[16,32]{1,0:T(8,128)} %param.22) | copy-start | bytes 6148
  10.4 26.2 %collective-permute-start = (bf16[2,256,1024]{2,1,0:T(8,128)(2,1)}, bf16[2,256,1024]{2,1,0:T(8,128)(2,1)S(1)}, u32[]{:S(2)}, u32[]{:S(2)}) collective-permute-start(bf16[2,256,1024]{2,1,0:T(8,128)(2,1)} %get-tuple-element.27), channel_id=1, source_target_pairs={{0,8},{8,16},{16,24},{24,32},{32,40},{40,48},{48,56},{56,64},{64,7... | collective-permute-start | bytes 3145736 | tf_op jit(solution)/shard_map/ppermute | solution.py:195
  14.0 26.8 %collective-permute-start.1 = (bf16[2,256,1024]{2,1,0:T(8,128)(2,1)}, bf16[2,256,1024]{2,1,0:T(8,128)(2,1)}, u32[]{:S(2)}, u32[]{:S(2)}) collective-permute-start(bf16[2,256,1024]{2,1,0:T(8,128)(2,1)} %get-tuple-element.26), channel_id=1, source_target_pairs={{8,0},{16,8},{24,16},{32,24},{40,32},{48,40},{56,48},{64,56},{72,6... | collective-permute-start | bytes 3145736 | tf_op jit(solution)/shard_map/ppermute | solution.py:196
  17.4 3.5 %copy-start.2 = (bf16[4096,512]{1,0:T(8,128)(2,1)S(1)}, bf16[4096,512]{1,0:T(8,128)(2,1)}, u32[]{:S(2)}) copy-start(bf16[4096,512]{1,0:T(8,128)(2,1)} %param.24) | copy-start | bytes 12582916
  18.0 3.8 %copy-start.6 = (bf16[1024,1024]{1,0:T(8,128)(2,1)S(1)}, bf16[1024,1024]{1,0:T(8,128)(2,1)}, u32[]{:S(2)}) copy-start(bf16[1024,1024]{1,0:T(8,128)(2,1)} %param.18) | copy-start | bytes 6291460
  18.0 4.2 %copy-start.7 = (bf16[1024,1024]{1,0:T(8,128)(2,1)S(1)}, bf16[1024,1024]{1,0:T(8,128)(2,1)}, u32[]{:S(2)}) copy-start(bf16[1024,1024]{1,0:T(8,128)(2,1)} %param.20) | copy-start | bytes 6291460
  22.1 20.4 %copy-start.8 = (bf16[1024,1024]{1,0:T(8,128)(2,1)S(1)}, bf16[1024,1024]{1,0:T(8,128)(2,1)}, u32[]{:S(2)}) copy-start(bf16[1024,1024]{1,0:T(8,128)(2,1)} %param.19) | copy-start | bytes 6291460
  50.1 48.2 %copy-start.9 = (bf16[1024,512]{1,0:T(8,128)(2,1)S(1)}, bf16[1024,512]{1,0:T(8,128)(2,1)}, u32[]{:S(2)}) copy-start(bf16[1024,512]{1,0:T(8,128)(2,1)} %param.26) | copy-start | bytes 3145732
  50.1 48.2 %copy-start.10 = (bf16[1024,512]{1,0:T(8,128)(2,1)S(1)}, bf16[1024,512]{1,0:T(8,128)(2,1)}, u32[]{:S(2)}) copy-start(bf16[1024,512]{1,0:T(8,128)(2,1)} %param.25) | copy-start | bytes 3145732
  100.0 21.3 %all-to-all-start = ((bf16[16,16,1152]{2,1,0:T(8,128)(2,1)}), bf16[16,16,1152]{2,1,0:T(8,128)(2,1)S(1)}, u32[]{:S(2)}, u32[]{:S(2)}) async-start(bf16[16,16,1152]{2,1,0:T(8,128)(2,1)} %fusion.30), calls=%async_computation | async-start | bytes 1179648 | tf_op jit(solution)/shard_map/all_to_all | solution.py:244
  108.5 76.8 %reduce-scatter.2.cloned.1.call-start = ((), (), s32[]{:S(2)}) async-start(), calls=%async_computation.3 | async-start | bytes 4718592 | tf_op jit(solution)/shard_map/reduce_scatter | solution.py:274
  121.2 3.1 %copy-start.1 = (bf16[16,16,1152]{2,1,0:T(8,128)(2,1)}, bf16[16,16,1152]{2,1,0:T(8,128)(2,1)S(1)}, u32[]{:S(2)}) copy-start(bf16[16,16,1152]{2,1,0:T(8,128)(2,1)S(1)} %all-to-all-done) | copy-start | bytes 1769476
Sparse Core Ops, SparseCore 0:
  149.7 35.4 reduce-scatter.1

commit v13 on v12

--- a/solution.py
+++ b/solution.py
@@ -256,13 +256,9 @@
     heads_here = local_width // dec_head
     share_width = dec_width // lax.axis_size("head")
     vocab = embedding.shape[0]
-    onehot = (
-        token_ids[:, :, None] == jnp.arange(vocab, dtype=jnp.int32)[None, None, :]
-    ).astype(jnp.bfloat16)
     own_table = lax.dynamic_slice_in_dim(embedding, head_pos * share_width, share_width, 1)
-    own_part = jnp.einsum(
-        "stv,vd->std", onehot, own_table, preferred_element_type=jnp.float32
-    ).astype(jnp.bfloat16)
+    own_part = jnp.take(own_table, token_ids, axis=0)
+    own_part, received = lax.optimization_barrier((own_part, received))
     query_one = jnp.take(query_table, ids_one[0], axis=0)[None]
     mem_bias = jnp.where(mem_valid, pooled_bias, masked_score)[:, None, :]
     context_one = cross_attention(query_one, received, mem_bias, heads_here, dec_head)

time: 195 us -> 197 us (1.010)
  waiting for transfers between devices: 53.6 us -> 49 us
  matrix products: 28.3 us -> 32 us
    ppermute x1, waiting for transfers between devices: 4.11 us -> 0.01 us  [per_device(): low_edge = lax.ppermute(spectra[:, bin_dev - half_span:], 'seq', forward)]
    gather x0 -> x1, local copies, waits for them, and re-layouts: none -> 2.19 us  [per_device(): own_part = jnp.take(own_table, token_ids, axis=0)]
    dot_general x1 -> x0, matrix products: 2.19 us -> none  [per_device(): jnp.einsum('stv,vd->std', onehot, own_table, preferred_element_type=jnp.f...]
    dot_general x1, matrix products: 0.86 us -> 3.05 us  [per_device(): jnp.einsum('vd,de->ve', rms_rows(embedding), dec_query, preferred_element...]
    dot_general x1, matrix products: 10.4 us -> 12.4 us  [per_device(): jnp.einsum('sbd,de->sbe', normed, qkv_weights, preferred_element_type=jnp...]
    convert_element_type x0 -> x1, other arithmetic: none -> 1.99 us  [per_device(): decoded = (own_part.astype(jnp.float32) + summed).astype(jnp.bfloat16)]
  transfers between devices with their start and end apart: 4 -> 4, of which waited for: 4 -> 3; matrix products, arithmetic and copies ran while one was open for 10% -> 13% of each run, Pallas kernels for 0% -> 0%
where the time goes in v13:
time: 197 us; the launch traced here: 196 us
  waiting for transfers between devices  49 us (25%)
  Pallas kernels  37.5 us (19%)
  matrix products  32 us (16%)
  blocking collectives  29 us (15%)
  between operations  14.3 us (7%)
  starting transfers between devices  13.4 us (7%)
  other arithmetic  12.2 us (6%)
  local copies, waits for them, and re-layouts  8.48 us (4%)
    reduce_scatter x1, waiting for transfers between devices, per_device(): lax.psum_scatter(partial_sums.astype(jnp.bfloat16), 'head', scatter_dimen...  35.7 us
    pallas_call x1, Pallas kernels, band_attention(): pl.pallas_call(band_kernel, out_shape=(jax.ShapeDtypeStruct((spec_dev, bi...  33.3 us
    all_gather x1, blocking collectives, per_device(): spectra_all = lax.all_gather(pooled, 'head', axis=0, tiled=True)  14.5 us
    all_to_all x1, blocking collectives, per_device(): dec_context = lax.all_to_all(context_one, 'seq', 0, 0, tiled=True)  14.4 us
    dot_general x1, matrix products, per_device(): jnp.einsum('sbd,de->sbe', normed, qkv_weights, preferred_element_type=jnp...  12.4 us
    all_to_all x1, waiting for transfers between devices, per_device(): received = lax.all_to_all(payload, 'seq', 0, 1, tiled=True)  10.3 us
    dot_general x1, matrix products, per_device(): jnp.einsum('sbd,de->sbe', edges, kv_weights, preferred_element_type=jnp.f...  8.1 us
    all_to_all x1, starting transfers between devices, per_device(): received = lax.all_to_all(payload, 'seq', 0, 1, tiled=True)  7.63 us
  transfers between devices with their start and end apart: 4, of which 3 were waited for; matrix products, arithmetic and copies ran while one was open for 13% of the time, Pallas kernels for 0%

profile of v13, /device:TPU:0, one launch (start us, length us, event | category | flops | bytes accessed | tf_op | source)
XLA Modules:
  0.0 195.9 jit_solution(14959967993554147573)
XLA Ops:
  7.2 0.0 copy-start
  7.2 0.0 copy-start.5
  7.2 0.0 copy-start.3
  7.2 0.0 copy-start.2
  7.2 0.0 copy-start.4
  7.2 3.2 %fusion.39 = (bf16[2,256,1024]{2,1,0:T(8,128)(2,1)}, bf16[2,256,1024]{2,1,0:T(8,128)(2,1)}) fusion(bf16[2,512,1024]{2,1,0:T(8,128)(2,1)} %sp_ref.1), kind=kLoop, calls=%fused_computation.87 | loop fusion | bytes 4194304 | tf_op jit(solution)/shard_map/slice | solution.py:196
  10.4 4.4 %collective-permute-start = (bf16[2,256,1024]{2,1,0:T(8,128)(2,1)}, bf16[2,256,1024]{2,1,0:T(8,128)(2,1)}, u32[]{:S(2)}, u32[]{:S(2)}) collective-permute-start(bf16[2,256,1024]{2,1,0:T(8,128)(2,1)} %get-tuple-element.31), channel_id=1, source_target_pairs={{0,8},{8,16},{16,24},{24,32},{32,40},{40,48},{48,56},{56,64},{64,7... | collective-permute-start | bytes 3145736 | tf_op jit(solution)/shard_map/ppermute | solution.py:195
  14.9 1.3 collective-permute-start.1
  16.2 0.0 copy-done.5
  16.2 0.7 broadcast_subtract_fusion
  16.9 0.0 copy-done.3
  16.9 0.1 and_select_fusion
  17.0 0.0 copy-done
  17.0 0.5 fusion.6
  17.5 0.1 dynamic-slice_reduce_fusion
  17.6 0.6 dynamic_slice.18
  18.2 0.1 iota_add_fusion.1
  18.3 0.2 fusion.32
  18.5 0.3 fusion.26
  18.8 0.0 copy-done.2
  18.8 0.2 fusion.28
  19.0 0.0 copy-done.4
  19.1 0.1 reshape.264
  19.2 0.1 reshape.258
  19.3 1.1 broadcast_select_fusion.1.be_ref
  20.3 1.6 broadcast_select_fusion.bm_ref
  21.9 3.0 %convolution_convert_fusion.1 = bf16[28,512]{1,0:T(8,128)(2,1)S(1)} fusion(bf16[4096,512]{1,0:T(8,128)(2,1)} %param.24, bf16[28,4096]{1,0:T(8,128)(2,1)S(1)} %copy-done.2, f32[28]{0:T(128)S(1)} %add_rsqrt_fusion.3), kind=kOutput, calls=%fused_computation.38 | convolution fusion | flops 117798912 | bytes 4452464 | tf_op jit(solution)/shard_map/vd,de->ve/dot_general | solution.py:202
  25.0 0.1 reduce_max.11
  25.1 1.2 compare_select_fusion.3.b_ref
  26.3 0.0 copy-start.6
  26.3 0.0 copy-start.7
  26.3 12.4 %fusion.5.q_ref.km_ref.vm_ref = bf16[2,512,3072]{2,1,0:T(8,128)(2,1)} fusion(bf16[1024,1024]{1,0:T(8,128)(2,1)} %param.20, bf16[1024,1024]{1,0:T(8,128)(2,1)} %param.19, bf16[1024,1024]{1,0:T(8,128)(2,1)} %param.18, bf16[2,512,1024]{2,1,0:T(8,128)(2,1)S(1)} %copy-done, f32[2,512]{1,0:T(2,128)S(1)} %add_rsqrt_fusion.2), kind=kOutput, calls=%fused_computation.9 | convolution fusion | flops 6467616768 | bytes 14684160 | tf_op jit(solution)/shard_map/sbd,de->sbe/dot_general | solution.py:199
  38.7 0.0 collective-permute-done
  38.7 3.0 %collective-permute-done.1 = bf16[2,256,1024]{2,1,0:T(8,128)(2,1)} collective-permute-done((bf16[2,256,1024]{2,1,0:T(8,128)(2,1)}, bf16[2,256,1024]{2,1,0:T(8,128)(2,1)}, u32[]{:S(2)}, u32[]{:S(2)}) %collective-permute-start.1) | collective-permute-done | bytes 1048608 | tf_op jit(solution)/shard_map/ppermute | solution.py:196
  41.7 2.0 %fusion.8 = f32[2,512]{1,0:T(2,128)S(1)} fusion(bf16[2,256,1024]{2,1,0:T(8,128)(2,1)} %collective-permute-done.1, bf16[2,256,1024]{2,1,0:T(8,128)(2,1)} %collective-permute-done), kind=kLoop, calls=%fused_computation.16 | loop fusion | flops 6290432 | bytes 2101248 | tf_op jit(solution)/shard_map/reduce_sum | solution.py:23
  43.7 0.0 copy-done.6
  43.8 0.0 copy-done.7
  43.8 8.1 %fusion.14.ke_ref.ve_ref = bf16[2,512,2048]{2,1,0:T(8,128)(2,1)} fusion(bf16[1024,1024]{1,0:T(8,128)(2,1)S(1)} %copy-done.6, bf16[1024,1024]{1,0:T(8,128)(2,1)S(1)} %copy-done.7, f32[2,512]{1,0:T(2,128)S(1)} %add_rsqrt_fusion.1, bf16[2,256,1024]{2,1,0:T(8,128)(2,1)} %collective-permute-done.1, bf16[2,256,1024]{2,1,0:T(8,128)(2,1)} %collective-permute-done), kind=kOutput, calls=%fused_computation.23 | convolution fusion | flops 4311744512 | bytes 10489856 | tf_op jit(solution)/shard_map/sbd,de->sbe/dot_general | solution.py:209
  51.9 0.0 copy-start.8
  51.9 33.3 %shard_map.140 = (bf16[2,512,1024]{2,1,0:T(8,128)(2,1)}, bf16[2,16,1024]{2,1,0:T(8,128)(2,1)}) custom-call(bf16[2,512,3072]{2,1,0:T(8,128)(2,1)} %fusion.5.q_ref.km_ref.vm_ref, bf16[2,512,3072]{2,1,0:T(8,128)(2,1)} %fusion.5.q_ref.km_ref.vm_ref, bf16[2,512,3072]{2,1,0:T(8,128)(2,1)} %fusion.5.q_ref.km_ref.vm_ref, ...), custom_call_target="tpu_custom_call" | custom-call | flops 8589934592 | bytes 19922944 | tf_op jit(solution)/shard_map/pallas_call | solution.py:92
  85.1 14.5 %all_gather.3 = bf16[16,16,1024]{2,1,0:T(8,128)(2,1)S(1)} all-gather(bf16[2,16,1024]{2,1,0:T(8,128)(2,1)} %get-tuple-element.24), channel_id=1, replica_groups=mesh['seq'=16,'head'=8] {'head'}, dimensions={0}, use_global_device_ids=true | all-gather | bytes 589824 | tf_op jit(solution)/shard_map/all_gather | solution.py:233
  99.7 0.2 fusion.24
  99.9 0.0 copy-done.8
  99.9 2.0 %fusion.22 = bf16[16,16,1024]{2,1,0:T(8,128)(2,1)S(1)} fusion(bf16[1024,512]{1,0:T(8,128)(2,1)S(1)} %copy-done.8, bf16[1024,512]{1,0:T(8,128)(2,1)} %param.25, bf16[16,16,1024]{2,1,0:T(8,128)(2,1)S(1)} %all_gather.3, f32[16,16]{1,0:T(8,128)S(1)} %add_rsqrt_fusion), kind=kOutput, calls=%fused_computation.35 | convolution fusion | flops 542113792 | bytes 3146752 | tf_op jit(solution)/shard_map/spd,de->spe/dot_general | solution.py:236
  101.9 0.9 fusion.27
  102.7 7.6 %all-to-all-start = ((bf16[16,16,1152]{2,1,0:T(8,128)(2,1)}), bf16[16,16,1152]{2,1,0:T(8,128)(2,1)S(1)}, u32[]{:S(2)}, u32[]{:S(2)}) async-start(bf16[16,16,1152]{2,1,0:T(8,128)(2,1)} %fusion.27), calls=%async_computation | async-start | bytes 1179648 | tf_op jit(solution)/shard_map/all_to_all | solution.py:244
  110.4 0.0 reduce-scatter.2.cloned.1.call-start
  110.4 2.2 %gather_fusion = bf16[512,512]{1,0:T(8,128)(2,1)S(1)} fusion(bf16[28,512]{1,0:T(8,128)(2,1)S(1)} %constant_dynamic-slice_fusion, s32[1024]{0:T(1024)S(1)} %pad_clamp_fusion.1), kind=kCustom, calls=%fused_computation | custom fusion | bytes 1050624 | tf_op jit(solution)/shard_map/jit(_take)/gather | solution.py:260
  112.6 0.1 broadcast_select_fusion.2
  112.8 10.3 %all-to-all-done = bf16[16,16,1152]{2,1,0:T(8,128)(2,1)S(1)} async-done(((bf16[16,16,1152]{2,1,0:T(8,128)(2,1)}), bf16[16,16,1152]{2,1,0:T(8,128)(2,1)S(1)}, u32[]{:S(2)}, u32[]{:S(2)}) %all-to-all-start) | async-done | bytes 589856 | tf_op jit(solution)/shard_map/all_to_all | solution.py:244
  123.1 0.0 copy-start.1
  123.1 0.1 reshape.261
  123.2 0.1 reshape.260
  123.3 2.0 %gather_fusion.1 = bf16[512,512]{1,0:T(8,128)(2,1)S(1)} fusion(bf16[28,512]{1,0:T(8,128)(2,1)S(1)} %convolution_convert_fusion.1, s32[1024]{0:T(1024)S(1)} %pad_clamp_fusion), kind=kCustom, calls=%fused_computation.1 | custom fusion | bytes 1050624 | tf_op jit(solution)/shard_map/jit(_take)/gather | solution.py:262
  125.3 0.9 bitcast_select_fusion.q_ref
  126.2 0.0 copy-done.1
  126.2 4.2 %shard_map.141 = bf16[1,512,512]{2,1,0:T(8,128)(2,1)} custom-call(bf16[1,512,512]{2,1,0:T(8,128)(2,1)} %bitcast_select_fusion.q_ref, bf16[1,256,1152]{2,1,0:T(8,128)(2,1)} %bitcast.31, bf16[1,256,1152]{2,1,0:T(8,128)(2,1)} %bitcast.32, f32[1,1,256]{2,1,0:T(1,128)} %compare_select_fusion.3.b_ref), custom_call_target="tpu_custom_call" | custom-call | flops 268435456 | bytes 1572864 | tf_op jit(solution)/shard_map/pallas_call | solution.py:144
  130.5 14.4 %all_to_all.17 = bf16[16,32,512]{2,1,0:T(8,128)(2,1)S(1)} all-to-all(bf16[16,32,512]{2,1,0:T(8,128)(2,1)} %bitcast.34), channel_id=1, replica_groups=mesh['seq'=16,'head'=8] {'seq'}, dimensions={0} | all-to-all | bytes 1048576 | tf_op jit(solution)/shard_map/all_to_all | solution.py:266
  144.9 6.5 %convolution_convert_fusion = bf16[16,32,4096]{2,1,0:T(8,128)(2,1)} fusion(bf16[16,32,512]{2,1,0:T(8,128)(2,1)S(1)} %all_to_all.17, bf16[512,4096]{1,0:T(8,128)(2,1)} %param.27), kind=kOutput, calls=%fused_computation.8 | convolution fusion | flops 2149580800 | bytes 8912896 | tf_op jit(solution)/shard_map/ste,ed->std/dot_general | solution.py:267
  151.4 0.0 reduce-scatter.2.cloned.1.call-update
  151.4 35.7 %reduce-scatter.2.cloned.1.call-done = bf16[16,32,512]{2,1,0:T(8,128)(2,1)} async-done(((bf16[16,32,4096]{2,1,0:T(8,128)(2,1)}), bf16[16,32,512]{2,1,0:T(8,128)(2,1)}) %reduce-scatter.2.cloned.1.call-update) | async-done | bytes 524304 | tf_op jit(solution)/shard_map/reduce_scatter | solution.py:270
  187.1 2.0 %add_convert_fusion = bf16[16,32,512]{2,1,0:T(8,128)(2,1)} fusion(bf16[16,32,512]{2,1,0:T(8,128)(2,1)} %reduce-scatter.2.cloned.1.call-done, bf16[16,32,512]{2,1,0:T(8,128)(2,1)S(1)} %broadcast_select_fusion.2), kind=kLoop, calls=%fused_computation.41 | loop fusion | flops 1048576 | bytes 1572864 | tf_op jit(solution)/shard_map/convert_element_type | solution.py:273
  (22 shorter events, 0.2 us)
Async XLA Ops:
  7.2 9.9 %copy-start = (bf16[2,512,1024]{2,1,0:T(8,128)(2,1)S(1)}, bf16[2,512,1024]{2,1,0:T(8,128)(2,1)}, u32[]{:S(2)}) copy-start(bf16[2,512,1024]{2,1,0:T(8,128)(2,1)} %sp_ref.1) | copy-start | bytes 6291460
  7.2 9.1 %copy-start.5 = (s32[16]{0:T(128)S(1)}, s32[16]{0:T(128)}, u32[]{:S(2)}) copy-start(s32[16]{0:T(128)} %param.17) | copy-start | bytes 196
  7.2 9.7 %copy-start.3 = (f32[16,8192]{1,0:T(8,128)S(1)}, f32[16,8192]{1,0:T(8,128)}, u32[]{:S(2)}) copy-start(f32[16,8192]{1,0:T(8,128)} %param.16) | copy-start | bytes 1572868
  7.2 11.6 %copy-start.2 = (bf16[28,4096]{1,0:T(8,128)(2,1)S(1)}, bf16[28,4096]{1,0:T(8,128)(2,1)}, u32[]{:S(2)}) copy-start(bf16[28,4096]{1,0:T(8,128)(2,1)} %param.23) | copy-start | bytes 688132
  7.2 11.8 %copy-start.4 = (s32[16,32]{1,0:T(8,128)S(1)}, s32[16,32]{1,0:T(8,128)}, u32[]{:S(2)}) copy-start(s32[16,32]{1,0:T(8,128)} %param.22) | copy-start | bytes 6148
  10.4 28.3 %collective-permute-start = (bf16[2,256,1024]{2,1,0:T(8,128)(2,1)}, bf16[2,256,1024]{2,1,0:T(8,128)(2,1)}, u32[]{:S(2)}, u32[]{:S(2)}) collective-permute-start(bf16[2,256,1024]{2,1,0:T(8,128)(2,1)} %get-tuple-element.31), channel_id=1, source_target_pairs={{0,8},{8,16},{16,24},{24,32},{32,40},{40,48},{48,56},{56,64},{64,7... | collective-permute-start | bytes 3145736 | tf_op jit(solution)/shard_map/ppermute | solution.py:195
  14.9 26.8 %collective-permute-start.1 = (bf16[2,256,1024]{2,1,0:T(8,128)(2,1)}, bf16[2,256,1024]{2,1,0:T(8,128)(2,1)}, u32[]{:S(2)}, u32[]{:S(2)}) collective-permute-start(bf16[2,256,1024]{2,1,0:T(8,128)(2,1)} %get-tuple-element.30), channel_id=1, source_target_pairs={{8,0},{16,8},{24,16},{32,24},{40,32},{48,40},{56,48},{64,56},{72,6... | collective-permute-start | bytes 3145736 | tf_op jit(solution)/shard_map/ppermute | solution.py:196
  26.3 17.4 %copy-start.6 = (bf16[1024,1024]{1,0:T(8,128)(2,1)S(1)}, bf16[1024,1024]{1,0:T(8,128)(2,1)}, u32[]{:S(2)}) copy-start(bf16[1024,1024]{1,0:T(8,128)(2,1)} %param.20) | copy-start | bytes 6291460
  26.3 17.5 %copy-start.7 = (bf16[1024,1024]{1,0:T(8,128)(2,1)S(1)}, bf16[1024,1024]{1,0:T(8,128)(2,1)}, u32[]{:S(2)}) copy-start(bf16[1024,1024]{1,0:T(8,128)(2,1)} %param.19) | copy-start | bytes 6291460
  51.9 48.0 %copy-start.8 = (bf16[1024,512]{1,0:T(8,128)(2,1)S(1)}, bf16[1024,512]{1,0:T(8,128)(2,1)}, u32[]{:S(2)}) copy-start(bf16[1024,512]{1,0:T(8,128)(2,1)} %param.26) | copy-start | bytes 3145732
  102.7 20.4 %all-to-all-start = ((bf16[16,16,1152]{2,1,0:T(8,128)(2,1)}), bf16[16,16,1152]{2,1,0:T(8,128)(2,1)S(1)}, u32[]{:S(2)}, u32[]{:S(2)}) async-start(bf16[16,16,1152]{2,1,0:T(8,128)(2,1)} %fusion.27), calls=%async_computation | async-start | bytes 1179648 | tf_op jit(solution)/shard_map/all_to_all | solution.py:244
  110.4 76.7 %reduce-scatter.2.cloned.1.call-start = ((), (), s32[]{:S(2)}) async-start(), calls=%async_computation.3 | async-start | bytes 4718592 | tf_op jit(solution)/shard_map/reduce_scatter | solution.py:270
  123.1 3.1 %copy-start.1 = (bf16[16,16,1152]{2,1,0:T(8,128)(2,1)}, bf16[16,16,1152]{2,1,0:T(8,128)(2,1)S(1)}, u32[]{:S(2)}) copy-start(bf16[16,16,1152]{2,1,0:T(8,128)(2,1)S(1)} %all-to-all-done) | copy-start | bytes 1769476
Sparse Core Ops, SparseCore 0:
  151.5 35.4 reduce-scatter.1

commit v14 on v12

--- a/solution.py
+++ b/solution.py
@@ -202,8 +202,9 @@
     query_table = jnp.einsum(
         "vd,de->ve", rms_rows(embedding), dec_query, preferred_element_type=jnp.float32
     ).astype(jnp.bfloat16)
-    query_table, low_edge, high_edge = lax.optimization_barrier(
-        (query_table, low_edge, high_edge)
+    mem_weights = jnp.concatenate([mem_key, mem_value], axis=1)
+    query_table, mem_weights, low_edge, high_edge = lax.optimization_barrier(
+        (query_table, mem_weights, low_edge, high_edge)
     )
     edges = rms_rows(jnp.concatenate([low_edge, high_edge], axis=1))
     keyval_edges = jnp.einsum(
@@ -231,7 +232,6 @@
         qkv, keyval_edges, bias_mid, bias_edge, enc_out, spectra, row_limit
     )
     spectra_all = lax.all_gather(pooled, "head", axis=0, tiled=True)
-    mem_weights = jnp.concatenate([mem_key, mem_value], axis=1)
     local_width = mem_key.shape[1]
     memory_part = jnp.einsum(
         "spd,de->spe", rms_rows(spectra_all), mem_weights, preferred_element_type=jnp.float32

time: 195 us -> 195 us (level)
  no operation moved by 1% of the time
where the time goes in v14:
time: 195 us; the launch traced here: 194 us
  waiting for transfers between devices  52.6 us (27%)
  Pallas kernels  37.7 us (19%)
  blocking collectives  29 us (15%)
  matrix products  26.8 us (14%)
  between operations  14.3 us (7%)
  starting transfers between devices  13.4 us (7%)
  other arithmetic  12.1 us (6%)
  local copies, waits for them, and re-layouts  8.31 us (4%)
    reduce_scatter x1, waiting for transfers between devices, per_device(): lax.psum_scatter(partial_sums.astype(jnp.bfloat16), 'head', scatter_dimen...  35.6 us
    pallas_call x1, Pallas kernels, band_attention(): pl.pallas_call(band_kernel, out_shape=(jax.ShapeDtypeStruct((spec_dev, bi...  33.5 us
    all_gather x1, blocking collectives, per_device(): spectra_all = lax.all_gather(pooled, 'head', axis=0, tiled=True)  14.5 us
    all_to_all x1, blocking collectives, per_device(): dec_context = lax.all_to_all(context_one, 'seq', 0, 0, tiled=True)  14.4 us
    all_to_all x1, waiting for transfers between devices, per_device(): received = lax.all_to_all(payload, 'seq', 0, 1, tiled=True)  9.62 us
    dot_general x1, matrix products, per_device(): jnp.einsum('sbd,de->sbe', normed, qkv_weights, preferred_element_type=jnp...  8.92 us
    all_to_all x1, starting transfers between devices, per_device(): received = lax.all_to_all(payload, 'seq', 0, 1, tiled=True)  8.5 us
    dot_general x1, matrix products, per_device(): jnp.einsum('sbd,de->sbe', edges, kv_weights, preferred_element_type=jnp.f...  7.57 us
  transfers between devices with their start and end apart: 4, of which 4 were waited for; matrix products, arithmetic and copies ran while one was open for 10% of the time, Pallas kernels for 0%

profile of v14, /device:TPU:0, one launch (start us, length us, event | category | flops | bytes accessed | tf_op | source)
XLA Modules:
  0.0 194.2 jit_solution(9059965298901408472)
XLA Ops:
  7.2 0.0 copy-start
  7.2 0.0 copy-start.8
  7.2 0.0 copy-start.4
  7.2 0.0 copy-start.7
  7.2 3.2 %fusion.46 = (bf16[2,256,1024]{2,1,0:T(8,128)(2,1)}, bf16[2,256,1024]{2,1,0:T(8,128)(2,1)}) fusion(bf16[2,512,1024]{2,1,0:T(8,128)(2,1)} %sp_ref.1), kind=kLoop, calls=%fused_computation.87 | loop fusion | bytes 4194304 | tf_op jit(solution)/shard_map/slice | solution.py:196
  10.4 3.5 %collective-permute-start = (bf16[2,256,1024]{2,1,0:T(8,128)(2,1)}, bf16[2,256,1024]{2,1,0:T(8,128)(2,1)S(1)}, u32[]{:S(2)}, u32[]{:S(2)}) collective-permute-start(bf16[2,256,1024]{2,1,0:T(8,128)(2,1)} %get-tuple-element.29), channel_id=1, source_target_pairs={{0,8},{8,16},{16,24},{24,32},{32,40},{40,48},{48,56},{56,64},{64,7... | collective-permute-start | bytes 3145736 | tf_op jit(solution)/shard_map/ppermute | solution.py:195
  14.0 1.3 collective-permute-start.1
  15.3 0.0 copy-done.8
  15.3 0.6 broadcast_subtract_fusion
  15.9 0.8 and_select_fusion
  16.8 0.0 copy-done
  16.8 0.5 fusion.6
  17.3 0.0 copy-start.5
  17.3 0.0 copy-start.6
  17.3 0.1 iota_add_fusion.1
  17.4 0.0 copy-start.2
  17.4 0.2 fusion.36
  17.6 0.3 fusion.30
  17.9 0.0 copy-done.4
  17.9 0.2 fusion.32
  18.1 0.0 copy-done.7
  18.1 1.1 broadcast_select_fusion.1.be_ref
  19.2 1.7 broadcast_select_fusion.bm_ref
  20.9 0.0 copy-done.5
  20.9 0.0 copy-done.6
  20.9 0.0 copy-start.9
  20.9 0.0 copy-start.10
  20.9 0.0 copy-start.11
  20.9 1.6 pad_maximum_fusion
  22.5 0.0 copy-done.2
  22.5 0.9 convolution_convert_fusion.2
  23.3 0.0 copy-done.9
  23.4 0.5 copy-done.10
  23.9 0.6 copy-done.11
  24.5 8.9 %fusion.5.q_ref.km_ref.vm_ref = bf16[2,512,3072]{2,1,0:T(8,128)(2,1)} fusion(bf16[1024,1024]{1,0:T(8,128)(2,1)S(1)} %copy-done.10, bf16[1024,1024]{1,0:T(8,128)(2,1)S(1)} %copy-done.11, bf16[1024,1024]{1,0:T(8,128)(2,1)S(1)} %copy-done.9, bf16[2,512,1024]{2,1,0:T(8,128)(2,1)S(1)} %copy-done, f32[2,512]{1,0:T(2,128)S(1)} %add_rsqrt_fusion.2), kind=kOutput, calls=%fused_computation.8 | convolution fusion | flops 6467616768 | bytes 14684160 | tf_op jit(solution)/shard_map/sbd,de->sbe/dot_general | solution.py:199
  33.4 3.2 %collective-permute-done = bf16[2,256,1024]{2,1,0:T(8,128)(2,1)S(1)} collective-permute-done((bf16[2,256,1024]{2,1,0:T(8,128)(2,1)}, bf16[2,256,1024]{2,1,0:T(8,128)(2,1)S(1)}, u32[]{:S(2)}, u32[]{:S(2)}) %collective-permute-start) | collective-permute-done | bytes 1048608 | tf_op jit(solution)/shard_map/ppermute | solution.py:195
  36.6 4.2 %collective-permute-done.1 = bf16[2,256,1024]{2,1,0:T(8,128)(2,1)} collective-permute-done((bf16[2,256,1024]{2,1,0:T(8,128)(2,1)}, bf16[2,256,1024]{2,1,0:T(8,128)(2,1)}, u32[]{:S(2)}, u32[]{:S(2)}) %collective-permute-start.1) | collective-permute-done | bytes 1048608 | tf_op jit(solution)/shard_map/ppermute | solution.py:196
  40.8 1.7 fusion.8
  42.5 7.6 %fusion.14.ke_ref.ve_ref = bf16[2,512,2048]{2,1,0:T(8,128)(2,1)} fusion(bf16[1024,1024]{1,0:T(8,128)(2,1)S(1)} %copy-done.10, bf16[1024,1024]{1,0:T(8,128)(2,1)S(1)} %copy-done.11, f32[2,512]{1,0:T(2,128)S(1)} %add_rsqrt_fusion.1, bf16[2,256,1024]{2,1,0:T(8,128)(2,1)} %collective-permute-done.1, bf16[2,256,1024]{2,1,0:T(8,128)(2,1)S(1)} %collective-permute-done), kind=kOutput, calls=%fused_computation.22 | convolution fusion | flops 4311744512 | bytes 10489856 | tf_op jit(solution)/shard_map/sbd,de->sbe/dot_general | solution.py:210
  50.1 33.5 %shard_map.140 = (bf16[2,512,1024]{2,1,0:T(8,128)(2,1)}, bf16[2,16,1024]{2,1,0:T(8,128)(2,1)}) custom-call(bf16[2,512,3072]{2,1,0:T(8,128)(2,1)} %fusion.5.q_ref.km_ref.vm_ref, bf16[2,512,3072]{2,1,0:T(8,128)(2,1)} %fusion.5.q_ref.km_ref.vm_ref, bf16[2,512,3072]{2,1,0:T(8,128)(2,1)} %fusion.5.q_ref.km_ref.vm_ref, ...), custom_call_target="tpu_custom_call" | custom-call | flops 8589934592 | bytes 19922944 | tf_op jit(solution)/shard_map/pallas_call | solution.py:92
  83.6 14.5 %all_gather.3 = bf16[16,16,1024]{2,1,0:T(8,128)(2,1)S(1)} all-gather(bf16[2,16,1024]{2,1,0:T(8,128)(2,1)} %get-tuple-element.23), channel_id=1, replica_groups=mesh['seq'=16,'head'=8] {'head'}, dimensions={0}, use_global_device_ids=true | all-gather | bytes 589824 | tf_op jit(solution)/shard_map/all_gather | solution.py:234
  98.1 0.2 fusion.28
  98.3 0.0 copy-done.3
  98.3 0.8 fusion.21
  99.1 0.9 fusion.31
  99.9 8.5 %all-to-all-start = ((bf16[16,16,1152]{2,1,0:T(8,128)(2,1)}), bf16[16,16,1152]{2,1,0:T(8,128)(2,1)S(1)}, u32[]{:S(2)}, u32[]{:S(2)}) async-start(bf16[16,16,1152]{2,1,0:T(8,128)(2,1)} %fusion.31), calls=%async_computation | async-start | bytes 1179648 | tf_op jit(solution)/shard_map/all_to_all | solution.py:244
  108.4 0.0 reduce-scatter.2.cloned.1.call-start
  108.5 0.6 dynamic_slice.18
  109.1 1.0 dynamic-slice_reduce_fusion
  110.1 0.1 reshape.255
  110.2 0.1 reduce_max.11
  110.3 1.2 compare_select_fusion.2.b_ref
  111.6 9.6 %all-to-all-done = bf16[16,16,1152]{2,1,0:T(8,128)(2,1)S(1)} async-done(((bf16[16,16,1152]{2,1,0:T(8,128)(2,1)}), bf16[16,16,1152]{2,1,0:T(8,128)(2,1)S(1)}, u32[]{:S(2)}, u32[]{:S(2)}) %all-to-all-start) | async-done | bytes 589856 | tf_op jit(solution)/shard_map/all_to_all | solution.py:244
  121.2 0.1 reshape.258
  121.3 0.1 reshape.257
  121.4 2.0 %gather_fusion = bf16[512,512]{1,0:T(8,128)(2,1)S(1)} fusion(bf16[28,512]{1,0:T(8,128)(2,1)S(1)} %convolution_convert_fusion.2, s32[1024]{0:T(1024)S(1)} %pad_clamp_fusion), kind=kCustom, calls=%fused_computation | custom fusion | bytes 1050624 | tf_op jit(solution)/shard_map/jit(_take)/gather | solution.py:266
  123.4 0.9 bitcast_select_fusion.q_ref
  124.3 0.0 copy-done.1
  124.3 4.2 %shard_map.141 = bf16[1,512,512]{2,1,0:T(8,128)(2,1)} custom-call(bf16[1,512,512]{2,1,0:T(8,128)(2,1)} %bitcast_select_fusion.q_ref, bf16[1,256,1152]{2,1,0:T(8,128)(2,1)} %bitcast.33, bf16[1,256,1152]{2,1,0:T(8,128)(2,1)} %bitcast.34, f32[1,1,256]{2,1,0:T(1,128)} %compare_select_fusion.2.b_ref), custom_call_target="tpu_custom_call" | custom-call | flops 268435456 | bytes 1572864 | tf_op jit(solution)/shard_map/pallas_call | solution.py:144
  128.6 14.4 %all_to_all.17 = bf16[16,32,512]{2,1,0:T(8,128)(2,1)S(1)} all-to-all(bf16[16,32,512]{2,1,0:T(8,128)(2,1)} %bitcast.35), channel_id=1, replica_groups=mesh['seq'=16,'head'=8] {'seq'}, dimensions={0} | all-to-all | bytes 1048576 | tf_op jit(solution)/shard_map/all_to_all | solution.py:270
  143.0 6.5 %convolution_convert_fusion = bf16[16,32,4096]{2,1,0:T(8,128)(2,1)} fusion(bf16[16,32,512]{2,1,0:T(8,128)(2,1)S(1)} %all_to_all.17, bf16[512,4096]{1,0:T(8,128)(2,1)} %param.27), kind=kOutput, calls=%fused_computation.7 | convolution fusion | flops 2149580800 | bytes 8912896 | tf_op jit(solution)/shard_map/ste,ed->std/dot_general | solution.py:271
  149.5 0.0 reduce-scatter.2.cloned.1.call-update
  149.6 35.6 %reduce-scatter.2.cloned.1.call-done = bf16[16,32,512]{2,1,0:T(8,128)(2,1)} async-done(((bf16[16,32,4096]{2,1,0:T(8,128)(2,1)}), bf16[16,32,512]{2,1,0:T(8,128)(2,1)}) %reduce-scatter.2.cloned.1.call-update) | async-done | bytes 524304 | tf_op jit(solution)/shard_map/reduce_scatter | solution.py:274
  185.1 2.2 %fusion.26 = bf16[16,32,512]{2,1,0:T(8,128)(2,1)} fusion(bf16[16,32,512]{2,1,0:T(8,128)(2,1)} %reduce-scatter.2.cloned.1.call-done, s32[16,32]{1,0:T(8,128)S(1)} %copy-done.7, bf16[28,4096]{1,0:T(8,128)(2,1)S(1)} %copy-done.4, s32[]{:T(128)S(6)} %select_n.71), kind=kOutput, calls=%fused_computation.37 | convolution fusion | flops 16005120 | bytes 1089540 | tf_op jit(solution)/shard_map/stv,vd->std/dot_general | solution.py:263
  (21 shorter events, 0.2 us)
Async XLA Ops:
  7.2 9.6 %copy-start = (bf16[2,512,1024]{2,1,0:T(8,128)(2,1)S(1)}, bf16[2,512,1024]{2,1,0:T(8,128)(2,1)}, u32[]{:S(2)}) copy-start(bf16[2,512,1024]{2,1,0:T(8,128)(2,1)} %sp_ref.1) | copy-start | bytes 6291460
  7.2 8.2 %copy-start.8 = (s32[16]{0:T(128)S(1)}, s32[16]{0:T(128)}, u32[]{:S(2)}) copy-start(s32[16]{0:T(128)} %param.17) | copy-start | bytes 196
  7.2 10.7 %copy-start.4 = (bf16[28,4096]{1,0:T(8,128)(2,1)S(1)}, bf16[28,4096]{1,0:T(8,128)(2,1)}, u32[]{:S(2)}) copy-start(bf16[28,4096]{1,0:T(8,128)(2,1)} %param.23) | copy-start | bytes 688132
  7.2 10.9 %copy-start.7 = (s32[16,32]{1,0:T(8,128)S(1)}, s32[16,32]{1,0:T(8,128)}, u32[]{:S(2)}) copy-start(s32[16,32]{1,0:T(8,128)} %param.22) | copy-start | bytes 6148
  10.4 26.2 %collective-permute-start = (bf16[2,256,1024]{2,1,0:T(8,128)(2,1)}, bf16[2,256,1024]{2,1,0:T(8,128)(2,1)S(1)}, u32[]{:S(2)}, u32[]{:S(2)}) collective-permute-start(bf16[2,256,1024]{2,1,0:T(8,128)(2,1)} %get-tuple-element.29), channel_id=1, source_target_pairs={{0,8},{8,16},{16,24},{24,32},{32,40},{40,48},{48,56},{56,64},{64,7... | collective-permute-start | bytes 3145736 | tf_op jit(solution)/shard_map/ppermute | solution.py:195
  14.0 26.8 %collective-permute-start.1 = (bf16[2,256,1024]{2,1,0:T(8,128)(2,1)}, bf16[2,256,1024]{2,1,0:T(8,128)(2,1)}, u32[]{:S(2)}, u32[]{:S(2)}) collective-permute-start(bf16[2,256,1024]{2,1,0:T(8,128)(2,1)} %get-tuple-element.28), channel_id=1, source_target_pairs={{8,0},{16,8},{24,16},{32,24},{40,32},{48,40},{56,48},{64,56},{72,6... | collective-permute-start | bytes 3145736 | tf_op jit(solution)/shard_map/ppermute | solution.py:196
  17.3 3.6 %copy-start.5 = (bf16[1024,512]{1,0:T(8,128)(2,1)S(1)}, bf16[1024,512]{1,0:T(8,128)(2,1)}, u32[]{:S(2)}) copy-start(bf16[1024,512]{1,0:T(8,128)(2,1)} %param.26) | copy-start | bytes 3145732
  17.3 3.6 %copy-start.6 = (bf16[1024,512]{1,0:T(8,128)(2,1)S(1)}, bf16[1024,512]{1,0:T(8,128)(2,1)}, u32[]{:S(2)}) copy-start(bf16[1024,512]{1,0:T(8,128)(2,1)} %param.25) | copy-start | bytes 3145732
  17.4 5.1 %copy-start.2 = (bf16[4096,512]{1,0:T(8,128)(2,1)S(1)}, bf16[4096,512]{1,0:T(8,128)(2,1)}, u32[]{:S(2)}) copy-start(bf16[4096,512]{1,0:T(8,128)(2,1)} %param.24) | copy-start | bytes 12582916
  20.9 2.5 %copy-start.9 = (bf16[1024,1024]{1,0:T(8,128)(2,1)S(1)}, bf16[1024,1024]{1,0:T(8,128)(2,1)}, u32[]{:S(2)}) copy-start(bf16[1024,1024]{1,0:T(8,128)(2,1)} %param.18) | copy-start | bytes 6291460
  20.9 3.0 %copy-start.10 = (bf16[1024,1024]{1,0:T(8,128)(2,1)S(1)}, bf16[1024,1024]{1,0:T(8,128)(2,1)}, u32[]{:S(2)}) copy-start(bf16[1024,1024]{1,0:T(8,128)(2,1)} %param.20) | copy-start | bytes 6291460
  20.9 3.6 %copy-start.11 = (bf16[1024,1024]{1,0:T(8,128)(2,1)S(1)}, bf16[1024,1024]{1,0:T(8,128)(2,1)}, u32[]{:S(2)}) copy-start(bf16[1024,1024]{1,0:T(8,128)(2,1)} %param.19) | copy-start | bytes 6291460
  50.1 48.2 %copy-start.3 = (bf16[1024,1024]{1,0:T(8,128)(2,1)S(1)}, bf16[1024,1024]{1,0:T(8,128)(2,1)}, u32[]{:S(2)}) copy-start(bf16[1024,1024]{1,0:T(8,128)(2,1)} %pad_maximum_fusion) | copy-start | bytes 6291460
  99.9 21.3 %all-to-all-start = ((bf16[16,16,1152]{2,1,0:T(8,128)(2,1)}), bf16[16,16,1152]{2,1,0:T(8,128)(2,1)S(1)}, u32[]{:S(2)}, u32[]{:S(2)}) async-start(bf16[16,16,1152]{2,1,0:T(8,128)(2,1)} %fusion.31), calls=%async_computation | async-start | bytes 1179648 | tf_op jit(solution)/shard_map/all_to_all | solution.py:244
  108.4 76.7 %reduce-scatter.2.cloned.1.call-start = ((), (), s32[]{:S(2)}) async-start(), calls=%async_computation.3 | async-start | bytes 4718592 | tf_op jit(solution)/shard_map/reduce_scatter | solution.py:274
  121.2 3.1 %copy-start.1 = (bf16[16,16,1152]{2,1,0:T(8,128)(2,1)}, bf16[16,16,1152]{2,1,0:T(8,128)(2,1)S(1)}, u32[]{:S(2)}) copy-start(bf16[16,16,1152]{2,1,0:T(8,128)(2,1)S(1)} %all-to-all-done) | copy-start | bytes 1769476
Sparse Core Ops, SparseCore 0:
  149.7 35.4 reduce-scatter.1
